TPU v7x, 512 devices: a whole 4x8x8 slice. The times are simulated.
512 devices in a mesh: dp: 8 (over x, core), expert: 64 (over z, y).
Axes of the slice: x: 4, y: 8, z: 8, core: 2. Of those that a mesh axis runs over, the one named last changes fastest.
Arguments:
- tokens: bfloat16 [65536, 512], P(('dp', 'expert')), may hold values from -6 to 6
- modality: int32 [65536], P(('dp', 'expert')), may hold values 0 or 1
- modal_gains: float32 [2, 512], replicated, may hold values from 0.5 to 2
- routes: int32 [65536, 2], P(('dp', 'expert')), may hold values from 0 to 63, all different within a row; in each aligned block of 128 rows (0 to 127, 128 to 255, ...) at most 8 rows name the same one
- gate_share: int32 [65536], P(('dp', 'expert')), may hold values from 1 to 15
- up_weight: bfloat16 [64, 2048, 512], P('expert', 'dp'), may hold values from -0.25 to 0.25
- down_weight: bfloat16 [64, 2048, 512], P('expert', 'dp'), may hold values from -0.125 to 0.125
- cotangent: bfloat16 [65536, 512], P(('dp', 'expert')), may hold values from -6 to 6
Outputs:
- moe_output: bfloat16 [65536, 512], P(('dp', 'expert'))
- token_grad: bfloat16 [65536, 512], P(('dp', 'expert'))
- up_grad: bfloat16 [64, 2048, 512], P('expert', 'dp')
- down_grad: bfloat16 [64, 2048, 512], P('expert', 'dp')
Inputs may be any that keep to these rules, and one draw needn't show every extreme that they name: `routes`: each row names two different experts; among the 128 rows of one device no expert is named more than 8 times, and in every draw some device names some expert exactly 8 times.
All inputs are finite; a program needn't handle non-finite values. No bound on the sum of `modality` on one device may be relied on, other than what follows from the above.
Results may differ from a plain program's by a relative error of at most 0.014.
Values may be sent and summed in bfloat16 or wider, within the bound.
No kernel may reach another device: no remote copies, remote signals or barrier semaphores. Data moves between devices by JAX's collectives and lax.ppermute only.
A program may use at most 64 MiB of HBM per device.

v0:
```python
import math

import jax
import jax.numpy as jnp
from jax import lax
from jax.sharding import PartitionSpec as P

root_half = 0.7071067811865476
density = 0.3989422804014327


def sent_together(arrays, axis, dim, along):
    both = jnp.concatenate(arrays, axis=along)
    out, at, outs = (lax.all_gather(both, axis, axis=dim, tiled=True), 0, [])
    for a in arrays:
        outs.append(lax.slice_in_dim(out, at, at + a.shape[along], axis=along))
        at += a.shape[along]
    return tuple(outs)


def gelu_value(values):
    return values * 0.5 * (1.0 + lax.erf(values * root_half))


def gelu_slope(values):
    return (
        0.5 * (1.0 + lax.erf(values * root_half))
        + values * jnp.exp(-0.5 * values * values) * density
    )


def row_product(left_side, right_side, right_axis):
    numbers = (((1,), (right_axis,)), ((), ()))
    return lax.dot_general(left_side, right_side, numbers, preferred_element_type=jnp.float32)


def row_contract(left_side, right_side):
    numbers = (((0,), (0,)), ((), ()))
    return lax.dot_general(left_side, right_side, numbers, preferred_element_type=jnp.float32)


def on_device(tokens, modality, modal_gains, routes, gate_share, up_weight, down_weight, cotangent):
    tok_count = tokens.shape[0]
    model_width = tokens.shape[1]
    expert_count = lax.axis_size("expert")
    replica_count = lax.axis_size("dp")
    capacity = 4 * tok_count // expert_count
    slot_count = expert_count * capacity
    grad_scale = 1.0 / math.sqrt(2 * tok_count * replica_count)
    x_float = tokens.astype(jnp.float32)
    inv_rms = lax.rsqrt(jnp.mean(x_float * x_float, axis=-1, keepdims=True) + 1e-06)
    gain_rows = jnp.where(modality[:, None] == 1, modal_gains[1][None, :], modal_gains[0][None, :])
    normed = (x_float * inv_rms * gain_rows).astype(jnp.bfloat16)
    gate_first = gate_share.astype(jnp.float32) / 16.0
    gate_pair = jnp.stack([gate_first, 1.0 - gate_first], axis=1)
    flat_routes = routes.reshape(-1)
    one_hot = (flat_routes[:, None] == jnp.arange(expert_count, dtype=jnp.int32)[None, :]).astype(
        jnp.int32
    )
    earlier = jnp.cumsum(one_hot, axis=0) - one_hot
    position = jnp.sum(earlier * one_hot, axis=1)
    slot_index = flat_routes * capacity + position
    normed_routes = jnp.repeat(normed, 2, axis=0)
    empty_rows = jnp.zeros((slot_count, model_width), jnp.bfloat16)
    send_rows = (
        empty_rows.at[slot_index].set(normed_routes).reshape(expert_count, capacity, model_width)
    )
    route_grad = (
        (gate_pair[:, :, None] * cotangent.astype(jnp.float32)[:, None, :])
        .astype(jnp.bfloat16)
        .reshape(2 * tok_count, model_width)
    )
    send_grad = (
        empty_rows.at[slot_index].set(route_grad).reshape(expert_count, capacity, model_width)
    )
    sent_counts = jnp.sum(one_hot, axis=0).astype(jnp.bfloat16).reshape(expert_count, 1)
    both_sent = jnp.concatenate([send_rows, send_grad], axis=1)
    arrived_both, arrived_counts = (
        lax.all_to_all(both_sent, "expert", split_axis=0, concat_axis=0, tiled=True),
        lax.all_to_all(sent_counts, "expert", split_axis=0, concat_axis=0, tiled=True),
    )
    arrived = arrived_both[:, :capacity]
    arrived_grad = arrived_both[:, capacity:]
    expert_rows = arrived.reshape(slot_count, model_width)
    whole_up, whole_down = sent_together((up_weight, down_weight), "dp", 1, 0)
    pre_act = row_product(expert_rows, whole_up[0], 1)
    activated = gelu_value(pre_act).astype(jnp.bfloat16)
    expert_out = row_product(activated, whole_down[0], 0)
    outgoing = expert_out.astype(jnp.bfloat16).reshape(expert_count, capacity, model_width)
    grad_rows = arrived_grad.reshape(slot_count, model_width)
    hidden_grad = row_product(grad_rows, whole_down[0], 1)
    pre_grad = (hidden_grad * gelu_slope(pre_act)).astype(jnp.bfloat16)
    normed_part = row_product(pre_grad, whole_up[0], 0)
    returning = normed_part.astype(jnp.bfloat16).reshape(expert_count, capacity, model_width)
    both_back = lax.all_to_all(
        jnp.concatenate([outgoing, returning], axis=1),
        "expert",
        split_axis=0,
        concat_axis=0,
        tiled=True,
    )
    back_rows = both_back[:, :capacity]
    back_grad = both_back[:, capacity:]
    route_out = (
        back_rows.reshape(slot_count, model_width)[slot_index]
        .astype(jnp.float32)
        .reshape(tok_count, 2, model_width)
    )
    moe_output = jnp.sum(gate_pair[:, :, None] * route_out, axis=1).astype(jnp.bfloat16)
    route_back = (
        back_grad.reshape(slot_count, model_width)[slot_index]
        .astype(jnp.float32)
        .reshape(tok_count, 2, model_width)
    )
    normed_grad = jnp.sum(route_back, axis=1)
    scaled = gain_rows * normed_grad
    token_grad = (
        inv_rms * scaled - x_float * inv_rms**3 * jnp.mean(x_float * scaled, axis=-1, keepdims=True)
    ).astype(jnp.bfloat16)
    up_term = row_contract(pre_grad, expert_rows)
    down_term = row_contract(activated, grad_rows)
    grad_pair = lax.psum_scatter(
        (jnp.stack([up_term, down_term], axis=1) * grad_scale).astype(jnp.bfloat16),
        "dp",
        scatter_dimension=0,
        tiled=True,
    ).astype(jnp.float32)
    up_grad = grad_pair[:, 0][None].astype(jnp.bfloat16)
    down_grad = grad_pair[:, 1][None].astype(jnp.bfloat16)
    return (moe_output, token_grad, up_grad, down_grad)


def solution(mesh):
    placed = (
        P(("dp", "expert"), None),
        P(("dp", "expert")),
        P(),
        P(("dp", "expert"), None),
        P(("dp", "expert")),
        P("expert", "dp", None),
        P("expert", "dp", None),
        P(("dp", "expert"), None),
    )
    return jax.shard_map(
        on_device,
        mesh=mesh,
        in_specs=placed,
        out_specs=(
            P(("dp", "expert"), None),
            P(("dp", "expert"), None),
            P("expert", "dp", None),
            P("expert", "dp", None),
        ),
        check_vma=False,
    )
```

profile of v0, /device:TPU:6, one launch (start us, length us, event | category | flops | bytes accessed | tf_op | source)
XLA Modules:
  0.0 134.2 jit_solution(9797662723324753839)
XLA Ops:
  7.2 0.0 copy-start
  7.2 0.0 all-gather.2.cloned.1.call-start
  7.2 1.9 %pad_maximum_fusion.2 = bf16[2,256,512]{2,1,0:T(8,128)(2,1)} fusion(bf16[1,256,512]{2,1,0:T(8,128)(2,1)} %param.14, bf16[1,256,512]{2,1,0:T(8,128)(2,1)} %param.13), kind=kLoop, calls=%fused_computation.32 | loop fusion | flops 262144 | bytes 1048576 | tf_op jit(solution)/shard_map/concatenate | solution.py:13
  9.1 0.0 all-gather.2.cloned.1.call-update
  9.1 0.0 reduce-scatter.2.cloned.1.call-start
  9.2 0.8 copy.15
  10.0 0.1 eq.32
  10.1 0.1 eq.36
  10.3 0.7 broadcast_multiply_fusion
  11.0 0.1 copy.14
  11.1 0.1 mul.130
  11.2 0.6 reduce-window.6
  11.8 0.2 slice_reduce_fusion
  12.1 1.1 mul.138
  13.1 0.4 mul.139
  13.5 0.7 fusion.29
  14.2 0.1 copy.13
  14.3 0.1 mul.136
  14.4 1.0 fusion.15
  15.4 0.7 broadcast_compare_fusion
  16.1 0.8 fusion.30
  16.9 0.0 copy-done
  16.9 0.1 fusion.14
  17.0 0.1 broadcast_in_dim.51
  17.1 0.1 reshape.172
  17.3 0.1 fusion.27
  17.4 1.7 %scatter_custom_fusion = bf16[512,512]{1,0:T(8,128)(2,1)S(1)} fusion(s32[256]{0:T(256)S(1)} %bitcast.86, bf16[256,512]{1,0:T(8,128)(2,1)S(1)} %reshape.172, bf16[]{:T(256)} %constant.17.clone.1), kind=kCustom, calls=%fused_computation.52 | custom fusion | bytes 524290 | tf_op jit(solution)/shard_map/scatter | solution.py:66
  19.0 1.7 %scatter_custom_fusion.1 = bf16[512,512]{1,0:T(8,128)(2,1)S(1)} fusion(s32[256]{0:T(256)S(1)} %bitcast.87, f32[256,512]{1,0:T(8,128)S(1)} %mul.139, f32[256]{0:T(256)S(1)} %mul.136, bf16[]{:T(256)} %constant.17.clone.1), kind=kCustom, calls=%fused_computation.47 | custom fusion | flops 262144 | bytes 1049602 | tf_op jit(solution)/shard_map/scatter | solution.py:74
  20.8 0.1 pad_maximum_fusion
  20.9 46.2 %all_to_all.10 = bf16[64,16,512]{2,1,0:T(8,128)(2,1)S(1)} all-to-all(bf16[64,16,512]{2,1,0:T(8,128)(2,1)S(1)} %pad_maximum_fusion), channel_id=1, replica_groups=mesh['dp'=8,'expert'=64] {'expert'}, dimensions={0} | all-to-all | bytes 2097152 | tf_op jit(solution)/shard_map/all_to_all | solution.py:79
  67.1 0.0 all-gather.2.cloned.1.call-done
  67.1 0.0 copy-start.1
  67.1 3.1 %multiply_convert_fusion = (bf16[512,2048]{1,0:T(8,128)(2,1)S(1)}, f32[512,2048]{1,0:T(8,128)S(1)}) fusion(bf16[2,2048,512]{2,1,0:T(8,128)(2,1)} %all-gather.2.cloned.1.call-done, bf16[64,16,512]{2,1,0:T(8,128)(2,1)S(1)} %all_to_all.10), kind=kOutput, calls=%fused_computation.13 | convolution fusion | flops 1078984704 | bytes 8912896 | tf_op jit(solution)/shard_map/dot_general | solution.py:34
  70.2 0.0 copy-done.1
  70.2 2.8 %fusion.6 = bf16[512,2048]{1,0:T(8,128)(2,1)S(1)} fusion(f32[512,2048]{1,0:T(8,128)S(1)} %get-tuple-element.15, bf16[2,2048,512]{2,1,0:T(8,128)(2,1)S(1)} %copy-done.1, bf16[64,16,512]{2,1,0:T(8,128)(2,1)S(1)} %all_to_all.10), kind=kOutput, calls=%fused_computation.12 | convolution fusion | flops 1084227584 | bytes 8912896 | tf_op jit(solution)/shard_map/dot_general | solution.py:34
  73.0 0.0 copy-start.3
  73.0 1.3 convolution_bitcast_fusion
  74.3 1.3 convolution_bitcast_fusion.1
  75.7 0.0 copy-done.3
  75.7 2.6 %fusion = bf16[2048,2,512]{2,0,1:T(8,128)(2,1)} fusion(f32[2048,1,512]{2,0,1:T(8,128)S(1)} %convolution_bitcast_fusion, f32[2048,1,512]{2,0,1:T(8,128)S(1)} %convolution_bitcast_fusion.1), kind=kLoop, calls=%fused_computation.5 | loop fusion | flops 6291456 | bytes 12582912 | tf_op jit(solution)/shard_map/convert_element_type | solution.py:123
  78.3 0.0 reduce-scatter.2.cloned.1.call-update
  78.3 0.0 copy-start.2
  78.3 3.6 %fusion.12 = bf16[64,8,512]{2,1,0:T(8,128)(2,1)S(1)} fusion(bf16[512,2048]{1,0:T(8,128)(2,1)} %copy-done.3, bf16[2,2048,512]{2,1,0:T(8,128)(2,1)} %all-gather.2.cloned.1.call-done), kind=kOutput, calls=%fused_computation.24 | convolution fusion | flops 1074003968 | bytes 4718592 | tf_op jit(solution)/shard_map/dot_general | solution.py:34
  82.0 0.0 copy-done.2
  82.0 1.2 fusion.13
  83.2 1.1 pad_maximum_fusion.1
  84.3 6.4 %all-to-all-start.1 = ((bf16[64,16,512]{2,1,0:T(8,128)(2,1)}), bf16[64,16,512]{2,1,0:T(8,128)(2,1)S(1)}, u32[]{:S(2)}, u32[]{:S(2)}) async-start(bf16[64,16,512]{2,1,0:T(8,128)(2,1)} %pad_maximum_fusion.1), calls=%async_computation.1 | async-start | bytes 2097152 | tf_op jit(solution)/shard_map/all_to_all | solution.py:95
  90.8 28.7 %all-to-all-done.1 = bf16[64,16,512]{2,1,0:T(8,128)(2,1)S(1)} async-done(((bf16[64,16,512]{2,1,0:T(8,128)(2,1)}), bf16[64,16,512]{2,1,0:T(8,128)(2,1)S(1)}, u32[]{:S(2)}, u32[]{:S(2)}) %all-to-all-start.1) | async-done | bytes 1048608 | tf_op jit(solution)/shard_map/all_to_all | solution.py:95
  119.5 0.1 slice_bitcast_fusion.14
  119.5 1.2 gather_fusion
  120.7 0.3 reshape.150
  121.0 1.2 gather_fusion.1
  122.2 0.3 reshape.151
  122.5 0.6 reduce_sum.51
  123.2 0.2 fusion.19
  123.3 1.4 %multiply_reduce_fusion = bf16[128,512]{1,0:T(8,128)(2,1)} fusion(f32[128,2,512]{2,1,0:T(2,128)S(1)} %reshape.150, f32[128,2]{1,0:T(8,128)S(1)} %copy.13), kind=kLoop, calls=%fused_computation.33 | loop fusion | flops 196608 | bytes 656384 | tf_op jit(solution)/shard_map/reduce_sum | solution.py:109
  124.7 0.8 fusion.18
  125.5 0.0 reduce-scatter.2.cloned.1.call-done
  125.5 1.9 %slice_bitcast_fusion.22 = (bf16[1,256,512]{2,1,0:T(8,128)(2,1)}, bf16[1,256,512]{2,1,0:T(8,128)(2,1)}) fusion(bf16[256,2,512]{2,0,1:T(8,128)(2,1)} %reduce-scatter.2.cloned.1.call-done), kind=kLoop, calls=%fused_computation.48 | loop fusion | bytes 1048576 | tf_op jit(solution)/shard_map/convert_element_type | solution.py:129
  (8 shorter events, 0.1 us)
Async XLA Ops:
  7.2 9.7 %copy-start = (bf16[128,512]{1,0:T(8,128)(2,1)S(1)}, bf16[128,512]{1,0:T(8,128)(2,1)}, u32[]{:S(2)}) copy-start(bf16[128,512]{1,0:T(8,128)(2,1)} %param.8) | copy-start | bytes 393220
  7.2 59.9 %all-gather.2.cloned.1.call-start = ((), (), s32[]{:S(2)}) async-start(), calls=%async_computation.3 | async-start | bytes 4718592 | tf_op jit(solution)/shard_map/all_gather | solution.py:14
  9.1 116.4 %reduce-scatter.2.cloned.1.call-start = ((), (), s32[]{:S(2)}) async-start(), calls=%async_computation.4 | async-start | bytes 4718592 | tf_op jit(solution)/shard_map/reduce_scatter | solution.py:122
  67.1 3.1 %copy-start.1 = (bf16[2,2048,512]{2,1,0:T(8,128)(2,1)S(1)}, bf16[2,2048,512]{2,1,0:T(8,128)(2,1)}, u32[]{:S(2)}) copy-start(bf16[2,2048,512]{2,1,0:T(8,128)(2,1)} %all-gather.2.cloned.1.call-done) | copy-start | bytes 12582916
  73.0 2.6 %copy-start.3 = (bf16[512,2048]{1,0:T(8,128)(2,1)}, bf16[512,2048]{1,0:T(8,128)(2,1)S(1)}, u32[]{:S(2)}) copy-start(bf16[512,2048]{1,0:T(8,128)(2,1)S(1)} %fusion.6) | copy-start | bytes 6291460
  78.3 3.6 %copy-start.2 = (bf16[2,2048,512]{2,1,0:T(8,128)(2,1)S(1)}, bf16[2,2048,512]{2,1,0:T(8,128)(2,1)}, u32[]{:S(2)}) copy-start(bf16[2,2048,512]{2,1,0:T(8,128)(2,1)} %all-gather.2.cloned.1.call-done) | copy-start | bytes 12582916
  84.3 35.1 %all-to-all-start.1 = ((bf16[64,16,512]{2,1,0:T(8,128)(2,1)}), bf16[64,16,512]{2,1,0:T(8,128)(2,1)S(1)}, u32[]{:S(2)}, u32[]{:S(2)}) async-start(bf16[64,16,512]{2,1,0:T(8,128)(2,1)} %pad_maximum_fusion.1), calls=%async_computation.1 | async-start | bytes 2097152 | tf_op jit(solution)/shard_map/all_to_all | solution.py:95
Sparse Core Ops, SparseCore 0:
  10.1 40.1 all-gather.1
  78.4 34.4 reduce-scatter.1
where the time goes:
time: 135 us; the launch traced here: 134 us
  blocking collectives  46.2 us (34%)
  waiting for transfers between devices  28.7 us (21%)
  other arithmetic  14.4 us (11%)
  between operations  14.3 us (11%)
  matrix products  13.4 us (10%)
  local copies, waits for them, and re-layouts  10.8 us (8%)
  starting transfers between devices  6.48 us (5%)
    all_to_all x1, blocking collectives, on_device(): lax.all_to_all(both_sent, 'expert', split_axis=0, concat_axis=0, tiled=True)  46.2 us
    all_to_all x1, waiting for transfers between devices, on_device(): lax.all_to_all(jnp.concatenate([outgoing, returning], axis=1), 'expert',...  28.7 us
    dot_general x4, matrix products, row_product(): lax.dot_general(left_side, right_side, numbers, preferred_element_type=jn...  10.8 us
    all_to_all x1, starting transfers between devices, on_device(): lax.all_to_all(jnp.concatenate([outgoing, returning], axis=1), 'expert',...  6.4 us
  transfers between devices with their start and end apart: 3, of which 1 were waited for; matrix products, arithmetic and copies ran while one was open for 18% of the time, Pallas kernels for 0%

commit v1 on v0

v1 whole, which is shorter than its diff:
```python
import math

import jax
import jax.numpy as jnp
from jax import lax
from jax.sharding import PartitionSpec as P

root_half = 0.7071067811865476
density = 0.3989422804014327


def gelu_value(values):
    return values * 0.5 * (1.0 + lax.erf(values * root_half))


def gelu_slope(values):
    return (
        0.5 * (1.0 + lax.erf(values * root_half))
        + values * jnp.exp(-0.5 * values * values) * density
    )


def row_product(left_side, right_side, right_axis):
    numbers = (((1,), (right_axis,)), ((), ()))
    return lax.dot_general(left_side, right_side, numbers, preferred_element_type=jnp.float32)


def row_contract(left_side, right_side):
    numbers = (((0,), (0,)), ((), ()))
    return lax.dot_general(left_side, right_side, numbers, preferred_element_type=jnp.float32)


def exchange(rows, expert_count, capacity):
    model_width = rows.shape[-1]
    moved = lax.all_to_all(
        rows.reshape(expert_count, capacity, model_width), "expert", split_axis=0, concat_axis=0, tiled=True
    )
    return moved.reshape(expert_count * capacity, model_width)


def on_device(tokens, modality, modal_gains, routes, gate_share, up_weight, down_weight, cotangent):
    tok_count = tokens.shape[0]
    model_width = tokens.shape[1]
    expert_count = lax.axis_size("expert")
    replica_count = lax.axis_size("dp")
    capacity = 4 * tok_count // expert_count
    slot_count = expert_count * capacity
    route_count = 2 * tok_count
    grad_scale = 1.0 / math.sqrt(2 * tok_count * replica_count)
    whole = lax.all_gather(jnp.concatenate([up_weight, down_weight], axis=0), "dp", axis=1, tiled=True)
    whole_up, whole_down = whole[0], whole[1]
    x_float = tokens.astype(jnp.float32)
    inv_rms = lax.rsqrt(jnp.mean(x_float * x_float, axis=-1, keepdims=True) + 1e-06)
    gain_rows = jnp.where(modality[:, None] == 1, modal_gains[1][None, :], modal_gains[0][None, :])
    normed = (x_float * inv_rms * gain_rows).astype(jnp.bfloat16)
    gate_first = gate_share.astype(jnp.float32) / 16.0
    flat_routes = routes.reshape(-1)
    one_hot = flat_routes[:, None] == jnp.arange(expert_count, dtype=jnp.int32)[None, :]
    route_ids = jnp.arange(route_count, dtype=jnp.int32)
    before = (route_ids[None, :] < route_ids[:, None]).astype(jnp.bfloat16)
    earlier = jnp.dot(before, one_hot.astype(jnp.bfloat16), preferred_element_type=jnp.float32)
    position = jnp.sum(jnp.where(one_hot, earlier, 0.0), axis=1).astype(jnp.int32)
    slot_index = (flat_routes * capacity + position).reshape(tok_count, 2)
    slot_ids = jnp.arange(slot_count, dtype=jnp.int32)[:, None]
    first_hit = slot_ids == slot_index[:, 0][None, :]
    second_hit = slot_ids == slot_index[:, 1][None, :]
    pick = (first_hit | second_hit).astype(jnp.bfloat16)
    weigh = jnp.where(first_hit, gate_first[None, :], jnp.where(second_hit, 1.0 - gate_first[None, :], 0.0)).astype(
        jnp.bfloat16
    )
    send_rows = jnp.dot(pick, normed, preferred_element_type=jnp.float32).astype(jnp.bfloat16)
    send_grad = jnp.dot(weigh, cotangent, preferred_element_type=jnp.float32).astype(jnp.bfloat16)
    expert_rows = exchange(send_rows, expert_count, capacity)
    grad_rows = exchange(send_grad, expert_count, capacity)
    pre_act = row_product(expert_rows, whole_up, 1)
    activated = gelu_value(pre_act).astype(jnp.bfloat16)
    expert_out = row_product(activated, whole_down, 0).astype(jnp.bfloat16)
    back_rows = exchange(expert_out, expert_count, capacity)
    hidden_grad = row_product(grad_rows, whole_down, 1)
    pre_grad = (hidden_grad * gelu_slope(pre_act)).astype(jnp.bfloat16)
    normed_part = row_product(pre_grad, whole_up, 0).astype(jnp.bfloat16)
    back_grad = exchange(normed_part, expert_count, capacity)
    up_term = row_contract(pre_grad, expert_rows)
    down_term = row_contract(activated, grad_rows)
    grad_pair = lax.psum_scatter(
        (jnp.stack([up_term, down_term], axis=1) * grad_scale).astype(jnp.bfloat16),
        "dp",
        scatter_dimension=0,
        tiled=True,
    ).astype(jnp.float32)
    up_grad = grad_pair[:, 0][None].astype(jnp.bfloat16)
    down_grad = grad_pair[:, 1][None].astype(jnp.bfloat16)
    moe_output = row_contract(weigh, back_rows).astype(jnp.bfloat16)
    normed_grad = row_contract(pick, back_grad)
    scaled = gain_rows * normed_grad
    token_grad = (
        inv_rms * scaled - x_float * inv_rms**3 * jnp.mean(x_float * scaled, axis=-1, keepdims=True)
    ).astype(jnp.bfloat16)
    return (moe_output, token_grad, up_grad, down_grad)


def solution(mesh):
    placed = (
        P(("dp", "expert"), None),
        P(("dp", "expert")),
        P(),
        P(("dp", "expert"), None),
        P(("dp", "expert")),
        P("expert", "dp", None),
        P("expert", "dp", None),
        P(("dp", "expert"), None),
    )
    return jax.shard_map(
        on_device,
        mesh=mesh,
        in_specs=placed,
        out_specs=(
            P(("dp", "expert"), None),
            P(("dp", "expert"), None),
            P("expert", "dp", None),
            P("expert", "dp", None),
        ),
        check_vma=False,
    )
```

time: 135 us -> 147 us (1.089)
  blocking collectives: 46.2 us -> 0 us
  waiting for transfers between devices: 28.7 us -> 64 us
  starting transfers between devices: 6.48 us -> 31.7 us
  matrix products: 13.4 us -> 24.3 us
  local copies, waits for them, and re-layouts: 10.8 us -> 3.83 us
  other arithmetic: 14.4 us -> 8.46 us
    all_to_all x1 -> x0, blocking collectives: 46.2 us -> none  [on_device(): lax.all_to_all(both_sent, 'expert', split_axis=0, concat_axis=0, tiled=True)]
    all_to_all x1 -> x4, waiting for transfers between devices: 28.7 us -> 63.9 us  [exchange(): lax.all_to_all(rows.reshape(expert_count, capacity, model_width), 'expert...]
    all_to_all x1 -> x4, starting transfers between devices: 6.4 us -> 31.6 us  [exchange(): lax.all_to_all(rows.reshape(expert_count, capacity, model_width), 'expert...]
    dot_general x4, matrix products: 10.8 us -> 17 us  [row_product(): lax.dot_general(left_side, right_side, numbers, preferred_element_type=jn...]
    dot_general x0 -> x3, matrix products: none -> 3.4 us  [the longest x1 2.08 us: on_device(): jnp.dot(pick, normed, preferred_element_type=jnp.float32)]
    gather x2 -> x0, local copies, waits for them, and re-layouts: 2.31 us -> none  [the longest x1 1.15 us: on_device(): back_rows.reshape(slot_count, model_width)[slot_index].astype(jnp.float32)]
    reduce_sum x4 -> x0, other arithmetic: 2.28 us -> none  [the longest x1 1.37 us: on_device(): jnp.sum(gate_pair[:, :, None] * route_out, axis=1).astype(jnp.bfloat16)]
    mul x5 -> x0, local copies, waits for them, and re-layouts: 1.8 us -> none  [the longest x2 1.41 us: on_device(): gate_pair[:, :, None] * cotangent.astype(jnp.float32)[:, None, :]]
  transfers between devices with their start and end apart: 3 -> 6, of which waited for: 1 -> 4; matrix products, arithmetic and copies ran while one was open for 18% -> 16% of each run, Pallas kernels for 0% -> 0%
where the time goes in v1:
time: 147 us; the launch traced here: 146 us
  waiting for transfers between devices  64 us (44%)
  starting transfers between devices  31.7 us (22%)
  matrix products  24.3 us (17%)
  between operations  14.2 us (10%)
  other arithmetic  8.46 us (6%)
  local copies, waits for them, and re-layouts  3.83 us (3%)
    all_to_all x4, waiting for transfers between devices, exchange(): lax.all_to_all(rows.reshape(expert_count, capacity, model_width), 'expert...  63.9 us
    all_to_all x4, starting transfers between devices, exchange(): lax.all_to_all(rows.reshape(expert_count, capacity, model_width), 'expert...  31.6 us
    dot_general x4, matrix products, row_product(): lax.dot_general(left_side, right_side, numbers, preferred_element_type=jn...  17 us
    dot_general x4, matrix products, row_contract(): lax.dot_general(left_side, right_side, numbers, preferred_element_type=jn...  3.9 us
  transfers between devices with their start and end apart: 6, of which 4 were waited for; matrix products, arithmetic and copies ran while one was open for 16% of the time, Pallas kernels for 0%

profile of v1, /device:TPU:6, one launch (start us, length us, event | category | flops | bytes accessed | tf_op | source)
XLA Modules:
  0.0 146.4 jit_solution(11591336004212337281)
XLA Ops:
  7.2 0.0 copy-start
  7.2 0.0 all-gather.2.cloned.1.call-start
  7.2 1.9 %pad_maximum_fusion = bf16[2,256,512]{2,1,0:T(8,128)(2,1)} fusion(bf16[1,256,512]{2,1,0:T(8,128)(2,1)} %param.14, bf16[1,256,512]{2,1,0:T(8,128)(2,1)} %param.13), kind=kLoop, calls=%fused_computation.30 | loop fusion | flops 262144 | bytes 1048576 | tf_op jit(solution)/shard_map/concatenate | solution.py:50
  9.1 0.0 all-gather.2.cloned.1.call-update
  9.2 0.8 copy.18
  9.9 0.1 eq.53
  10.1 0.2 fusion.16
  10.3 0.1 convert_element_type.75
  10.5 0.1 copy.19
  10.5 1.0 fusion.24
  11.6 0.7 broadcast_compare_fusion
  12.2 0.7 multiply_add_fusion
  12.9 0.8 fusion.54
  13.7 2.1 %fusion.12 = bf16[64,8,512]{2,1,0:T(8,128)(2,1)} fusion(bf16[128,512]{1,0:T(8,128)(2,1)} %param.8, f32[512]{0:T(512)S(1)} %bitcast.67, f32[512]{0:T(512)S(1)} %bitcast.65, f32[128]{0:T(128)S(1)} %get-tuple-element.11, s32[128]{0:T(128)S(1)} %get-tuple-element.9, s32[128]{0:T(128)S(1)} %get-tuple-element.8, pred[128]{0:T(512)(128)(4,1)S(1)} %broadcast_compare_fusion), kind=kOutput, calls=%fused_computation.22 | convolution fusion | flops 67895296 | bytes 661120 | tf_op jit(solution)/shard_map/dot_general | solution.py:71
  15.8 16.6 %all-to-all-start = ((bf16[64,8,512]{2,1,0:T(8,128)(2,1)}), bf16[64,8,512]{2,1,0:T(8,128)(2,1)S(1)}, u32[]{:S(2)}, u32[]{:S(2)}) async-start(bf16[64,8,512]{2,1,0:T(8,128)(2,1)} %fusion.12), calls=%async_computation | async-start | bytes 1048576 | tf_op jit(solution)/shard_map/all_to_all | solution.py:35
  32.4 0.7 convert_multiply_fusion.4
  33.0 0.0 copy-done
  33.0 1.1 fusion.13
  34.1 17.9 %all-to-all-done = bf16[64,8,512]{2,1,0:T(8,128)(2,1)S(1)} async-done(((bf16[64,8,512]{2,1,0:T(8,128)(2,1)}), bf16[64,8,512]{2,1,0:T(8,128)(2,1)S(1)}, u32[]{:S(2)}, u32[]{:S(2)}) %all-to-all-start) | async-done | bytes 524320 | tf_op jit(solution)/shard_map/all_to_all | solution.py:35
  52.1 5.0 %all-to-all-start.2 = ((bf16[64,8,512]{2,1,0:T(8,128)(2,1)}), bf16[64,8,512]{2,1,0:T(8,128)(2,1)S(1)}, u32[]{:S(2)}, u32[]{:S(2)}) async-start(bf16[64,8,512]{2,1,0:T(8,128)(2,1)} %fusion.13), calls=%async_computation.2 | async-start | bytes 1048576 | tf_op jit(solution)/shard_map/all_to_all | solution.py:35
  57.1 0.0 reduce-scatter.2.cloned.1.call-start
  57.1 0.0 all-gather.2.cloned.1.call-done
  57.2 4.5 %multiply_convert_fusion = (bf16[512,2048]{1,0:T(8,128)(2,1)S(1)}, f32[512,2048]{1,0:T(8,128)}) fusion(bf16[2,2048,512]{2,1,0:T(8,128)(2,1)} %all-gather.2.cloned.1.call-done, bf16[64,8,512]{2,1,0:T(8,128)(2,1)S(1)} %all-to-all-done), kind=kOutput, calls=%fused_computation.9 | convolution fusion | flops 1078984704 | bytes 8912896 | tf_op jit(solution)/shard_map/dot_general | solution.py:25
  61.7 14.3 %all-to-all-done.2 = bf16[64,8,512]{2,1,0:T(8,128)(2,1)S(1)} async-done(((bf16[64,8,512]{2,1,0:T(8,128)(2,1)}), bf16[64,8,512]{2,1,0:T(8,128)(2,1)S(1)}, u32[]{:S(2)}, u32[]{:S(2)}) %all-to-all-start.2) | async-done | bytes 524320 | tf_op jit(solution)/shard_map/all_to_all | solution.py:35
  76.0 4.5 %fusion.6 = bf16[512,2048]{1,0:T(8,128)(2,1)S(1)} fusion(f32[512,2048]{1,0:T(8,128)} %get-tuple-element.15, bf16[2,2048,512]{2,1,0:T(8,128)(2,1)} %all-gather.2.cloned.1.call-done, bf16[64,8,512]{2,1,0:T(8,128)(2,1)S(1)} %all-to-all-done.2), kind=kOutput, calls=%fused_computation.8 | convolution fusion | flops 1084227584 | bytes 8912896 | tf_op jit(solution)/shard_map/dot_general | solution.py:25
  80.5 0.0 copy-start.2
  80.5 1.3 convolution_bitcast_fusion
  81.8 0.1 copy-done.2
  81.8 1.3 convolution_bitcast_fusion.1
  83.2 2.7 %fusion = bf16[2048,2,512]{2,0,1:T(8,128)(2,1)} fusion(f32[2048,1,512]{2,0,1:T(8,128)S(1)} %convolution_bitcast_fusion, f32[2048,1,512]{2,0,1:T(8,128)S(1)} %convolution_bitcast_fusion.1), kind=kLoop, calls=%fused_computation.1 | loop fusion | flops 6291456 | bytes 12582912 | tf_op jit(solution)/shard_map/convert_element_type | solution.py:86
  85.8 0.0 reduce-scatter.2.cloned.1.call-update
  85.9 4.3 %fusion.14 = bf16[64,8,512]{2,1,0:T(8,128)(2,1)} fusion(bf16[512,2048]{1,0:T(8,128)(2,1)} %copy-done.2, bf16[2,2048,512]{2,1,0:T(8,128)(2,1)} %all-gather.2.cloned.1.call-done), kind=kOutput, calls=%fused_computation.24 | convolution fusion | flops 1074003968 | bytes 4718592 | tf_op jit(solution)/shard_map/dot_general | solution.py:25
  90.1 5.0 %all-to-all-start.3 = ((bf16[64,8,512]{2,1,0:T(8,128)(2,1)}), bf16[64,8,512]{2,1,0:T(8,128)(2,1)S(1)}, u32[]{:S(2)}, u32[]{:S(2)}) async-start(bf16[64,8,512]{2,1,0:T(8,128)(2,1)} %fusion.14), calls=%async_computation.3 | async-start | bytes 1048576 | tf_op jit(solution)/shard_map/all_to_all | solution.py:35
  95.1 0.0 copy-start.1
  95.1 3.7 %fusion.15 = bf16[64,8,512]{2,1,0:T(8,128)(2,1)} fusion(bf16[512,2048]{1,0:T(8,128)(2,1)S(1)} %get-tuple-element.14, bf16[2,2048,512]{2,1,0:T(8,128)(2,1)} %all-gather.2.cloned.1.call-done), kind=kOutput, calls=%fused_computation.25 | convolution fusion | flops 1074003968 | bytes 4718592 | tf_op jit(solution)/shard_map/dot_general | solution.py:25
  98.9 14.6 %all-to-all-done.3 = bf16[64,8,512]{2,1,0:T(8,128)(2,1)S(1)} async-done(((bf16[64,8,512]{2,1,0:T(8,128)(2,1)}), bf16[64,8,512]{2,1,0:T(8,128)(2,1)S(1)}, u32[]{:S(2)}, u32[]{:S(2)}) %all-to-all-start.3) | async-done | bytes 524320 | tf_op jit(solution)/shard_map/all_to_all | solution.py:35
  113.5 5.0 %all-to-all-start.1 = ((bf16[64,8,512]{2,1,0:T(8,128)(2,1)}), bf16[64,8,512]{2,1,0:T(8,128)(2,1)S(1)}, u32[]{:S(2)}, u32[]{:S(2)}) async-start(bf16[64,8,512]{2,1,0:T(8,128)(2,1)} %fusion.15), calls=%async_computation.1 | async-start | bytes 1048576 | tf_op jit(solution)/shard_map/all_to_all | solution.py:35
  118.5 0.0 copy-done.1
  118.5 0.4 fusion.28
  118.9 0.8 fusion.27
  119.7 17.1 %all-to-all-done.1 = bf16[64,8,512]{2,1,0:T(8,128)(2,1)S(1)} async-done(((bf16[64,8,512]{2,1,0:T(8,128)(2,1)}), bf16[64,8,512]{2,1,0:T(8,128)(2,1)S(1)}, u32[]{:S(2)}, u32[]{:S(2)}) %all-to-all-start.1) | async-done | bytes 524320 | tf_op jit(solution)/shard_map/all_to_all | solution.py:35
  136.8 0.9 convolution_convert_fusion.2
  137.7 0.0 reduce-scatter.2.cloned.1.call-done
  137.7 1.9 %slice_bitcast_fusion.14 = (bf16[1,256,512]{2,1,0:T(8,128)(2,1)}, bf16[1,256,512]{2,1,0:T(8,128)(2,1)}) fusion(bf16[256,2,512]{2,0,1:T(8,128)(2,1)} %reduce-scatter.2.cloned.1.call-done), kind=kLoop, calls=%fused_computation.48 | loop fusion | bytes 1048576 | tf_op jit(solution)/shard_map/convert_element_type | solution.py:92
  (4 shorter events, 0.0 us)
Async XLA Ops:
  7.2 25.9 %copy-start = (bf16[128,512]{1,0:T(8,128)(2,1)S(1)}, bf16[128,512]{1,0:T(8,128)(2,1)}, u32[]{:S(2)}) copy-start(bf16[128,512]{1,0:T(8,128)(2,1)} %param.15) | copy-start | bytes 393220
  7.2 50.0 %all-gather.2.cloned.1.call-start = ((), (), s32[]{:S(2)}) async-start(), calls=%async_computation.5 | async-start | bytes 4718592 | tf_op jit(solution)/shard_map/all_gather | solution.py:50
  15.8 36.3 %all-to-all-start = ((bf16[64,8,512]{2,1,0:T(8,128)(2,1)}), bf16[64,8,512]{2,1,0:T(8,128)(2,1)S(1)}, u32[]{:S(2)}, u32[]{:S(2)}) async-start(bf16[64,8,512]{2,1,0:T(8,128)(2,1)} %fusion.12), calls=%async_computation | async-start | bytes 1048576 | tf_op jit(solution)/shard_map/all_to_all | solution.py:35
  52.1 23.9 %all-to-all-start.2 = ((bf16[64,8,512]{2,1,0:T(8,128)(2,1)}), bf16[64,8,512]{2,1,0:T(8,128)(2,1)S(1)}, u32[]{:S(2)}, u32[]{:S(2)}) async-start(bf16[64,8,512]{2,1,0:T(8,128)(2,1)} %fusion.13), calls=%async_computation.2 | async-start | bytes 1048576 | tf_op jit(solution)/shard_map/all_to_all | solution.py:35
  57.1 80.6 %reduce-scatter.2.cloned.1.call-start = ((), (), s32[]{:S(2)}) async-start(), calls=%async_computation.6 | async-start | bytes 4718592 | tf_op jit(solution)/shard_map/reduce_scatter | solution.py:85
  80.5 1.4 copy-start.2
  90.1 23.4 %all-to-all-start.3 = ((bf16[64,8,512]{2,1,0:T(8,128)(2,1)}), bf16[64,8,512]{2,1,0:T(8,128)(2,1)S(1)}, u32[]{:S(2)}, u32[]{:S(2)}) async-start(bf16[64,8,512]{2,1,0:T(8,128)(2,1)} %fusion.14), calls=%async_computation.3 | async-start | bytes 1048576 | tf_op jit(solution)/shard_map/all_to_all | solution.py:35
  95.1 23.4 %copy-start.1 = (bf16[128,512]{1,0:T(8,128)(2,1)S(1)}, bf16[128,512]{1,0:T(8,128)(2,1)}, u32[]{:S(2)}) copy-start(bf16[128,512]{1,0:T(8,128)(2,1)} %param.8) | copy-start | bytes 393220
  113.5 23.3 %all-to-all-start.1 = ((bf16[64,8,512]{2,1,0:T(8,128)(2,1)}), bf16[64,8,512]{2,1,0:T(8,128)(2,1)S(1)}, u32[]{:S(2)}, u32[]{:S(2)}) async-start(bf16[64,8,512]{2,1,0:T(8,128)(2,1)} %fusion.15), calls=%async_computation.1 | async-start | bytes 1048576 | tf_op jit(solution)/shard_map/all_to_all | solution.py:35
Sparse Core Ops, SparseCore 0:
  10.1 40.1 all-gather.1
  86.0 33.1 reduce-scatter.1

commit v2 on v1

--- a/solution.py
+++ b/solution.py
@@ -30,12 +30,34 @@
     return lax.dot_general(left_side, right_side, numbers, preferred_element_type=jnp.float32)
 
 
-def exchange(rows, expert_count, capacity):
-    model_width = rows.shape[-1]
-    moved = lax.all_to_all(
-        rows.reshape(expert_count, capacity, model_width), "expert", split_axis=0, concat_axis=0, tiled=True
-    )
-    return moved.reshape(expert_count * capacity, model_width)
+def ring_shift(value, chips, cores, shift):
+    pairs = [(c * cores + k, ((c + shift) % chips) * cores + k) for c in range(chips) for k in range(cores)]
+    return lax.ppermute(value, "dp", pairs)
+
+
+def core_swap(value, chips, cores):
+    pairs = [(c * cores + k, c * cores + (k + 1) % cores) for c in range(chips) for k in range(cores)]
+    return lax.ppermute(value, "dp", pairs)
+
+
+def gather_weights(shard, chips, cores):
+    mine = jnp.stack([shard] + [ring_shift(shard, chips, cores, k) for k in range(1, chips)])
+    other = core_swap(mine, chips, cores)
+    both = jnp.stack([mine, other])
+    width = shard.shape[-1]
+    up = both[:, :, 0].reshape(-1, width)
+    down = both[:, :, 1].reshape(-1, width)
+    return up, down
+
+
+def scatter_grads(parts, chips, cores):
+    from_other = core_swap(parts[1], chips, cores)
+    summed = parts[0].astype(jnp.float32) + from_other.astype(jnp.float32)
+    sent = summed.astype(jnp.bfloat16)
+    total = summed[0]
+    for k in range(1, chips):
+        total = total + ring_shift(sent[k], chips, cores, -k).astype(jnp.float32)
+    return total.astype(jnp.bfloat16)
 
 
 def on_device(tokens, modality, modal_gains, routes, gate_share, up_weight, down_weight, cotangent):
@@ -43,12 +65,14 @@
     model_width = tokens.shape[1]
     expert_count = lax.axis_size("expert")
     replica_count = lax.axis_size("dp")
+    cores = 2
+    chips = replica_count // cores
     capacity = 4 * tok_count // expert_count
     slot_count = expert_count * capacity
     route_count = 2 * tok_count
     grad_scale = 1.0 / math.sqrt(2 * tok_count * replica_count)
-    whole = lax.all_gather(jnp.concatenate([up_weight, down_weight], axis=0), "dp", axis=1, tiled=True)
-    whole_up, whole_down = whole[0], whole[1]
+    shard = jnp.concatenate([up_weight, down_weight], axis=0)
+    whole_up, whole_down = gather_weights(shard, chips, cores)
     x_float = tokens.astype(jnp.float32)
     inv_rms = lax.rsqrt(jnp.mean(x_float * x_float, axis=-1, keepdims=True) + 1e-06)
     gain_rows = jnp.where(modality[:, None] == 1, modal_gains[1][None, :], modal_gains[0][None, :])
@@ -68,30 +92,43 @@
     weigh = jnp.where(first_hit, gate_first[None, :], jnp.where(second_hit, 1.0 - gate_first[None, :], 0.0)).astype(
         jnp.bfloat16
     )
-    send_rows = jnp.dot(pick, normed, preferred_element_type=jnp.float32).astype(jnp.bfloat16)
-    send_grad = jnp.dot(weigh, cotangent, preferred_element_type=jnp.float32).astype(jnp.bfloat16)
-    expert_rows = exchange(send_rows, expert_count, capacity)
-    grad_rows = exchange(send_grad, expert_count, capacity)
+    pick = pick.reshape(expert_count, 1, capacity, tok_count)
+    weigh = weigh.reshape(expert_count, 1, capacity, tok_count)
+    blank = jnp.zeros_like(pick)
+    gather_side = jnp.concatenate(
+        [jnp.concatenate([pick, blank], axis=3), jnp.concatenate([blank, weigh], axis=3)], axis=1
+    ).reshape(2 * slot_count, 2 * tok_count)
+    return_side = jnp.concatenate(
+        [jnp.concatenate([weigh, blank], axis=3), jnp.concatenate([blank, pick], axis=3)], axis=1
+    ).reshape(2 * slot_count, 2 * tok_count)
+    sources = jnp.concatenate([normed, cotangent], axis=0)
+    sending = jnp.dot(gather_side, sources, preferred_element_type=jnp.float32).astype(jnp.bfloat16)
+    arrived = lax.all_to_all(
+        sending.reshape(expert_count, 2 * capacity, model_width), "expert", split_axis=0, concat_axis=0, tiled=True
+    )
+    expert_rows = arrived[:, :capacity].reshape(slot_count, model_width)
+    grad_rows = arrived[:, capacity:].reshape(slot_count, model_width)
     pre_act = row_product(expert_rows, whole_up, 1)
     activated = gelu_value(pre_act).astype(jnp.bfloat16)
     expert_out = row_product(activated, whole_down, 0).astype(jnp.bfloat16)
-    back_rows = exchange(expert_out, expert_count, capacity)
     hidden_grad = row_product(grad_rows, whole_down, 1)
     pre_grad = (hidden_grad * gelu_slope(pre_act)).astype(jnp.bfloat16)
     normed_part = row_product(pre_grad, whole_up, 0).astype(jnp.bfloat16)
-    back_grad = exchange(normed_part, expert_count, capacity)
-    up_term = row_contract(pre_grad, expert_rows)
-    down_term = row_contract(activated, grad_rows)
-    grad_pair = lax.psum_scatter(
-        (jnp.stack([up_term, down_term], axis=1) * grad_scale).astype(jnp.bfloat16),
-        "dp",
-        scatter_dimension=0,
-        tiled=True,
-    ).astype(jnp.float32)
-    up_grad = grad_pair[:, 0][None].astype(jnp.bfloat16)
-    down_grad = grad_pair[:, 1][None].astype(jnp.bfloat16)
-    moe_output = row_contract(weigh, back_rows).astype(jnp.bfloat16)
-    normed_grad = row_contract(pick, back_grad)
+    leaving = jnp.concatenate(
+        [expert_out.reshape(expert_count, capacity, model_width), normed_part.reshape(expert_count, capacity, model_width)],
+        axis=1,
+    )
+    back = lax.all_to_all(leaving, "expert", split_axis=0, concat_axis=0, tiled=True)
+    up_term = row_contract(pre_grad, expert_rows) * grad_scale
+    down_term = row_contract(activated, grad_rows) * grad_scale
+    parts = jnp.stack([up_term, down_term]).astype(jnp.bfloat16)
+    parts = parts.reshape(2, cores, chips, -1, model_width).transpose(1, 2, 0, 3, 4)
+    grad_pair = scatter_grads(parts, chips, cores)
+    up_grad = grad_pair[0][None]
+    down_grad = grad_pair[1][None]
+    combined = row_contract(return_side, back.reshape(2 * slot_count, model_width))
+    moe_output = combined[:tok_count].astype(jnp.bfloat16)
+    normed_grad = combined[tok_count:]
     scaled = gain_rows * normed_grad
     token_grad = (
         inv_rms * scaled - x_float * inv_rms**3 * jnp.mean(x_float * scaled, axis=-1, keepdims=True)

time: 147 us -> 169 us (1.15)
  the two profiles are of different devices: /device:TPU:6 before, /device:TPU:24 now
where the time goes in v2:
time: 169 us; the launch traced here: 168 us
  waiting for transfers between devices  81.1 us (48%)
  starting transfers between devices  46.5 us (28%)
  other arithmetic  15.8 us (9%)
  matrix products  15.4 us (9%)
  local copies, waits for them, and re-layouts  8.31 us (5%)
    ppermute x6, waiting for transfers between devices, ring_shift(): return lax.ppermute(value, 'dp', pairs)  34.8 us
    all_to_all x1, waiting for transfers between devices, on_device(): lax.all_to_all(sending.reshape(expert_count, 2 * capacity, model_width),...  26.5 us
    all_to_all x1, waiting for transfers between devices, on_device(): lax.all_to_all(leaving, 'expert', split_axis=0, concat_axis=0, tiled=True)  19.8 us
    ppermute x6, starting transfers between devices, ring_shift(): return lax.ppermute(value, 'dp', pairs)  18.7 us
    all_to_all x1, starting transfers between devices, on_device(): lax.all_to_all(sending.reshape(expert_count, 2 * capacity, model_width),...  16.4 us
    dot_general x4, matrix products, row_product(): lax.dot_general(left_side, right_side, numbers, preferred_element_type=jn...  7.81 us
    all_to_all x1, starting transfers between devices, on_device(): lax.all_to_all(leaving, 'expert', split_axis=0, concat_axis=0, tiled=True)  7.57 us
    dot_general x3, matrix products, row_contract(): lax.dot_general(left_side, right_side, numbers, preferred_element_type=jn...  5.85 us
  transfers between devices with their start and end apart: 10, of which 6 were waited for; matrix products, arithmetic and copies ran while one was open for 12% of the time, Pallas kernels for 0%

profile of v2, /device:TPU:24, one launch (start us, length us, event | category | flops | bytes accessed | tf_op | source)
XLA Modules:
  0.0 168.0 jit_solution(17081057164177318477)
XLA Ops:
  0.6 0.0 copy-start.1
  0.6 0.0 copy-start.6
  0.7 1.0 constant_dynamic-update-slice_fusion.1
  1.7 1.0 constant_dynamic-update-slice_fusion
  2.6 4.7 %collective-permute-start.2 = (bf16[2,256,512]{2,1,0:T(8,128)(2,1)S(1)}, bf16[2,256,512]{2,1,0:T(8,128)(2,1)S(1)}, u32[]{:S(2)}, u32[]{:S(2)}) collective-permute-start(bf16[2,256,512]{2,1,0:T(8,128)(2,1)S(1)} %constant_dynamic-update-slice_fusion), channel_id=1, source_target_pairs={{0,384},{64,448},{128,0},{192,64},{256,128},{320,192},{384,256},{4... | collective-permute-start | bytes 1572872 | tf_op jit(solution)/shard_map/ppermute | solution.py:35
  7.3 2.7 %collective-permute-start.1 = (bf16[2,256,512]{2,1,0:T(8,128)(2,1)S(1)}, bf16[2,256,512]{2,1,0:T(8,128)(2,1)}, u32[]{:S(2)}, u32[]{:S(2)}) collective-permute-start(bf16[2,256,512]{2,1,0:T(8,128)(2,1)S(1)} %constant_dynamic-update-slice_fusion), channel_id=1, source_target_pairs={{0,256},{64,320},{128,384},{192,448},{256,0},{320,64},{384,128},{4... | collective-permute-start | bytes 1572872 | tf_op jit(solution)/shard_map/ppermute | solution.py:35
  10.0 2.8 %collective-permute-start = (bf16[2,256,512]{2,1,0:T(8,128)(2,1)S(1)}, bf16[2,256,512]{2,1,0:T(8,128)(2,1)S(1)}, u32[]{:S(2)}, u32[]{:S(2)}) collective-permute-start(bf16[2,256,512]{2,1,0:T(8,128)(2,1)S(1)} %constant_dynamic-update-slice_fusion), channel_id=1, source_target_pairs={{0,128},{64,192},{128,256},{192,320},{256,384},{320,448},{384,0},{... | collective-permute-start | bytes 1572872 | tf_op jit(solution)/shard_map/ppermute | solution.py:35
  12.8 0.7 broadcast_compare_fusion
  13.5 1.0 fusion.23
  14.5 0.7 convert_multiply_fusion.4
  15.2 0.8 copy.24
  16.0 0.1 eq.88
  16.1 0.2 fusion.9
  16.4 0.1 convert_element_type.84
  16.5 0.1 copy.25
  16.6 0.7 multiply_add_fusion.1
  17.3 0.1 fusion.31
  17.4 0.1 fusion.21
  17.6 0.9 fusion.19
  18.5 0.1 fusion.22
  18.6 11.2 %collective-permute-done.2 = bf16[2,256,512]{2,1,0:T(8,128)(2,1)S(1)} collective-permute-done((bf16[2,256,512]{2,1,0:T(8,128)(2,1)S(1)}, bf16[2,256,512]{2,1,0:T(8,128)(2,1)S(1)}, u32[]{:S(2)}, u32[]{:S(2)}) %collective-permute-start.2) | collective-permute-done | bytes 524320 | tf_op jit(solution)/shard_map/ppermute | solution.py:35
  29.7 0.0 collective-permute-done.1
  29.7 5.6 %collective-permute-done = bf16[2,256,512]{2,1,0:T(8,128)(2,1)S(1)} collective-permute-done((bf16[2,256,512]{2,1,0:T(8,128)(2,1)S(1)}, bf16[2,256,512]{2,1,0:T(8,128)(2,1)S(1)}, u32[]{:S(2)}, u32[]{:S(2)}) %collective-permute-start) | collective-permute-done | bytes 524320 | tf_op jit(solution)/shard_map/ppermute | solution.py:35
  35.3 0.8 copy-done.4
  36.1 2.9 %pad_maximum_fusion.1 = (bf16[4,2,256,512]{3,2,1,0:T(8,128)(2,1)}, bf16[1,4,2,256,512]{4,3,2,1,0:T(8,128)(2,1)S(1)}) fusion(bf16[1,2,256,512]{3,2,1,0:T(8,128)(2,1)S(1)} %bitcast.87, bf16[1,2,256,512]{3,2,1,0:T(8,128)(2,1)} %bitcast.10, bf16[1,2,256,512]{3,2,1,0:T(8,128)(2,1)} %bitcast.88, bf16[1,2,256,512]{3,2,1,0:T(8,128)(2,1)S(1)} %bitcast.86), kind=kLoop, calls=%fused_computation.19 | loop fusion | flops 3145728 | bytes 6291456 | tf_op jit(solution)/shard_map/stack | solution.py:44
  39.0 1.9 %collective-permute-start.3 = (bf16[4,2,256,512]{3,2,1,0:T(8,128)(2,1)}, bf16[4,2,256,512]{3,2,1,0:T(8,128)(2,1)}, u32[]{:S(2)}, u32[]{:S(2)}) collective-permute-start(bf16[4,2,256,512]{3,2,1,0:T(8,128)(2,1)} %get-tuple-element.11), channel_id=1, source_target_pairs={{0,64},{64,0},{128,192},{192,128},{256,320},{320,256},{384,448},{4... | collective-permute-start | bytes 6291464 | tf_op jit(solution)/shard_map/ppermute | solution.py:40
  41.0 0.0 copy-done.5
  41.0 1.5 convolution_convert_fusion
  42.5 16.4 %all-to-all-start = ((bf16[64,16,512]{2,1,0:T(8,128)(2,1)}), bf16[64,16,512]{2,1,0:T(8,128)(2,1)S(1)}, u32[]{:S(2)}, u32[]{:S(2)}) async-start(bf16[64,16,512]{2,1,0:T(8,128)(2,1)} %bitcast.6), calls=%async_computation | async-start | bytes 2097152 | tf_op jit(solution)/shard_map/all_to_all | solution.py:106
  58.8 0.0 collective-permute-done.3
  58.8 3.4 %pad_maximum_fusion = (bf16[2,4,1,256,512]{4,3,2,1,0:T(8,128)(2,1)}, bf16[2,4,1,256,512]{4,3,2,1,0:T(8,128)(2,1)}) fusion(bf16[1,4,2,256,512]{4,3,2,1,0:T(8,128)(2,1)} %bitcast.13, bf16[1,4,2,256,512]{4,3,2,1,0:T(8,128)(2,1)S(1)} %get-tuple-element.12), kind=kLoop, calls=%fused_computation.18 | loop fusion | flops 2097152 | bytes 8388608 | tf_op jit(solution)/shard_map/stack | solution.py:46
  62.2 26.5 %all-to-all-done = bf16[64,16,512]{2,1,0:T(8,128)(2,1)S(1)} async-done(((bf16[64,16,512]{2,1,0:T(8,128)(2,1)}), bf16[64,16,512]{2,1,0:T(8,128)(2,1)S(1)}, u32[]{:S(2)}, u32[]{:S(2)}) %all-to-all-start) | async-done | bytes 1048608 | tf_op jit(solution)/shard_map/all_to_all | solution.py:106
  88.7 3.1 %multiply_convert_fusion.2 = (bf16[512,2048]{1,0:T(8,128)(2,1)S(1)}, f32[512,2048]{1,0:T(8,128)S(1)}) fusion(bf16[2048,512]{1,0:T(8,128)(2,1)} %bitcast.80, bf16[64,16,512]{2,1,0:T(8,128)(2,1)S(1)} %all-to-all-done), kind=kOutput, calls=%fused_computation.13 | convolution fusion | flops 1078984704 | bytes 8912896 | tf_op jit(solution)/shard_map/dot_general | solution.py:25
  91.8 0.0 copy-start.7
  91.8 0.0 copy-done.3
  91.8 1.2 fusion.7
  93.1 0.1 copy-done.7
  93.1 2.3 %fusion.5 = bf16[512,2048]{1,0:T(8,128)(2,1)S(1)} fusion(f32[512,2048]{1,0:T(8,128)S(1)} %get-tuple-element.26, bf16[2048,512]{1,0:T(8,128)(2,1)S(1)} %bitcast.83, bf16[64,16,512]{2,1,0:T(8,128)(2,1)S(1)} %all-to-all-done), kind=kOutput, calls=%fused_computation.6 | convolution fusion | flops 1084227584 | bytes 8912896 | tf_op jit(solution)/shard_map/dot_general | solution.py:25
  95.4 1.2 fusion.8
  96.7 0.0 copy-done.9
  96.7 1.1 pad_maximum_fusion.2
  97.8 7.6 %all-to-all-start.1 = ((bf16[64,16,512]{2,1,0:T(8,128)(2,1)}), bf16[64,16,512]{2,1,0:T(8,128)(2,1)S(1)}, u32[]{:S(2)}, u32[]{:S(2)}) async-start(bf16[64,16,512]{2,1,0:T(8,128)(2,1)} %pad_maximum_fusion.2), calls=%async_computation.1 | async-start | bytes 2097152 | tf_op jit(solution)/shard_map/all_to_all | solution.py:121
  105.4 3.0 %multiply_convert_fusion.1 = bf16[2048,512]{1,0:T(8,128)(2,1)S(1)} fusion(bf16[512,2048]{1,0:T(8,128)(2,1)} %copy-done.9, bf16[64,16,512]{2,1,0:T(8,128)(2,1)S(1)} %all-to-all-done), kind=kOutput, calls=%fused_computation.12 | convolution fusion | flops 1075838976 | bytes 4718592 | tf_op jit(solution)/shard_map/dot_general | solution.py:30
  108.5 1.3 multiply_convert_fusion
  109.8 0.4 maximum_bitcast_fusion
  110.2 1.7 %slice_bitcast_fusion = bf16[4,2,256,512]{3,2,1,0:T(8,128)(2,1)} fusion(bf16[2,4,2,256,512]{4,3,2,1,0:T(8,128)(2,1)S(1)} %maximum_bitcast_fusion), kind=kLoop, calls=%fused_computation.16 | loop fusion | bytes 4194304 | tf_op jit(solution)/shard_map/squeeze | solution.py:54
  111.9 0.9 copy-done
  112.8 1.9 %collective-permute-start.4 = (bf16[4,2,256,512]{3,2,1,0:T(8,128)(2,1)}, bf16[4,2,256,512]{3,2,1,0:T(8,128)(2,1)S(1)}, u32[]{:S(2)}, u32[]{:S(2)}) collective-permute-start(bf16[4,2,256,512]{3,2,1,0:T(8,128)(2,1)} %slice_bitcast_fusion), channel_id=1, source_target_pairs={{0,64},{64,0},{128,192},{192,128},{256,320},{320,256},{384,448},{4... | collective-permute-start | bytes 6291464 | tf_op jit(solution)/shard_map/ppermute | solution.py:40
  114.7 19.8 %all-to-all-done.1 = bf16[64,16,512]{2,1,0:T(8,128)(2,1)S(1)} async-done(((bf16[64,16,512]{2,1,0:T(8,128)(2,1)}), bf16[64,16,512]{2,1,0:T(8,128)(2,1)S(1)}, u32[]{:S(2)}, u32[]{:S(2)}) %all-to-all-start.1) | async-done | bytes 1048608 | tf_op jit(solution)/shard_map/all_to_all | solution.py:121
  134.5 1.5 fusion.38
  136.0 0.0 collective-permute-done.4
  136.0 2.4 %fusion.34 = (bf16[4,2,256,512]{3,2,1,0:T(8,128)(2,1)S(1)}, f32[4,2,256,512]{3,2,1,0:T(8,128)S(1)}) fusion(bf16[4,2,256,512]{3,2,1,0:T(8,128)(2,1)S(1)} %collective-permute-done.4, bf16[2,4,2,256,512]{4,3,2,1,0:T(8,128)(2,1)} %copy-done), kind=kLoop, calls=%fused_computation.84 | loop fusion | flops 4194304 | bytes 10485760 | tf_op jit(solution)/shard_map/convert_element_type | solution.py:56
  138.4 0.2 slice_bitcast_fusion.5
  138.6 2.5 %collective-permute-start.5 = (bf16[2,256,512]{2,1,0:T(8,128)(2,1)S(1)}, bf16[2,256,512]{2,1,0:T(8,128)(2,1)S(1)}, u32[]{:S(2)}, u32[]{:S(2)}) collective-permute-start(bf16[2,256,512]{2,1,0:T(8,128)(2,1)S(1)} %get-tuple-element.8), channel_id=1, source_target_pairs={{0,384},{64,448},{128,0},{192,64},{256,128},{320,192},{384,256},{4... | collective-permute-start | bytes 1572872 | tf_op jit(solution)/shard_map/ppermute | solution.py:35
  141.1 3.3 %collective-permute-start.7 = (bf16[2,256,512]{2,1,0:T(8,128)(2,1)S(1)}, bf16[2,256,512]{2,1,0:T(8,128)(2,1)S(1)}, u32[]{:S(2)}, u32[]{:S(2)}) collective-permute-start(bf16[2,256,512]{2,1,0:T(8,128)(2,1)S(1)} %get-tuple-element.9), channel_id=1, source_target_pairs={{0,128},{64,192},{128,256},{192,320},{256,384},{320,448},{384,0},{... | collective-permute-start | bytes 1572872 | tf_op jit(solution)/shard_map/ppermute | solution.py:35
  144.5 2.7 %collective-permute-start.6 = (bf16[2,256,512]{2,1,0:T(8,128)(2,1)S(1)}, bf16[2,256,512]{2,1,0:T(8,128)(2,1)S(1)}, u32[]{:S(2)}, u32[]{:S(2)}) collective-permute-start(bf16[2,256,512]{2,1,0:T(8,128)(2,1)S(1)} %get-tuple-element.10), channel_id=1, source_target_pairs={{0,256},{64,320},{128,384},{192,448},{256,0},{320,64},{384,128},{4... | collective-permute-start | bytes 1572872 | tf_op jit(solution)/shard_map/ppermute | solution.py:35
  147.2 0.2 fusion.27
  147.4 0.7 slice.125
  148.1 0.8 fusion.26
  148.9 6.5 %collective-permute-done.5 = bf16[2,256,512]{2,1,0:T(8,128)(2,1)S(1)} collective-permute-done((bf16[2,256,512]{2,1,0:T(8,128)(2,1)S(1)}, bf16[2,256,512]{2,1,0:T(8,128)(2,1)S(1)}, u32[]{:S(2)}, u32[]{:S(2)}) %collective-permute-start.5) | collective-permute-done | bytes 524320 | tf_op jit(solution)/shard_map/ppermute | solution.py:35
  155.4 11.6 %collective-permute-done.7 = bf16[2,256,512]{2,1,0:T(8,128)(2,1)S(1)} collective-permute-done((bf16[2,256,512]{2,1,0:T(8,128)(2,1)S(1)}, bf16[2,256,512]{2,1,0:T(8,128)(2,1)S(1)}, u32[]{:S(2)}, u32[]{:S(2)}) %collective-permute-start.7) | collective-permute-done | bytes 524320 | tf_op jit(solution)/shard_map/ppermute | solution.py:35
  166.9 0.0 collective-permute-done.6
  166.9 0.3 fusion.13
  167.2 0.8 fusion.36
  (17 shorter events, 0.1 us)
Async XLA Ops:
  0.6 17.8 %copy-start.1 = (bf16[128,512]{1,0:T(8,128)(2,1)S(1)}, bf16[128,512]{1,0:T(8,128)(2,1)}, u32[]{:S(2)}) copy-start(bf16[128,512]{1,0:T(8,128)(2,1)} %param.8) | copy-start | bytes 393220
  0.6 17.8 %copy-start.6 = (f32[2,512]{1,0:T(2,128)S(1)}, f32[2,512]{1,0:T(2,128)}, u32[]{:S(2)}) copy-start(f32[2,512]{1,0:T(2,128)} %param.10) | copy-start | bytes 12292
  2.6 27.1 %collective-permute-start.2 = (bf16[2,256,512]{2,1,0:T(8,128)(2,1)S(1)}, bf16[2,256,512]{2,1,0:T(8,128)(2,1)S(1)}, u32[]{:S(2)}, u32[]{:S(2)}) collective-permute-start(bf16[2,256,512]{2,1,0:T(8,128)(2,1)S(1)} %constant_dynamic-update-slice_fusion), channel_id=1, source_target_pairs={{0,384},{64,448},{128,0},{192,64},{256,128},{320,192},{384,256},{4... | collective-permute-start | bytes 1572872 | tf_op jit(solution)/shard_map/ppermute | solution.py:35
  7.3 22.4 %collective-permute-start.1 = (bf16[2,256,512]{2,1,0:T(8,128)(2,1)S(1)}, bf16[2,256,512]{2,1,0:T(8,128)(2,1)}, u32[]{:S(2)}, u32[]{:S(2)}) collective-permute-start(bf16[2,256,512]{2,1,0:T(8,128)(2,1)S(1)} %constant_dynamic-update-slice_fusion), channel_id=1, source_target_pairs={{0,256},{64,320},{128,384},{192,448},{256,0},{320,64},{384,128},{4... | collective-permute-start | bytes 1572872 | tf_op jit(solution)/shard_map/ppermute | solution.py:35
  10.0 25.3 %collective-permute-start = (bf16[2,256,512]{2,1,0:T(8,128)(2,1)S(1)}, bf16[2,256,512]{2,1,0:T(8,128)(2,1)S(1)}, u32[]{:S(2)}, u32[]{:S(2)}) collective-permute-start(bf16[2,256,512]{2,1,0:T(8,128)(2,1)S(1)} %constant_dynamic-update-slice_fusion), channel_id=1, source_target_pairs={{0,128},{64,192},{128,256},{192,320},{256,384},{320,448},{384,0},{... | collective-permute-start | bytes 1572872 | tf_op jit(solution)/shard_map/ppermute | solution.py:35
  35.3 0.8 copy-start.4
  36.1 4.8 %copy-start.5 = (bf16[128,512]{1,0:T(8,128)(2,1)S(1)}, bf16[128,512]{1,0:T(8,128)(2,1)}, u32[]{:S(2)}) copy-start(bf16[128,512]{1,0:T(8,128)(2,1)} %param.15) | copy-start | bytes 393220
  39.0 19.8 %collective-permute-start.3 = (bf16[4,2,256,512]{3,2,1,0:T(8,128)(2,1)}, bf16[4,2,256,512]{3,2,1,0:T(8,128)(2,1)}, u32[]{:S(2)}, u32[]{:S(2)}) collective-permute-start(bf16[4,2,256,512]{3,2,1,0:T(8,128)(2,1)} %get-tuple-element.11), channel_id=1, source_target_pairs={{0,64},{64,0},{128,192},{192,128},{256,320},{320,256},{384,448},{4... | collective-permute-start | bytes 6291464 | tf_op jit(solution)/shard_map/ppermute | solution.py:40
  42.5 46.3 %all-to-all-start = ((bf16[64,16,512]{2,1,0:T(8,128)(2,1)}), bf16[64,16,512]{2,1,0:T(8,128)(2,1)S(1)}, u32[]{:S(2)}, u32[]{:S(2)}) async-start(bf16[64,16,512]{2,1,0:T(8,128)(2,1)} %bitcast.6), calls=%async_computation | async-start | bytes 2097152 | tf_op jit(solution)/shard_map/all_to_all | solution.py:106
  88.7 3.1 %copy-start.3 = (bf16[2,4,1,256,512]{4,3,2,1,0:T(8,128)(2,1)S(1)}, bf16[2,4,1,256,512]{4,3,2,1,0:T(8,128)(2,1)}, u32[]{:S(2)}) copy-start(bf16[2,4,1,256,512]{4,3,2,1,0:T(8,128)(2,1)} %get-tuple-element.6) | copy-start | bytes 6291460
  91.8 1.3 copy-start.7
  93.1 2.3 %copy-start.2 = (bf16[2,4,1,256,512]{4,3,2,1,0:T(8,128)(2,1)S(1)}, bf16[2,4,1,256,512]{4,3,2,1,0:T(8,128)(2,1)}, u32[]{:S(2)}) copy-start(bf16[2,4,1,256,512]{4,3,2,1,0:T(8,128)(2,1)} %get-tuple-element.7) | copy-start | bytes 6291460
  95.4 1.3 copy-start.9
  97.8 36.7 %all-to-all-start.1 = ((bf16[64,16,512]{2,1,0:T(8,128)(2,1)}), bf16[64,16,512]{2,1,0:T(8,128)(2,1)S(1)}, u32[]{:S(2)}, u32[]{:S(2)}) async-start(bf16[64,16,512]{2,1,0:T(8,128)(2,1)} %pad_maximum_fusion.2), calls=%async_computation.1 | async-start | bytes 2097152 | tf_op jit(solution)/shard_map/all_to_all | solution.py:121
  105.4 3.1 %copy-start.8 = (bf16[512,2048]{1,0:T(8,128)(2,1)S(1)}, bf16[512,2048]{1,0:T(8,128)(2,1)}, u32[]{:S(2)}) copy-start(bf16[512,2048]{1,0:T(8,128)(2,1)} %copy-done.7) | copy-start | bytes 6291460
  110.2 2.6 %copy-start = (bf16[2,4,2,256,512]{4,3,2,1,0:T(8,128)(2,1)}, bf16[2,4,2,256,512]{4,3,2,1,0:T(8,128)(2,1)S(1)}, u32[]{:S(2)}) copy-start(bf16[2,4,2,256,512]{4,3,2,1,0:T(8,128)(2,1)S(1)} %maximum_bitcast_fusion) | copy-start | bytes 12582916
  112.8 23.2 %collective-permute-start.4 = (bf16[4,2,256,512]{3,2,1,0:T(8,128)(2,1)}, bf16[4,2,256,512]{3,2,1,0:T(8,128)(2,1)S(1)}, u32[]{:S(2)}, u32[]{:S(2)}) collective-permute-start(bf16[4,2,256,512]{3,2,1,0:T(8,128)(2,1)} %slice_bitcast_fusion), channel_id=1, source_target_pairs={{0,64},{64,0},{128,192},{192,128},{256,320},{320,256},{384,448},{4... | collective-permute-start | bytes 6291464 | tf_op jit(solution)/shard_map/ppermute | solution.py:40
  138.6 16.8 %collective-permute-start.5 = (bf16[2,256,512]{2,1,0:T(8,128)(2,1)S(1)}, bf16[2,256,512]{2,1,0:T(8,128)(2,1)S(1)}, u32[]{:S(2)}, u32[]{:S(2)}) collective-permute-start(bf16[2,256,512]{2,1,0:T(8,128)(2,1)S(1)} %get-tuple-element.8), channel_id=1, source_target_pairs={{0,384},{64,448},{128,0},{192,64},{256,128},{320,192},{384,256},{4... | collective-permute-start | bytes 1572872 | tf_op jit(solution)/shard_map/ppermute | solution.py:35
  141.1 25.8 %collective-permute-start.7 = (bf16[2,256,512]{2,1,0:T(8,128)(2,1)S(1)}, bf16[2,256,512]{2,1,0:T(8,128)(2,1)S(1)}, u32[]{:S(2)}, u32[]{:S(2)}) collective-permute-start(bf16[2,256,512]{2,1,0:T(8,128)(2,1)S(1)} %get-tuple-element.9), channel_id=1, source_target_pairs={{0,128},{64,192},{128,256},{192,320},{256,384},{320,448},{384,0},{... | collective-permute-start | bytes 1572872 | tf_op jit(solution)/shard_map/ppermute | solution.py:35
  144.5 22.5 %collective-permute-start.6 = (bf16[2,256,512]{2,1,0:T(8,128)(2,1)S(1)}, bf16[2,256,512]{2,1,0:T(8,128)(2,1)S(1)}, u32[]{:S(2)}, u32[]{:S(2)}) collective-permute-start(bf16[2,256,512]{2,1,0:T(8,128)(2,1)S(1)} %get-tuple-element.10), channel_id=1, source_target_pairs={{0,256},{64,320},{128,384},{192,448},{256,0},{320,64},{384,128},{4... | collective-permute-start | bytes 1572872 | tf_op jit(solution)/shard_map/ppermute | solution.py:35

commit v3 on v2

--- a/solution.py
+++ b/solution.py
@@ -30,49 +30,18 @@
     return lax.dot_general(left_side, right_side, numbers, preferred_element_type=jnp.float32)
 
 
-def ring_shift(value, chips, cores, shift):
-    pairs = [(c * cores + k, ((c + shift) % chips) * cores + k) for c in range(chips) for k in range(cores)]
-    return lax.ppermute(value, "dp", pairs)
-
-
-def core_swap(value, chips, cores):
-    pairs = [(c * cores + k, c * cores + (k + 1) % cores) for c in range(chips) for k in range(cores)]
-    return lax.ppermute(value, "dp", pairs)
-
-
-def gather_weights(shard, chips, cores):
-    mine = jnp.stack([shard] + [ring_shift(shard, chips, cores, k) for k in range(1, chips)])
-    other = core_swap(mine, chips, cores)
-    both = jnp.stack([mine, other])
-    width = shard.shape[-1]
-    up = both[:, :, 0].reshape(-1, width)
-    down = both[:, :, 1].reshape(-1, width)
-    return up, down
-
-
-def scatter_grads(parts, chips, cores):
-    from_other = core_swap(parts[1], chips, cores)
-    summed = parts[0].astype(jnp.float32) + from_other.astype(jnp.float32)
-    sent = summed.astype(jnp.bfloat16)
-    total = summed[0]
-    for k in range(1, chips):
-        total = total + ring_shift(sent[k], chips, cores, -k).astype(jnp.float32)
-    return total.astype(jnp.bfloat16)
-
-
 def on_device(tokens, modality, modal_gains, routes, gate_share, up_weight, down_weight, cotangent):
     tok_count = tokens.shape[0]
     model_width = tokens.shape[1]
     expert_count = lax.axis_size("expert")
-    replica_count = lax.axis_size("dp")
-    cores = 2
-    chips = replica_count // cores
+    replica_count = lax.axis_size("x") * lax.axis_size("core")
     capacity = 4 * tok_count // expert_count
     slot_count = expert_count * capacity
     route_count = 2 * tok_count
     grad_scale = 1.0 / math.sqrt(2 * tok_count * replica_count)
     shard = jnp.concatenate([up_weight, down_weight], axis=0)
-    whole_up, whole_down = gather_weights(shard, chips, cores)
+    whole = lax.all_gather(lax.all_gather(shard, "x", axis=1, tiled=True), "core", axis=1, tiled=True)
+    whole_up, whole_down = whole[0], whole[1]
     x_float = tokens.astype(jnp.float32)
     inv_rms = lax.rsqrt(jnp.mean(x_float * x_float, axis=-1, keepdims=True) + 1e-06)
     gain_rows = jnp.where(modality[:, None] == 1, modal_gains[1][None, :], modal_gains[0][None, :])
@@ -121,11 +90,12 @@
     back = lax.all_to_all(leaving, "expert", split_axis=0, concat_axis=0, tiled=True)
     up_term = row_contract(pre_grad, expert_rows) * grad_scale
     down_term = row_contract(activated, grad_rows) * grad_scale
-    parts = jnp.stack([up_term, down_term]).astype(jnp.bfloat16)
-    parts = parts.reshape(2, cores, chips, -1, model_width).transpose(1, 2, 0, 3, 4)
-    grad_pair = scatter_grads(parts, chips, cores)
-    up_grad = grad_pair[0][None]
-    down_grad = grad_pair[1][None]
+    parts = jnp.stack([up_term, down_term], axis=1).astype(jnp.bfloat16)
+    grad_pair = lax.psum_scatter(
+        lax.psum_scatter(parts, "core", scatter_dimension=0, tiled=True), "x", scatter_dimension=0, tiled=True
+    )
+    up_grad = grad_pair[:, 0][None]
+    down_grad = grad_pair[:, 1][None]
     combined = row_contract(return_side, back.reshape(2 * slot_count, model_width))
     moe_output = combined[:tok_count].astype(jnp.bfloat16)
     normed_grad = combined[tok_count:]
@@ -137,25 +107,28 @@
 
 
 def solution(mesh):
+    dp_size, expert_size = mesh.devices.shape
+    cores = 2
+    mesh = jax.sharding.Mesh(mesh.devices.reshape(dp_size // cores, cores, expert_size), ("x", "core", "expert"))
     placed = (
-        P(("dp", "expert"), None),
-        P(("dp", "expert")),
+        P(("x", "core", "expert"), None),
+        P(("x", "core", "expert")),
         P(),
-        P(("dp", "expert"), None),
-        P(("dp", "expert")),
-        P("expert", "dp", None),
-        P("expert", "dp", None),
-        P(("dp", "expert"), None),
+        P(("x", "core", "expert"), None),
+        P(("x", "core", "expert")),
+        P("expert", ("x", "core"), None),
+        P("expert", ("x", "core"), None),
+        P(("x", "core", "expert"), None),
     )
     return jax.shard_map(
         on_device,
         mesh=mesh,
         in_specs=placed,
         out_specs=(
-            P(("dp", "expert"), None),
-            P(("dp", "expert"), None),
-            P("expert", "dp", None),
-            P("expert", "dp", None),
+            P(("x", "core", "expert"), None),
+            P(("x", "core", "expert"), None),
+            P("expert", ("x", "core"), None),
+            P("expert", ("x", "core"), None),
         ),
         check_vma=False,
     )

time: 169 us -> 178 us (1.053)
  the two profiles are of different devices: /device:TPU:24 before, /device:TPU:6 now
where the time goes in v3:
time: 178 us
  blocking collectives  85.9 us (48%)
  waiting for transfers between devices  52.6 us (30%)
  between operations  14.1 us (8%)
  matrix products  13.9 us (8%)
  other arithmetic  7.37 us (4%)
  local copies, waits for them, and re-layouts  4.15 us (2%)
    all_to_all x1, blocking collectives, on_device(): lax.all_to_all(leaving, 'expert', split_axis=0, concat_axis=0, tiled=True)  43 us
    all_to_all x1, blocking collectives, on_device(): lax.all_to_all(sending.reshape(expert_count, 2 * capacity, model_width),...  42.9 us
    all_gather x1, waiting for transfers between devices, on_device(): lax.all_gather(shard, 'x', axis=1, tiled=True)  37.1 us
    reduce_scatter x1, waiting for transfers between devices, on_device(): lax.psum_scatter(parts, 'core', scatter_dimension=0, tiled=True)  15.5 us
    dot_general x4, matrix products, row_product(): lax.dot_general(left_side, right_side, numbers, preferred_element_type=jn...  10.1 us
  transfers between devices with their start and end apart: 4, of which 2 were waited for; matrix products, arithmetic and copies ran while one was open for 6% of the time, Pallas kernels for 0%

profile of v3, /device:TPU:6, one launch (start us, length us, event | category | flops | bytes accessed | tf_op | source)
XLA Modules:
  0.0 178.2 jit_solution(408768301681310758)
XLA Ops:
  7.2 0.0 copy-start
  7.2 0.0 copy-start.5
  7.2 0.0 copy-start.2
  7.2 0.0 copy-start.1
  7.2 0.0 all-gather.3.cloned.1.call-start
  7.3 1.9 %pad_maximum_fusion.2 = bf16[2,256,512]{2,1,0:T(8,128)(2,1)} fusion(bf16[1,256,512]{2,1,0:T(8,128)(2,1)} %param.14, bf16[1,256,512]{2,1,0:T(8,128)(2,1)} %param.13), kind=kLoop, calls=%fused_computation.37 | loop fusion | flops 262144 | bytes 1048576 | tf_op jit(solution)/shard_map/concatenate | solution.py:42
  9.2 0.0 all-gather.3.cloned.1.call-update
  9.2 0.0 all-gather.5.cloned.1.call-start
  9.3 0.8 copy.18
  10.1 0.1 eq.88
  10.2 0.2 fusion.15
  10.4 0.1 convert_element_type.59
  10.6 0.1 copy.19
  10.6 0.7 convert_multiply_fusion.4
  11.3 0.7 multiply_add_fusion.1
  12.0 37.1 %all-gather.3.cloned.1.call-done = bf16[2,1024,512]{2,1,0:T(8,128)(2,1)} async-done(((bf16[2,256,512]{2,1,0:T(8,128)(2,1)}), bf16[2,1024,512]{2,1,0:T(8,128)(2,1)}) %all-gather.3.cloned.1.call-update) | async-done | bytes 2097168 | tf_op jit(solution)/shard_map/all_gather | solution.py:43
  49.1 0.0 all-gather.5.cloned.1.call-update
  49.1 0.0 reduce-scatter.3.cloned.1.call-start
  49.2 0.0 copy-done
  49.2 0.1 fusion.24
  49.3 0.1 fusion.32
  49.4 0.1 fusion.22
  49.6 0.1 fusion.21
  49.7 0.0 copy-done.5
  49.7 0.0 copy-done.2
  49.8 0.1 fusion.23
  49.9 0.0 copy-done.1
  49.9 0.4 convolution_convert_fusion
  50.3 42.9 %all_to_all.10 = bf16[64,16,512]{2,1,0:T(8,128)(2,1)S(1)} all-to-all(bf16[64,16,512]{2,1,0:T(8,128)(2,1)S(1)} %bitcast.57), channel_id=1, replica_groups=mesh['x'=4,'core'=2,'expert'=64] {'expert'}, dimensions={0} | all-to-all | bytes 2097152 | tf_op jit(solution)/shard_map/all_to_all | solution.py:75
  93.2 0.0 all-gather.5.cloned.1.call-done
  93.2 0.0 copy-start.3
  93.2 3.1 %multiply_convert_fusion.2 = (bf16[512,2048]{1,0:T(8,128)(2,1)S(1)}, f32[512,2048]{1,0:T(8,128)S(1)}) fusion(bf16[2,2048,512]{2,1,0:T(8,128)(2,1)} %all-gather.5.cloned.1.call-done, bf16[64,16,512]{2,1,0:T(8,128)(2,1)S(1)} %all_to_all.10), kind=kOutput, calls=%fused_computation.10 | convolution fusion | flops 1078984704 | bytes 8912896 | tf_op jit(solution)/shard_map/dot_general | solution.py:25
  96.3 0.0 copy-start.6
  96.3 0.0 copy-done.3
  96.3 2.8 %fusion.5 = bf16[512,2048]{1,0:T(8,128)(2,1)S(1)} fusion(f32[512,2048]{1,0:T(8,128)S(1)} %get-tuple-element.17, bf16[2,2048,512]{2,1,0:T(8,128)(2,1)S(1)} %copy-done.3, bf16[64,16,512]{2,1,0:T(8,128)(2,1)S(1)} %all_to_all.10), kind=kOutput, calls=%fused_computation.6 | convolution fusion | flops 1084227584 | bytes 8912896 | tf_op jit(solution)/shard_map/dot_general | solution.py:25
  99.1 0.0 copy-start.8
  99.1 0.0 copy-done.6
  99.2 1.3 fusion.7
  100.5 0.0 copy-done.8
  100.5 1.3 fusion.6
  101.8 2.3 %pad_maximum_fusion = bf16[2048,2,512]{2,0,1:T(8,128)(2,1)} fusion(bf16[2048,1,512]{2,0,1:T(8,128)(2,1)S(1)} %fusion.7, bf16[2048,1,512]{2,0,1:T(8,128)(2,1)S(1)} %fusion.6), kind=kLoop, calls=%fused_computation.7 | loop fusion | flops 2097152 | bytes 8388608 | tf_op jit(solution)/shard_map/stack | solution.py:93
  104.1 0.0 copy-start.9
  104.1 0.0 reduce-scatter.3.cloned.1.call-update
  104.2 0.0 reduce-scatter.5.cloned.1.call-start
  104.2 15.5 %reduce-scatter.3.cloned.1.call-done = bf16[1024,2,512]{2,0,1:T(8,128)(2,1)} async-done(((bf16[2048,2,512]{2,0,1:T(8,128)(2,1)}), bf16[1024,2,512]{2,0,1:T(8,128)(2,1)}) %reduce-scatter.3.cloned.1.call-update) | async-done | bytes 2097168 | tf_op jit(solution)/shard_map/reduce_scatter | solution.py:95
  119.7 0.0 reduce-scatter.5.cloned.1.call-update
  119.7 0.0 copy-done.9
  119.7 0.0 copy-start.4
  119.7 0.0 copy-start.7
  119.8 3.0 %fusion.13 = bf16[64,8,512]{2,1,0:T(8,128)(2,1)S(1)} fusion(bf16[512,2048]{1,0:T(8,128)(2,1)S(1)} %copy-done.9, bf16[2,2048,512]{2,1,0:T(8,128)(2,1)} %all-gather.5.cloned.1.call-done), kind=kOutput, calls=%fused_computation.22 | convolution fusion | flops 1074003968 | bytes 4718592 | tf_op jit(solution)/shard_map/dot_general | solution.py:25
  122.8 0.0 copy-done.4
  122.8 0.5 copy-done.7
  123.2 1.2 fusion.14
  124.5 0.1 pad_maximum_fusion.1
  124.6 43.0 %all_to_all.11 = bf16[64,16,512]{2,1,0:T(8,128)(2,1)S(1)} all-to-all(bf16[64,16,512]{2,1,0:T(8,128)(2,1)S(1)} %pad_maximum_fusion.1), channel_id=1, replica_groups=mesh['x'=4,'core'=2,'expert'=64] {'expert'}, dimensions={0} | all-to-all | bytes 2097152 | tf_op jit(solution)/shard_map/all_to_all | solution.py:90
  167.6 0.4 fusion.36
  168.1 0.7 slice.87
  168.8 0.2 fusion.28
  169.0 0.8 fusion.27
  169.8 0.0 reduce-scatter.5.cloned.1.call-done
  169.8 1.9 %slice_bitcast_fusion.20 = (bf16[1,256,512]{2,1,0:T(8,128)(2,1)}, bf16[1,256,512]{2,1,0:T(8,128)(2,1)}) fusion(bf16[256,2,512]{2,0,1:T(8,128)(2,1)} %reduce-scatter.5.cloned.1.call-done), kind=kLoop, calls=%fused_computation.54 | loop fusion | bytes 1048576 | tf_op jit(solution)/shard_map/broadcast_in_dim;squeeze | solution.py:98
  (7 shorter events, 0.0 us)
Async XLA Ops:
  7.2 42.0 %copy-start = (bf16[128,512]{1,0:T(8,128)(2,1)S(1)}, bf16[128,512]{1,0:T(8,128)(2,1)}, u32[]{:S(2)}) copy-start(bf16[128,512]{1,0:T(8,128)(2,1)} %param.8) | copy-start | bytes 393220
  7.2 42.5 %copy-start.5 = (s32[128]{0:T(128)S(1)}, s32[128]{0:T(128)}, u32[]{:S(2)}) copy-start(s32[128]{0:T(128)} %param.9) | copy-start | bytes 1540
  7.2 42.6 %copy-start.2 = (f32[2,512]{1,0:T(2,128)S(1)}, f32[2,512]{1,0:T(2,128)}, u32[]{:S(2)}) copy-start(f32[2,512]{1,0:T(2,128)} %param.10) | copy-start | bytes 12292
  7.2 42.7 %copy-start.1 = (bf16[128,512]{1,0:T(8,128)(2,1)S(1)}, bf16[128,512]{1,0:T(8,128)(2,1)}, u32[]{:S(2)}) copy-start(bf16[128,512]{1,0:T(8,128)(2,1)} %param.15) | copy-start | bytes 393220
  7.2 41.9 %all-gather.3.cloned.1.call-start = ((), (), s32[]{:S(2)}) async-start(), calls=%async_computation.4 | async-start | bytes 2621440 | tf_op jit(solution)/shard_map/all_gather | solution.py:43
  9.2 84.0 %all-gather.5.cloned.1.call-start = ((), (), s32[]{:S(2)}) async-start(), calls=%async_computation.5 | async-start | bytes 6291456 | tf_op jit(solution)/shard_map/all_gather | solution.py:43
  49.1 70.6 %reduce-scatter.3.cloned.1.call-start = ((), (), s32[]{:S(2)}) async-start(), calls=%async_computation.6 | async-start | bytes 6291456 | tf_op jit(solution)/shard_map/reduce_scatter | solution.py:95
  93.2 3.1 %copy-start.3 = (bf16[2,2048,512]{2,1,0:T(8,128)(2,1)S(1)}, bf16[2,2048,512]{2,1,0:T(8,128)(2,1)}, u32[]{:S(2)}) copy-start(bf16[2,2048,512]{2,1,0:T(8,128)(2,1)} %all-gather.5.cloned.1.call-done) | copy-start | bytes 12582916
  96.3 2.9 %copy-start.6 = (bf16[512,2048]{1,0:T(8,128)(2,1)}, bf16[512,2048]{1,0:T(8,128)(2,1)S(1)}, u32[]{:S(2)}) copy-start(bf16[512,2048]{1,0:T(8,128)(2,1)S(1)} %get-tuple-element.16) | copy-start | bytes 6291460
  99.1 1.3 copy-start.8
  104.1 15.6 %copy-start.9 = (bf16[512,2048]{1,0:T(8,128)(2,1)S(1)}, bf16[512,2048]{1,0:T(8,128)(2,1)}, u32[]{:S(2)}) copy-start(bf16[512,2048]{1,0:T(8,128)(2,1)} %copy-done.8) | copy-start | bytes 6291460
  104.2 65.6 %reduce-scatter.5.cloned.1.call-start = ((), (), s32[]{:S(2)}) async-start(), calls=%async_computation.7 | async-start | bytes 2621440 | tf_op jit(solution)/shard_map/reduce_scatter | solution.py:94
  119.7 3.0 %copy-start.4 = (bf16[2,2048,512]{2,1,0:T(8,128)(2,1)S(1)}, bf16[2,2048,512]{2,1,0:T(8,128)(2,1)}, u32[]{:S(2)}) copy-start(bf16[2,2048,512]{2,1,0:T(8,128)(2,1)} %all-gather.5.cloned.1.call-done) | copy-start | bytes 12582916
  119.7 3.5 %copy-start.7 = (bf16[512,2048]{1,0:T(8,128)(2,1)S(1)}, bf16[512,2048]{1,0:T(8,128)(2,1)}, u32[]{:S(2)}) copy-start(bf16[512,2048]{1,0:T(8,128)(2,1)} %copy-done.6) | copy-start | bytes 6291460
Sparse Core Ops, SparseCore 0:
  10.1 38.8 all-gather.2
  51.2 23.7 all-gather.4
  104.3 15.3 reduce-scatter.2
  122.6 34.4 reduce-scatter.4

commit v4 on v3

--- a/solution.py
+++ b/solution.py
@@ -34,13 +34,12 @@
     tok_count = tokens.shape[0]
     model_width = tokens.shape[1]
     expert_count = lax.axis_size("expert")
-    replica_count = lax.axis_size("x") * lax.axis_size("core")
+    replica_count = lax.axis_size("dp")
     capacity = 4 * tok_count // expert_count
     slot_count = expert_count * capacity
     route_count = 2 * tok_count
     grad_scale = 1.0 / math.sqrt(2 * tok_count * replica_count)
-    shard = jnp.concatenate([up_weight, down_weight], axis=0)
-    whole = lax.all_gather(lax.all_gather(shard, "x", axis=1, tiled=True), "core", axis=1, tiled=True)
+    whole = lax.all_gather(jnp.concatenate([up_weight, down_weight], axis=0), "dp", axis=1, tiled=True)
     whole_up, whole_down = whole[0], whole[1]
     x_float = tokens.astype(jnp.float32)
     inv_rms = lax.rsqrt(jnp.mean(x_float * x_float, axis=-1, keepdims=True) + 1e-06)
@@ -91,9 +90,7 @@
     up_term = row_contract(pre_grad, expert_rows) * grad_scale
     down_term = row_contract(activated, grad_rows) * grad_scale
     parts = jnp.stack([up_term, down_term], axis=1).astype(jnp.bfloat16)
-    grad_pair = lax.psum_scatter(
-        lax.psum_scatter(parts, "core", scatter_dimension=0, tiled=True), "x", scatter_dimension=0, tiled=True
-    )
+    grad_pair = lax.psum_scatter(parts, "dp", scatter_dimension=0, tiled=True)
     up_grad = grad_pair[:, 0][None]
     down_grad = grad_pair[:, 1][None]
     combined = row_contract(return_side, back.reshape(2 * slot_count, model_width))
@@ -107,28 +104,25 @@
 
 
 def solution(mesh):
-    dp_size, expert_size = mesh.devices.shape
-    cores = 2
-    mesh = jax.sharding.Mesh(mesh.devices.reshape(dp_size // cores, cores, expert_size), ("x", "core", "expert"))
     placed = (
-        P(("x", "core", "expert"), None),
-        P(("x", "core", "expert")),
+        P(("dp", "expert"), None),
+        P(("dp", "expert")),
         P(),
-        P(("x", "core", "expert"), None),
-        P(("x", "core", "expert")),
-        P("expert", ("x", "core"), None),
-        P("expert", ("x", "core"), None),
-        P(("x", "core", "expert"), None),
+        P(("dp", "expert"), None),
+        P(("dp", "expert")),
+        P("expert", "dp", None),
+        P("expert", "dp", None),
+        P(("dp", "expert"), None),
     )
     return jax.shard_map(
         on_device,
         mesh=mesh,
         in_specs=placed,
         out_specs=(
-            P(("x", "core", "expert"), None),
-            P(("x", "core", "expert"), None),
-            P("expert", ("x", "core"), None),
-            P("expert", ("x", "core"), None),
+            P(("dp", "expert"), None),
+            P(("dp", "expert"), None),
+            P("expert", "dp", None),
+            P("expert", "dp", None),
         ),
         check_vma=False,
     )

time: 178 us -> 126 us (0.71)
  waiting for transfers between devices: 52.6 us -> 0.04 us
  blocking collectives: 85.9 us -> 81.1 us
  other arithmetic: 7.37 us -> 9.81 us
  local copies, waits for them, and re-layouts: 4.15 us -> 6.5 us
    all_gather x2 -> x1, waiting for transfers between devices: 37.1 us -> 0.01 us  [on_device(): lax.all_gather(jnp.concatenate([up_weight, down_weight], axis=0), 'dp', a...]
    reduce_scatter x2 -> x1, waiting for transfers between devices: 15.5 us -> 0.01 us  [on_device(): grad_pair = lax.psum_scatter(parts, 'dp', scatter_dimension=0, tiled=True)]
    all_to_all x1, blocking collectives: 43 us -> 34.9 us  [on_device(): lax.all_to_all(leaving, 'expert', split_axis=0, concat_axis=0, tiled=True)]
    all_to_all x1, blocking collectives: 42.9 us -> 46.2 us  [on_device(): lax.all_to_all(sending.reshape(expert_count, 2 * capacity, model_width),...]
  transfers between devices with their start and end apart: 4 -> 2, of which waited for: 2 -> 0; matrix products, arithmetic and copies ran while one was open for 6% -> 11% of each run, Pallas kernels for 0% -> 0%
where the time goes in v4:
time: 126 us
  blocking collectives  81.1 us (64%)
  between operations  14.2 us (11%)
  matrix products  13.8 us (11%)
  other arithmetic  9.81 us (8%)
  local copies, waits for them, and re-layouts  6.5 us (5%)
    all_to_all x1, blocking collectives, on_device(): lax.all_to_all(sending.reshape(expert_count, 2 * capacity, model_width),...  46.2 us
    all_to_all x1, blocking collectives, on_device(): lax.all_to_all(leaving, 'expert', split_axis=0, concat_axis=0, tiled=True)  34.9 us
    dot_general x4, matrix products, row_product(): lax.dot_general(left_side, right_side, numbers, preferred_element_type=jn...  10.1 us
    dot_general x3, matrix products, row_contract(): lax.dot_general(left_side, right_side, numbers, preferred_element_type=jn...  3.07 us
    unnamed x17, local copies, waits for them, and re-layouts  2.87 us
  transfers between devices with their start and end apart: 2, of which 0 were waited for; matrix products, arithmetic and copies ran while one was open for 11% of the time, Pallas kernels for 0%

profile of v4, /device:TPU:6, one launch (start us, length us, event | category | flops | bytes accessed | tf_op | source)
XLA Modules:
  0.0 125.6 jit_solution(11324441013705255786)
XLA Ops:
  7.2 0.0 copy-start.1
  7.2 0.0 all-gather.2.cloned.1.call-start
  7.2 1.9 %pad_maximum_fusion.2 = bf16[2,256,512]{2,1,0:T(8,128)(2,1)} fusion(bf16[1,256,512]{2,1,0:T(8,128)(2,1)} %param.14, bf16[1,256,512]{2,1,0:T(8,128)(2,1)} %param.13), kind=kLoop, calls=%fused_computation.37 | loop fusion | flops 262144 | bytes 1048576 | tf_op jit(solution)/shard_map/concatenate | solution.py:42
  9.1 0.0 all-gather.2.cloned.1.call-update
  9.2 0.0 reduce-scatter.2.cloned.1.call-start
  9.2 0.8 copy.18
  10.0 0.1 eq.88
  10.1 0.2 fusion.15
  10.4 0.1 convert_element_type.59
  10.5 0.1 copy.19
  10.6 1.0 fusion.24
  11.6 0.7 convert_multiply_fusion.4
  12.3 0.7 multiply_add_fusion.1
  13.0 0.1 fusion.32
  13.1 0.1 fusion.22
  13.3 0.1 fusion.21
  13.4 0.7 broadcast_compare_fusion
  14.0 0.8 fusion.35
  14.8 1.0 fusion.23
  15.8 0.0 copy-done.1
  15.8 0.4 convolution_convert_fusion
  16.3 46.2 %all_to_all.10 = bf16[64,16,512]{2,1,0:T(8,128)(2,1)S(1)} all-to-all(bf16[64,16,512]{2,1,0:T(8,128)(2,1)S(1)} %bitcast.57), channel_id=1, replica_groups=mesh['dp'=8,'expert'=64] {'expert'}, dimensions={0} | all-to-all | bytes 2097152 | tf_op jit(solution)/shard_map/all_to_all | solution.py:74
  62.5 0.0 all-gather.2.cloned.1.call-done
  62.5 0.0 copy-start.2
  62.5 3.1 %multiply_convert_fusion.2 = (bf16[512,2048]{1,0:T(8,128)(2,1)S(1)}, f32[512,2048]{1,0:T(8,128)S(1)}) fusion(bf16[2,2048,512]{2,1,0:T(8,128)(2,1)} %all-gather.2.cloned.1.call-done, bf16[64,16,512]{2,1,0:T(8,128)(2,1)S(1)} %all_to_all.10), kind=kOutput, calls=%fused_computation.10 | convolution fusion | flops 1078984704 | bytes 8912896 | tf_op jit(solution)/shard_map/dot_general | solution.py:25
  65.5 0.0 copy-start.4
  65.5 0.0 copy-done.2
  65.6 2.8 %fusion.5 = bf16[512,2048]{1,0:T(8,128)(2,1)S(1)} fusion(f32[512,2048]{1,0:T(8,128)S(1)} %get-tuple-element.17, bf16[2,2048,512]{2,1,0:T(8,128)(2,1)S(1)} %copy-done.2, bf16[64,16,512]{2,1,0:T(8,128)(2,1)S(1)} %all_to_all.10), kind=kOutput, calls=%fused_computation.6 | convolution fusion | flops 1084227584 | bytes 8912896 | tf_op jit(solution)/shard_map/dot_general | solution.py:25
  68.4 0.0 copy-start.6
  68.4 0.0 copy-done.4
  68.4 1.3 %fusion.7 = bf16[2048,1,512]{2,0,1:T(8,128)(2,1)S(1)} fusion(bf16[512,2048]{1,0:T(8,128)(2,1)S(1)} %get-tuple-element.16, bf16[64,16,512]{2,1,0:T(8,128)(2,1)S(1)} %all_to_all.10), kind=kOutput, calls=%fused_computation.13 | convolution fusion | flops 1075838976 | bytes 4718592 | tf_op jit(solution)/shard_map/dot_general | solution.py:30
  69.7 0.0 copy-done.6
  69.7 1.3 %fusion.6 = bf16[2048,1,512]{2,0,1:T(8,128)(2,1)S(1)} fusion(bf16[512,2048]{1,0:T(8,128)(2,1)S(1)} %fusion.5, bf16[64,16,512]{2,1,0:T(8,128)(2,1)S(1)} %all_to_all.10), kind=kOutput, calls=%fused_computation.12 | convolution fusion | flops 1075838976 | bytes 4718592 | tf_op jit(solution)/shard_map/dot_general | solution.py:30
  71.1 2.3 %pad_maximum_fusion = bf16[2048,2,512]{2,0,1:T(8,128)(2,1)} fusion(bf16[2048,1,512]{2,0,1:T(8,128)(2,1)S(1)} %fusion.7, bf16[2048,1,512]{2,0,1:T(8,128)(2,1)S(1)} %fusion.6), kind=kLoop, calls=%fused_computation.7 | loop fusion | flops 2097152 | bytes 8388608 | tf_op jit(solution)/shard_map/stack | solution.py:92
  73.4 0.0 copy-start.7
  73.4 0.0 reduce-scatter.2.cloned.1.call-update
  73.4 1.6 %copy-done.7 = bf16[512,2048]{1,0:T(8,128)(2,1)S(1)} copy-done((bf16[512,2048]{1,0:T(8,128)(2,1)S(1)}, bf16[512,2048]{1,0:T(8,128)(2,1)}, u32[]{:S(2)}) %copy-start.7) | copy-done | bytes 2097176
  75.0 0.0 copy-start.3
  75.0 0.0 copy-start.5
  75.0 3.0 %fusion.13 = bf16[64,8,512]{2,1,0:T(8,128)(2,1)S(1)} fusion(bf16[512,2048]{1,0:T(8,128)(2,1)S(1)} %copy-done.7, bf16[2,2048,512]{2,1,0:T(8,128)(2,1)} %all-gather.2.cloned.1.call-done), kind=kOutput, calls=%fused_computation.22 | convolution fusion | flops 1074003968 | bytes 4718592 | tf_op jit(solution)/shard_map/dot_general | solution.py:25
  78.0 0.0 copy-done.3
  78.0 0.5 copy-done.5
  78.5 1.2 fusion.14
  79.7 0.0 copy-start
  79.8 0.1 pad_maximum_fusion.1
  79.9 34.9 %all_to_all.11 = bf16[64,16,512]{2,1,0:T(8,128)(2,1)S(1)} all-to-all(bf16[64,16,512]{2,1,0:T(8,128)(2,1)S(1)} %pad_maximum_fusion.1), channel_id=1, replica_groups=mesh['dp'=8,'expert'=64] {'expert'}, dimensions={0} | all-to-all | bytes 2097152 | tf_op jit(solution)/shard_map/all_to_all | solution.py:89
  114.8 0.4 fusion.36
  115.2 0.7 slice.87
  115.9 0.0 copy-done
  115.9 0.2 fusion.28
  116.1 0.8 fusion.27
  116.9 0.0 reduce-scatter.2.cloned.1.call-done
  116.9 1.9 %slice_bitcast_fusion.20 = (bf16[1,256,512]{2,1,0:T(8,128)(2,1)}, bf16[1,256,512]{2,1,0:T(8,128)(2,1)}) fusion(bf16[256,2,512]{2,0,1:T(8,128)(2,1)} %reduce-scatter.2.cloned.1.call-done), kind=kLoop, calls=%fused_computation.54 | loop fusion | bytes 1048576 | tf_op jit(solution)/shard_map/broadcast_in_dim;squeeze | solution.py:95
  (5 shorter events, 0.0 us)
Async XLA Ops:
  7.2 8.7 %copy-start.1 = (bf16[128,512]{1,0:T(8,128)(2,1)S(1)}, bf16[128,512]{1,0:T(8,128)(2,1)}, u32[]{:S(2)}) copy-start(bf16[128,512]{1,0:T(8,128)(2,1)} %param.15) | copy-start | bytes 393220
  7.2 55.3 %all-gather.2.cloned.1.call-start = ((), (), s32[]{:S(2)}) async-start(), calls=%async_computation.3 | async-start | bytes 4718592 | tf_op jit(solution)/shard_map/all_gather | solution.py:42
  9.2 107.8 %reduce-scatter.2.cloned.1.call-start = ((), (), s32[]{:S(2)}) async-start(), calls=%async_computation.4 | async-start | bytes 4718592 | tf_op jit(solution)/shard_map/reduce_scatter | solution.py:93
  62.5 3.1 %copy-start.2 = (bf16[2,2048,512]{2,1,0:T(8,128)(2,1)S(1)}, bf16[2,2048,512]{2,1,0:T(8,128)(2,1)}, u32[]{:S(2)}) copy-start(bf16[2,2048,512]{2,1,0:T(8,128)(2,1)} %all-gather.2.cloned.1.call-done) | copy-start | bytes 12582916
  65.5 2.9 %copy-start.4 = (bf16[512,2048]{1,0:T(8,128)(2,1)}, bf16[512,2048]{1,0:T(8,128)(2,1)S(1)}, u32[]{:S(2)}) copy-start(bf16[512,2048]{1,0:T(8,128)(2,1)S(1)} %get-tuple-element.16) | copy-start | bytes 6291460
  68.4 1.3 %copy-start.6 = (bf16[512,2048]{1,0:T(8,128)(2,1)}, bf16[512,2048]{1,0:T(8,128)(2,1)S(1)}, u32[]{:S(2)}) copy-start(bf16[512,2048]{1,0:T(8,128)(2,1)S(1)} %fusion.5) | copy-start | bytes 6291460
  73.4 1.6 %copy-start.7 = (bf16[512,2048]{1,0:T(8,128)(2,1)S(1)}, bf16[512,2048]{1,0:T(8,128)(2,1)}, u32[]{:S(2)}) copy-start(bf16[512,2048]{1,0:T(8,128)(2,1)} %copy-done.6) | copy-start | bytes 6291460
  75.0 3.0 %copy-start.3 = (bf16[2,2048,512]{2,1,0:T(8,128)(2,1)S(1)}, bf16[2,2048,512]{2,1,0:T(8,128)(2,1)}, u32[]{:S(2)}) copy-start(bf16[2,2048,512]{2,1,0:T(8,128)(2,1)} %all-gather.2.cloned.1.call-done) | copy-start | bytes 12582916
  75.0 3.5 %copy-start.5 = (bf16[512,2048]{1,0:T(8,128)(2,1)S(1)}, bf16[512,2048]{1,0:T(8,128)(2,1)}, u32[]{:S(2)}) copy-start(bf16[512,2048]{1,0:T(8,128)(2,1)} %copy-done.4) | copy-start | bytes 6291460
  79.7 36.2 %copy-start = (bf16[128,512]{1,0:T(8,128)(2,1)S(1)}, bf16[128,512]{1,0:T(8,128)(2,1)}, u32[]{:S(2)}) copy-start(bf16[128,512]{1,0:T(8,128)(2,1)} %param.8) | copy-start | bytes 393220
Sparse Core Ops, SparseCore 0:
  10.1 40.1 all-gather.1
  73.5 34.3 reduce-scatter.1

commit v5 on v4

--- a/solution.py
+++ b/solution.py
@@ -3,6 +3,8 @@
 import jax
 import jax.numpy as jnp
 from jax import lax
+from jax.experimental import pallas as pl
+from jax.experimental.pallas import tpu as pltpu
 from jax.sharding import PartitionSpec as P
 
 root_half = 0.7071067811865476
@@ -30,6 +32,63 @@
     return lax.dot_general(left_side, right_side, numbers, preferred_element_type=jnp.float32)
 
 
+def expert_body(x_ref, g_ref, up_ref, down_ref, out_ref, back_ref, grads_ref, out_acc, back_acc, *, scale):
+    step = pl.program_id(0)
+
+    @pl.when(step == 0)
+    def _():
+        out_acc[...] = jnp.zeros_like(out_acc)
+        back_acc[...] = jnp.zeros_like(back_acc)
+
+    x = x_ref[...]
+    g = g_ref[...]
+    up = up_ref[0]
+    down = down_ref[0]
+    pre_act = row_product(x, up, 1)
+    activated = gelu_value(pre_act).astype(jnp.bfloat16)
+    out_acc[...] += row_product(activated, down, 0)
+    hidden_grad = row_product(g, down, 1)
+    pre_grad = (hidden_grad * gelu_slope(pre_act)).astype(jnp.bfloat16)
+    back_acc[...] += row_product(pre_grad, up, 0)
+    grads_ref[0] = (row_contract(pre_grad, x) * scale).astype(jnp.bfloat16)
+    grads_ref[1] = (row_contract(activated, g) * scale).astype(jnp.bfloat16)
+
+    @pl.when(step == pl.num_programs(0) - 1)
+    def _():
+        out_ref[...] = out_acc[...].astype(jnp.bfloat16)
+        back_ref[...] = back_acc[...].astype(jnp.bfloat16)
+
+
+def expert_block(x_rows, g_rows, whole, scale, tile=512):
+    rows, width = x_rows.shape
+    hidden = whole.shape[1]
+    flops = 12 * rows * hidden * width
+    return pl.pallas_call(
+        lambda *refs: expert_body(*refs, scale=scale),
+        grid=(hidden // tile,),
+        in_specs=[
+            pl.BlockSpec((rows, width), lambda j: (0, 0)),
+            pl.BlockSpec((rows, width), lambda j: (0, 0)),
+            pl.BlockSpec((1, tile, width), lambda j: (0, j, 0)),
+            pl.BlockSpec((1, tile, width), lambda j: (1, j, 0)),
+        ],
+        out_specs=[
+            pl.BlockSpec((rows, width), lambda j: (0, 0)),
+            pl.BlockSpec((rows, width), lambda j: (0, 0)),
+            pl.BlockSpec((2, tile, width), lambda j: (0, j, 0)),
+        ],
+        out_shape=[
+            jax.ShapeDtypeStruct((rows, width), jnp.bfloat16),
+            jax.ShapeDtypeStruct((rows, width), jnp.bfloat16),
+            jax.ShapeDtypeStruct((2, hidden, width), jnp.bfloat16),
+        ],
+        scratch_shapes=[pltpu.VMEM((rows, width), jnp.float32), pltpu.VMEM((rows, width), jnp.float32)],
+        cost_estimate=pl.CostEstimate(
+            flops=flops, transcendentals=2 * rows * hidden, bytes_accessed=2 * (4 * rows * width + 4 * hidden * width)
+        ),
+    )(x_rows, g_rows, whole, whole)
+
+
 def on_device(tokens, modality, modal_gains, routes, gate_share, up_weight, down_weight, cotangent):
     tok_count = tokens.shape[0]
     model_width = tokens.shape[1]
@@ -40,7 +99,6 @@
     route_count = 2 * tok_count
     grad_scale = 1.0 / math.sqrt(2 * tok_count * replica_count)
     whole = lax.all_gather(jnp.concatenate([up_weight, down_weight], axis=0), "dp", axis=1, tiled=True)
-    whole_up, whole_down = whole[0], whole[1]
     x_float = tokens.astype(jnp.float32)
     inv_rms = lax.rsqrt(jnp.mean(x_float * x_float, axis=-1, keepdims=True) + 1e-06)
     gain_rows = jnp.where(modality[:, None] == 1, modal_gains[1][None, :], modal_gains[0][None, :])
@@ -76,20 +134,13 @@
     )
     expert_rows = arrived[:, :capacity].reshape(slot_count, model_width)
     grad_rows = arrived[:, capacity:].reshape(slot_count, model_width)
-    pre_act = row_product(expert_rows, whole_up, 1)
-    activated = gelu_value(pre_act).astype(jnp.bfloat16)
-    expert_out = row_product(activated, whole_down, 0).astype(jnp.bfloat16)
-    hidden_grad = row_product(grad_rows, whole_down, 1)
-    pre_grad = (hidden_grad * gelu_slope(pre_act)).astype(jnp.bfloat16)
-    normed_part = row_product(pre_grad, whole_up, 0).astype(jnp.bfloat16)
+    expert_out, normed_part, parts = expert_block(expert_rows, grad_rows, whole, grad_scale)
     leaving = jnp.concatenate(
         [expert_out.reshape(expert_count, capacity, model_width), normed_part.reshape(expert_count, capacity, model_width)],
         axis=1,
     )
     back = lax.all_to_all(leaving, "expert", split_axis=0, concat_axis=0, tiled=True)
-    up_term = row_contract(pre_grad, expert_rows) * grad_scale
-    down_term = row_contract(activated, grad_rows) * grad_scale
-    parts = jnp.stack([up_term, down_term], axis=1).astype(jnp.bfloat16)
+    parts = parts.transpose(1, 0, 2)
     grad_pair = lax.psum_scatter(parts, "dp", scatter_dimension=0, tiled=True)
     up_grad = grad_pair[:, 0][None]
     down_grad = grad_pair[:, 1][None]

time: 126 us -> 119 us (0.944)
  matrix products: 13.8 us -> 1.09 us
  Pallas kernels: 0 us -> 11.3 us
  other arithmetic: 9.81 us -> 3.79 us
    pallas_call x0 -> x1, Pallas kernels: none -> 11.3 us  [expert_block(): pl.pallas_call(lambda *refs: expert_body(*refs, scale=scale), grid=(hidde...]
    dot_general x4 -> x0, matrix products: 10.1 us -> none  [row_product(): lax.dot_general(left_side, right_side, numbers, preferred_element_type=jn...]
    dot_general x3 -> x1, matrix products: 3.07 us -> 0.45 us  [row_contract(): lax.dot_general(left_side, right_side, numbers, preferred_element_type=jn...]
    another operation x1 -> x0, other arithmetic: 2.34 us -> none  [on_device(): parts = jnp.stack([up_term, down_term], axis=1).astype(jnp.bfloat16)]
  transfers between devices with their start and end apart: 2 -> 2, of which waited for: 0 -> 0; matrix products, arithmetic and copies ran while one was open for 11% -> 5% of each run, Pallas kernels for 0% -> 0%
where the time goes in v5:
time: 119 us; the launch traced here: 118 us
  blocking collectives  81.1 us (68%)
  between operations  14.3 us (12%)
  Pallas kernels  11.3 us (9%)
  local copies, waits for them, and re-layouts  6 us (5%)
  other arithmetic  3.79 us (3%)
    all_to_all x1, blocking collectives, on_device(): lax.all_to_all(sending.reshape(expert_count, 2 * capacity, model_width),...  46.2 us
    all_to_all x1, blocking collectives, on_device(): lax.all_to_all(leaving, 'expert', split_axis=0, concat_axis=0, tiled=True)  34.9 us
    pallas_call x1, Pallas kernels, expert_block(): pl.pallas_call(lambda *refs: expert_body(*refs, scale=scale), grid=(hidde...  11.3 us
  transfers between devices with their start and end apart: 2, of which 0 were waited for; matrix products, arithmetic and copies ran while one was open for 5% of the time, Pallas kernels for 0%

profile of v5, /device:TPU:6, one launch (start us, length us, event | category | flops | bytes accessed | tf_op | source)
XLA Modules:
  0.0 117.6 jit_solution(9649986135749969486)
XLA Ops:
  7.2 0.0 copy-start.4
  7.2 0.0 copy-start
  7.2 0.0 copy-start.6
  7.2 0.0 copy-start.7
  7.2 0.0 copy-start.5
  7.2 0.0 copy-start.3
  7.2 0.0 all-gather.2.cloned.1.call-start
  7.3 2.0 %pad_maximum_fusion.1 = bf16[2,256,512]{2,1,0:T(8,128)(2,1)} fusion(bf16[1,256,512]{2,1,0:T(8,128)(2,1)} %param.14, bf16[1,256,512]{2,1,0:T(8,128)(2,1)} %param.13), kind=kLoop, calls=%fused_computation.14 | loop fusion | flops 262144 | bytes 1048576 | tf_op jit(solution)/shard_map/concatenate | solution.py:101
  9.3 0.0 all-gather.2.cloned.1.call-update
  9.3 0.0 reduce-scatter.2.cloned.1.call-start
  9.4 0.8 copy.18
  10.2 0.1 eq.88
  10.3 0.2 fusion
  10.5 0.1 convert_element_type.46
  10.7 0.1 copy.19
  10.8 0.0 copy-done
  10.8 0.1 fusion.9
  10.9 0.0 copy-done.6
  10.9 0.0 copy-done.4
  10.9 0.1 fusion.17
  11.1 0.1 fusion.7
  11.2 0.1 fusion.6
  11.3 0.0 copy-done.7
  11.4 0.0 copy-done.5
  11.4 0.1 fusion.8
  11.5 0.0 copy-done.3
  11.5 0.4 convolution_convert_fusion
  11.9 46.2 %all_to_all.10 = bf16[64,16,512]{2,1,0:T(8,128)(2,1)S(1)} all-to-all(bf16[64,16,512]{2,1,0:T(8,128)(2,1)S(1)} %bitcast.24), channel_id=1, replica_groups=mesh['dp'=8,'expert'=64] {'expert'}, dimensions={0} | all-to-all | bytes 2097152 | tf_op jit(solution)/shard_map/all_to_all | solution.py:132
  58.1 1.1 slice_bitcast_fusion
  59.3 0.0 all-gather.2.cloned.1.call-done.refs_2_.refs_3_
  59.3 11.3 %shard_map.111 = (bf16[512,512]{1,0:T(8,128)(2,1)}, bf16[512,512]{1,0:T(8,128)(2,1)}, bf16[2,2048,512]{2,1,0:T(8,128)(2,1)}) custom-call(bf16[512,512]{1,0:T(8,128)(2,1)} %get-tuple-element.11.refs_0_, bf16[512,512]{1,0:T(8,128)(2,1)} %get-tuple-element.10.refs_1_, bf16[2,2048,512]{2,1,0:T(8,128)(2,1)} %all-gather.2.cloned.1.call-done.refs_2_.refs_3_, ...), custom_call_target="tpu_custom_call" | custom-call | flops 6442450944 | bytes 10485760 | tf_op jit(solution)/shard_map/pallas_call | solution.py:66
  70.5 0.0 copy-start.1
  70.5 0.0 copy-start.2
  70.5 0.0 reduce-scatter.2.cloned.1.call-update
  70.6 1.0 copy-done.1
  71.6 0.2 copy-done.2
  71.7 0.1 pad_maximum_fusion
  71.9 34.9 %all_to_all.11 = bf16[64,16,512]{2,1,0:T(8,128)(2,1)S(1)} all-to-all(bf16[64,16,512]{2,1,0:T(8,128)(2,1)S(1)} %pad_maximum_fusion), channel_id=1, replica_groups=mesh['dp'=8,'expert'=64] {'expert'}, dimensions={0} | all-to-all | bytes 2097152 | tf_op jit(solution)/shard_map/all_to_all | solution.py:142
  106.8 0.4 fusion.21
  107.3 0.7 slice.59
  107.9 0.2 fusion.13
  108.1 0.8 fusion.12
  108.9 0.0 reduce-scatter.2.cloned.1.call-done
  108.9 1.9 %slice_bitcast_fusion.2 = (bf16[1,256,512]{2,1,0:T(8,128)(2,1)}, bf16[1,256,512]{2,1,0:T(8,128)(2,1)}) fusion(bf16[256,2,512]{2,0,1:T(8,128)(2,1)} %reduce-scatter.2.cloned.1.call-done), kind=kLoop, calls=%fused_computation.31 | loop fusion | bytes 1048576 | tf_op jit(solution)/shard_map/broadcast_in_dim;squeeze | solution.py:146
  (9 shorter events, 0.1 us)
Async XLA Ops:
  7.2 3.7 %copy-start.4 = (s32[128,2]{0,1:T(2,128)S(1)}, s32[128,2]{0,1:T(2,128)}, u32[]{:S(2)}) copy-start(s32[128,2]{0,1:T(2,128)} %param.11) | copy-start | bytes 3076
  7.2 3.6 %copy-start = (bf16[128,512]{1,0:T(8,128)(2,1)S(1)}, bf16[128,512]{1,0:T(8,128)(2,1)}, u32[]{:S(2)}) copy-start(bf16[128,512]{1,0:T(8,128)(2,1)} %param.8) | copy-start | bytes 393220
  7.2 3.7 %copy-start.6 = (s32[128]{0:T(128)S(1)}, s32[128]{0:T(128)}, u32[]{:S(2)}) copy-start(s32[128]{0:T(128)} %param.12) | copy-start | bytes 1540
  7.2 4.1 %copy-start.7 = (s32[128]{0:T(128)S(1)}, s32[128]{0:T(128)}, u32[]{:S(2)}) copy-start(s32[128]{0:T(128)} %param.9) | copy-start | bytes 1540
  7.2 4.2 %copy-start.5 = (f32[2,512]{1,0:T(2,128)S(1)}, f32[2,512]{1,0:T(2,128)}, u32[]{:S(2)}) copy-start(f32[2,512]{1,0:T(2,128)} %param.10) | copy-start | bytes 12292
  7.2 4.3 %copy-start.3 = (bf16[128,512]{1,0:T(8,128)(2,1)S(1)}, bf16[128,512]{1,0:T(8,128)(2,1)}, u32[]{:S(2)}) copy-start(bf16[128,512]{1,0:T(8,128)(2,1)} %param.15) | copy-start | bytes 393220
  7.2 52.0 %all-gather.2.cloned.1.call-start = ((), (), s32[]{:S(2)}) async-start(), calls=%async_computation.3 | async-start | bytes 4718592 | tf_op jit(solution)/shard_map/all_gather | solution.py:101
  9.3 99.6 %reduce-scatter.2.cloned.1.call-start = ((), (), s32[]{:S(2)}) async-start(), calls=%async_computation.4 | async-start | bytes 4718592 | tf_op jit(solution)/shard_map/reduce_scatter | solution.py:144
  70.5 1.0 copy-start.1
  70.5 1.2 %copy-start.2 = (bf16[512,512]{1,0:T(8,128)(2,1)S(1)}, bf16[512,512]{1,0:T(8,128)(2,1)}, u32[]{:S(2)}) copy-start(bf16[512,512]{1,0:T(8,128)(2,1)} %get-tuple-element.8) | copy-start | bytes 1572868
Sparse Core Ops, SparseCore 0:
  10.2 40.1 all-gather.1
  70.7 34.6 reduce-scatter.1

commit v6 on v5

--- a/solution.py
+++ b/solution.py
@@ -45,10 +45,12 @@
     up = up_ref[0]
     down = down_ref[0]
     pre_act = row_product(x, up, 1)
-    activated = gelu_value(pre_act).astype(jnp.bfloat16)
+    half_cdf = 0.5 * (1.0 + lax.erf(pre_act * root_half))
+    activated = (pre_act * half_cdf).astype(jnp.bfloat16)
     out_acc[...] += row_product(activated, down, 0)
     hidden_grad = row_product(g, down, 1)
-    pre_grad = (hidden_grad * gelu_slope(pre_act)).astype(jnp.bfloat16)
+    slope = half_cdf + pre_act * jnp.exp(-0.5 * pre_act * pre_act) * density
+    pre_grad = (hidden_grad * slope).astype(jnp.bfloat16)
     back_acc[...] += row_product(pre_grad, up, 0)
     grads_ref[0] = (row_contract(pre_grad, x) * scale).astype(jnp.bfloat16)
     grads_ref[1] = (row_contract(activated, g) * scale).astype(jnp.bfloat16)
@@ -89,6 +91,32 @@
     )(x_rows, g_rows, whole, whole)
 
 
+def copy_pieces_body(*refs, sources, targets):
+    count = len(sources)
+    sems = refs[-1]
+    copies = []
+    for i in range(count):
+        (src, src_at), (dst, dst_at) = sources[i], targets[i]
+        source = refs[src] if src_at is None else refs[src].at[src_at]
+        target = refs[dst] if dst_at is None else refs[dst].at[dst_at]
+        copies.append(pltpu.make_async_copy(source, target, sems.at[i]))
+    for c in copies:
+        c.start()
+    for c in copies:
+        c.wait()
+
+
+def copy_pieces(arrays, out_shapes, sources, targets):
+    anywhere = pl.BlockSpec(memory_space=pl.ANY)
+    return pl.pallas_call(
+        lambda *refs: copy_pieces_body(*refs, sources=sources, targets=targets),
+        in_specs=[anywhere] * len(arrays),
+        out_specs=[anywhere] * len(out_shapes),
+        out_shape=out_shapes,
+        scratch_shapes=[pltpu.SemaphoreType.DMA((len(sources),))],
+    )(*arrays)
+
+
 def on_device(tokens, modality, modal_gains, routes, gate_share, up_weight, down_weight, cotangent):
     tok_count = tokens.shape[0]
     model_width = tokens.shape[1]
@@ -98,7 +126,9 @@
     slot_count = expert_count * capacity
     route_count = 2 * tok_count
     grad_scale = 1.0 / math.sqrt(2 * tok_count * replica_count)
-    whole = lax.all_gather(jnp.concatenate([up_weight, down_weight], axis=0), "dp", axis=1, tiled=True)
+    both = jax.ShapeDtypeStruct((2,) + up_weight.shape[1:], up_weight.dtype)
+    (shard,) = copy_pieces([up_weight, down_weight], [both], [(0, 0), (1, 0)], [(2, 0), (2, 1)])
+    whole = lax.all_gather(shard, "dp", axis=1, tiled=True)
     x_float = tokens.astype(jnp.float32)
     inv_rms = lax.rsqrt(jnp.mean(x_float * x_float, axis=-1, keepdims=True) + 1e-06)
     gain_rows = jnp.where(modality[:, None] == 1, modal_gains[1][None, :], modal_gains[0][None, :])
@@ -140,10 +170,9 @@
         axis=1,
     )
     back = lax.all_to_all(leaving, "expert", split_axis=0, concat_axis=0, tiled=True)
-    parts = parts.transpose(1, 0, 2)
-    grad_pair = lax.psum_scatter(parts, "dp", scatter_dimension=0, tiled=True)
-    up_grad = grad_pair[:, 0][None]
-    down_grad = grad_pair[:, 1][None]
+    grad_pair = lax.psum_scatter(parts, "dp", scatter_dimension=1, tiled=True)
+    one = jax.ShapeDtypeStruct((1,) + grad_pair.shape[1:], grad_pair.dtype)
+    up_grad, down_grad = copy_pieces([grad_pair], [one, one], [(0, 0), (0, 1)], [(1, 0), (2, 0)])
     combined = row_contract(return_side, back.reshape(2 * slot_count, model_width))
     moe_output = combined[:tok_count].astype(jnp.bfloat16)
     normed_grad = combined[tok_count:]

time: 119 us -> 148 us (1.24)
  Pallas kernels: 11.3 us -> 45.2 us
  other arithmetic: 3.79 us -> 1.78 us
  local copies, waits for them, and re-layouts: 6 us -> 4.15 us
    pallas_call x0 -> x2, Pallas kernels: none -> 34 us  [copy_pieces(): pl.pallas_call(lambda *refs: copy_pieces_body(*refs, sources=sources, tar...]
    concatenate x1 -> x0, other arithmetic: 2.01 us -> none  [on_device(): jnp.concatenate([up_weight, down_weight], axis=0)]
    another operation x1 -> x0, local copies, waits for them, and re-layouts: 1.85 us -> none  [on_device(): down_grad = grad_pair[:, 1][None]]
  transfers between devices with their start and end apart: 2 -> 2, of which waited for: 0 -> 0; matrix products, arithmetic and copies ran while one was open for 5% -> 4% of each run, Pallas kernels for 0% -> 0%
where the time goes in v6:
time: 148 us
  blocking collectives  81.1 us (55%)
  Pallas kernels  45.2 us (31%)
  between operations  14.3 us (10%)
  local copies, waits for them, and re-layouts  4.15 us (3%)
  other arithmetic  1.78 us (1%)
    all_to_all x1, blocking collectives, on_device(): lax.all_to_all(sending.reshape(expert_count, 2 * capacity, model_width),...  46.2 us
    all_to_all x1, blocking collectives, on_device(): lax.all_to_all(leaving, 'expert', split_axis=0, concat_axis=0, tiled=True)  35 us
    pallas_call x2, Pallas kernels, copy_pieces(): pl.pallas_call(lambda *refs: copy_pieces_body(*refs, sources=sources, tar...  34 us
    pallas_call x1, Pallas kernels, expert_block(): pl.pallas_call(lambda *refs: expert_body(*refs, scale=scale), grid=(hidde...  11.2 us
  transfers between devices with their start and end apart: 2, of which 0 were waited for; matrix products, arithmetic and copies ran while one was open for 4% of the time, Pallas kernels for 0%

profile of v6, /device:TPU:6, one launch (start us, length us, event | category | flops | bytes accessed | tf_op | source)
XLA Modules:
  0.0 147.8 jit_solution(3061458349478266679)
XLA Ops:
  7.2 0.0 copy-start.4
  7.2 0.0 copy-start
  7.2 0.0 copy-start.6
  7.2 0.0 copy-start.7
  7.2 0.0 copy-start.5
  7.2 0.0 copy-start.3
  7.2 0.0 all-gather.2.cloned.1.call-start
  7.3 17.0 %shard_map.111 = bf16[2,256,512]{2,1,0:T(8,128)(2,1)} custom-call(bf16[1,256,512]{2,1,0:T(8,128)(2,1)} %refs_0_.1, bf16[1,256,512]{2,1,0:T(8,128)(2,1)} %refs_1_.1), custom_call_target="tpu_custom_call" | custom-call | tf_op jit(solution)/shard_map/pallas_call | solution.py:111
  24.3 0.0 all-gather.2.cloned.1.call-update
  24.3 0.0 reduce-scatter.2.cloned.1.call-start
  24.4 0.8 copy.18
  25.1 0.1 eq.88
  25.3 0.2 fusion
  25.5 0.1 convert_element_type.46
  25.7 0.1 copy.19
  25.7 0.0 copy-done
  25.8 0.1 fusion.9
  25.9 0.0 copy-done.6
  25.9 0.0 copy-done.4
  25.9 0.1 fusion.17
  26.1 0.1 fusion.7
  26.2 0.1 fusion.6
  26.3 0.0 copy-done.7
  26.4 0.0 copy-done.5
  26.4 0.1 fusion.8
  26.5 0.0 copy-done.3
  26.5 0.4 convolution_convert_fusion
  26.9 46.2 %all_to_all.10 = bf16[64,16,512]{2,1,0:T(8,128)(2,1)S(1)} all-to-all(bf16[64,16,512]{2,1,0:T(8,128)(2,1)S(1)} %bitcast.19), channel_id=1, replica_groups=mesh['dp'=8,'expert'=64] {'expert'}, dimensions={0} | all-to-all | bytes 2097152 | tf_op jit(solution)/shard_map/all_to_all | solution.py:162
  73.1 1.1 slice_bitcast_fusion
  74.3 0.0 all-gather.2.cloned.1.call-done.refs_2_.refs_3_
  74.3 11.2 %shard_map.112 = (bf16[512,512]{1,0:T(8,128)(2,1)}, bf16[512,512]{1,0:T(8,128)(2,1)}, bf16[2,2048,512]{2,1,0:T(8,128)(2,1)}) custom-call(bf16[512,512]{1,0:T(8,128)(2,1)} %get-tuple-element.15.refs_0_, bf16[512,512]{1,0:T(8,128)(2,1)} %get-tuple-element.14.refs_1_, bf16[2,2048,512]{2,1,0:T(8,128)(2,1)} %all-gather.2.cloned.1.call-done.refs_2_.refs_3_, ...), custom_call_target="tpu_custom_call" | custom-call | flops 6442450944 | bytes 10485760 | tf_op jit(solution)/shard_map/pallas_call | solution.py:68
  85.5 0.0 copy-start.1
  85.5 0.0 copy-start.2
  85.5 0.0 reduce-scatter.2.cloned.1.call-update
  85.5 1.0 copy-done.1
  86.5 0.2 copy-done.2
  86.7 0.1 pad_maximum_fusion
  86.8 35.0 %all_to_all.11 = bf16[64,16,512]{2,1,0:T(8,128)(2,1)S(1)} all-to-all(bf16[64,16,512]{2,1,0:T(8,128)(2,1)S(1)} %pad_maximum_fusion), channel_id=1, replica_groups=mesh['dp'=8,'expert'=64] {'expert'}, dimensions={0} | all-to-all | bytes 2097152 | tf_op jit(solution)/shard_map/all_to_all | solution.py:172
  121.8 0.4 fusion.21
  122.2 0.7 slice.47
  122.9 0.2 fusion.13
  123.1 0.8 fusion.12
  123.9 0.0 reduce-scatter.2.cloned.1.call-done.refs_0_
  123.9 17.0 %shard_map.113 = (bf16[1,256,512]{2,1,0:T(8,128)(2,1)}, bf16[1,256,512]{2,1,0:T(8,128)(2,1)}) custom-call(bf16[2,256,512]{2,1,0:T(8,128)(2,1)} %reduce-scatter.2.cloned.1.call-done.refs_0_), custom_call_target="tpu_custom_call" | custom-call | tf_op jit(solution)/shard_map/pallas_call | solution.py:111
  (9 shorter events, 0.1 us)
Async XLA Ops:
  7.2 18.7 %copy-start.4 = (s32[128,2]{0,1:T(2,128)S(1)}, s32[128,2]{0,1:T(2,128)}, u32[]{:S(2)}) copy-start(s32[128,2]{0,1:T(2,128)} %param.11) | copy-start | bytes 3076
  7.2 18.6 %copy-start = (bf16[128,512]{1,0:T(8,128)(2,1)S(1)}, bf16[128,512]{1,0:T(8,128)(2,1)}, u32[]{:S(2)}) copy-start(bf16[128,512]{1,0:T(8,128)(2,1)} %param.8) | copy-start | bytes 393220
  7.2 18.7 %copy-start.6 = (s32[128]{0:T(128)S(1)}, s32[128]{0:T(128)}, u32[]{:S(2)}) copy-start(s32[128]{0:T(128)} %param.12) | copy-start | bytes 1540
  7.2 19.1 %copy-start.7 = (s32[128]{0:T(128)S(1)}, s32[128]{0:T(128)}, u32[]{:S(2)}) copy-start(s32[128]{0:T(128)} %param.9) | copy-start | bytes 1540
  7.2 19.1 %copy-start.5 = (f32[2,512]{1,0:T(2,128)S(1)}, f32[2,512]{1,0:T(2,128)}, u32[]{:S(2)}) copy-start(f32[2,512]{1,0:T(2,128)} %param.10) | copy-start | bytes 12292
  7.2 19.3 %copy-start.3 = (bf16[128,512]{1,0:T(8,128)(2,1)S(1)}, bf16[128,512]{1,0:T(8,128)(2,1)}, u32[]{:S(2)}) copy-start(bf16[128,512]{1,0:T(8,128)(2,1)} %param.15) | copy-start | bytes 393220
  7.2 67.0 %all-gather.2.cloned.1.call-start = ((), (), s32[]{:S(2)}) async-start(), calls=%async_computation.3 | async-start | bytes 4718592 | tf_op jit(solution)/shard_map/all_gather | solution.py:131
  24.3 99.6 %reduce-scatter.2.cloned.1.call-start = ((), (), s32[]{:S(2)}) async-start(), calls=%async_computation.4 | async-start | bytes 4718592 | tf_op jit(solution)/shard_map/reduce_scatter | solution.py:173
  85.5 1.0 copy-start.1
  85.5 1.2 copy-start.2
Sparse Core Ops, SparseCore 0:
  24.4 40.1 all-gather.1
  85.6 34.6 reduce-scatter.1

commit v7 on v5

--- a/solution.py
+++ b/solution.py
@@ -32,61 +32,58 @@
     return lax.dot_general(left_side, right_side, numbers, preferred_element_type=jnp.float32)
 
 
-def expert_body(x_ref, g_ref, up_ref, down_ref, out_ref, back_ref, grads_ref, out_acc, back_acc, *, scale):
+def expert_body(x_ref, g_ref, up_ref, down_ref, leaving_ref, grads_ref, out_acc, back_acc, *, scale):
     step = pl.program_id(0)
-
     @pl.when(step == 0)
     def _():
         out_acc[...] = jnp.zeros_like(out_acc)
         back_acc[...] = jnp.zeros_like(back_acc)
-
-    x = x_ref[...]
-    g = g_ref[...]
+    sources, capacity, width = x_ref.shape
+    x = x_ref[...].reshape(sources * capacity, width)
+    g = g_ref[...].reshape(sources * capacity, width)
     up = up_ref[0]
     down = down_ref[0]
     pre_act = row_product(x, up, 1)
-    activated = gelu_value(pre_act).astype(jnp.bfloat16)
+    half_cdf = 0.5 * (1.0 + lax.erf(pre_act * root_half))
+    activated = (pre_act * half_cdf).astype(jnp.bfloat16)
     out_acc[...] += row_product(activated, down, 0)
     hidden_grad = row_product(g, down, 1)
-    pre_grad = (hidden_grad * gelu_slope(pre_act)).astype(jnp.bfloat16)
+    slope = half_cdf + pre_act * jnp.exp(-0.5 * pre_act * pre_act) * density
+    pre_grad = (hidden_grad * slope).astype(jnp.bfloat16)
     back_acc[...] += row_product(pre_grad, up, 0)
     grads_ref[0] = (row_contract(pre_grad, x) * scale).astype(jnp.bfloat16)
     grads_ref[1] = (row_contract(activated, g) * scale).astype(jnp.bfloat16)
-
     @pl.when(step == pl.num_programs(0) - 1)
     def _():
-        out_ref[...] = out_acc[...].astype(jnp.bfloat16)
-        back_ref[...] = back_acc[...].astype(jnp.bfloat16)
+        leaving_ref[:, :capacity, :] = out_acc[...].astype(jnp.bfloat16).reshape(sources, capacity, width)
+        leaving_ref[:, capacity:, :] = back_acc[...].astype(jnp.bfloat16).reshape(sources, capacity, width)
 
-
-def expert_block(x_rows, g_rows, whole, scale, tile=512):
-    rows, width = x_rows.shape
+def expert_block(arrived, whole, scale, tile=1024):
+    sources, both, width = arrived.shape
+    capacity = both // 2
+    rows = sources * capacity
     hidden = whole.shape[1]
-    flops = 12 * rows * hidden * width
     return pl.pallas_call(
         lambda *refs: expert_body(*refs, scale=scale),
         grid=(hidden // tile,),
         in_specs=[
-            pl.BlockSpec((rows, width), lambda j: (0, 0)),
-            pl.BlockSpec((rows, width), lambda j: (0, 0)),
+            pl.BlockSpec((sources, capacity, width), lambda j: (0, 0, 0)),
+            pl.BlockSpec((sources, capacity, width), lambda j: (0, 1, 0)),
             pl.BlockSpec((1, tile, width), lambda j: (0, j, 0)),
             pl.BlockSpec((1, tile, width), lambda j: (1, j, 0)),
         ],
         out_specs=[
-            pl.BlockSpec((rows, width), lambda j: (0, 0)),
-            pl.BlockSpec((rows, width), lambda j: (0, 0)),
+            pl.BlockSpec((sources, both, width), lambda j: (0, 0, 0)),
             pl.BlockSpec((2, tile, width), lambda j: (0, j, 0)),
         ],
         out_shape=[
-            jax.ShapeDtypeStruct((rows, width), jnp.bfloat16),
-            jax.ShapeDtypeStruct((rows, width), jnp.bfloat16),
+            jax.ShapeDtypeStruct((sources, both, width), jnp.bfloat16),
             jax.ShapeDtypeStruct((2, hidden, width), jnp.bfloat16),
         ],
         scratch_shapes=[pltpu.VMEM((rows, width), jnp.float32), pltpu.VMEM((rows, width), jnp.float32)],
-        cost_estimate=pl.CostEstimate(
-            flops=flops, transcendentals=2 * rows * hidden, bytes_accessed=2 * (4 * rows * width + 4 * hidden * width)
-        ),
-    )(x_rows, g_rows, whole, whole)
+        cost_estimate=pl.CostEstimate(flops=12 * rows * hidden * width, transcendentals=2 * rows * hidden,
+                                      bytes_accessed=2 * (4 * rows * width + 4 * hidden * width)),
+    )(arrived, arrived, whole, whole)
 
 
 def on_device(tokens, modality, modal_gains, routes, gate_share, up_weight, down_weight, cotangent):
@@ -132,13 +129,7 @@
     arrived = lax.all_to_all(
         sending.reshape(expert_count, 2 * capacity, model_width), "expert", split_axis=0, concat_axis=0, tiled=True
     )
-    expert_rows = arrived[:, :capacity].reshape(slot_count, model_width)
-    grad_rows = arrived[:, capacity:].reshape(slot_count, model_width)
-    expert_out, normed_part, parts = expert_block(expert_rows, grad_rows, whole, grad_scale)
-    leaving = jnp.concatenate(
-        [expert_out.reshape(expert_count, capacity, model_width), normed_part.reshape(expert_count, capacity, model_width)],
-        axis=1,
-    )
+    leaving, parts = expert_block(arrived, whole, grad_scale)
     back = lax.all_to_all(leaving, "expert", split_axis=0, concat_axis=0, tiled=True)
     parts = parts.transpose(1, 0, 2)
     grad_pair = lax.psum_scatter(parts, "dp", scatter_dimension=0, tiled=True)

time: 119 us -> 121 us (1.017)
  other arithmetic: 3.79 us -> 7.37 us
  transfers between devices with their start and end apart: 2 -> 2, of which waited for: 0 -> 0; matrix products, arithmetic and copies ran while one was open for 5% -> 8% of each run, Pallas kernels for 0% -> 0%
where the time goes in v7:
time: 121 us
  blocking collectives  81.2 us (67%)
  between operations  14.1 us (12%)
  Pallas kernels  11.1 us (9%)
  other arithmetic  7.37 us (6%)
  local copies, waits for them, and re-layouts  5.62 us (5%)
    all_to_all x1, blocking collectives, on_device(): lax.all_to_all(sending.reshape(expert_count, 2 * capacity, model_width),...  46.3 us
    all_to_all x1, blocking collectives, on_device(): lax.all_to_all(leaving, 'expert', split_axis=0, concat_axis=0, tiled=True)  34.9 us
    pallas_call x1, Pallas kernels, expert_block(): pl.pallas_call(lambda *refs: expert_body(*refs, scale=scale), grid=(hidde...  11.1 us
  transfers between devices with their start and end apart: 2, of which 0 were waited for; matrix products, arithmetic and copies ran while one was open for 8% of the time, Pallas kernels for 0%

profile of v7, /device:TPU:6, one launch (start us, length us, event | category | flops | bytes accessed | tf_op | source)
XLA Modules:
  0.0 120.6 jit_solution(3666847779891941017)
XLA Ops:
  7.2 0.0 copy-start.2
  7.2 0.0 all-gather.2.cloned.1.call-start
  7.2 1.9 %pad_maximum_fusion = bf16[2,256,512]{2,1,0:T(8,128)(2,1)} fusion(bf16[1,256,512]{2,1,0:T(8,128)(2,1)} %param.14, bf16[1,256,512]{2,1,0:T(8,128)(2,1)} %param.13), kind=kLoop, calls=%fused_computation.11 | loop fusion | flops 262144 | bytes 1048576 | tf_op jit(solution)/shard_map/concatenate | solution.py:98
  9.1 0.0 all-gather.2.cloned.1.call-update
  9.2 0.0 reduce-scatter.2.cloned.1.call-start
  9.2 0.8 copy.18
  10.0 0.1 eq.88
  10.2 0.2 fusion
  10.4 0.1 convert_element_type.46
  10.5 0.1 copy.19
  10.6 1.0 fusion.9
  11.6 0.7 convert_multiply_fusion.4
  12.3 0.7 multiply_add_fusion.1
  13.0 0.1 fusion.17
  13.1 0.1 fusion.7
  13.3 0.1 fusion.6
  13.4 0.7 broadcast_compare_fusion
  14.1 0.8 fusion.20
  14.8 1.0 fusion.8
  15.8 0.0 copy-done.2
  15.8 0.4 convolution_convert_fusion
  16.3 46.3 %all_to_all.10.refs_0_.refs_1_ = bf16[64,16,512]{2,1,0:T(8,128)(2,1)} all-to-all(bf16[64,16,512]{2,1,0:T(8,128)(2,1)S(1)} %bitcast.18), channel_id=1, replica_groups=mesh['dp'=8,'expert'=64] {'expert'}, dimensions={0} | all-to-all | bytes 2097152 | tf_op jit(solution)/shard_map/all_to_all | solution.py:129
  62.6 0.0 all-gather.2.cloned.1.call-done.refs_2_.refs_3_
  62.6 11.1 %shard_map.111 = (bf16[64,16,512]{2,1,0:T(8,128)(2,1)}, bf16[2,2048,512]{2,1,0:T(8,128)(2,1)}) custom-call(bf16[64,16,512]{2,1,0:T(8,128)(2,1)} %all_to_all.10.refs_0_.refs_1_, bf16[64,16,512]{2,1,0:T(8,128)(2,1)} %all_to_all.10.refs_0_.refs_1_, bf16[2,2048,512]{2,1,0:T(8,128)(2,1)} %all-gather.2.cloned.1.call-done.refs_2_.refs_3_, ...), custom_call_target="tpu_custom_call" | custom-call | flops 6442450944 | bytes 10485760 | tf_op jit(solution)/shard_map/pallas_call | solution.py:66
  73.6 0.0 copy-start.1
  73.6 0.0 copy-start
  73.6 0.0 reduce-scatter.2.cloned.1.call-update
  73.6 1.2 copy-done.1
  74.8 34.9 %all_to_all.11 = bf16[64,16,512]{2,1,0:T(8,128)(2,1)S(1)} all-to-all(bf16[64,16,512]{2,1,0:T(8,128)(2,1)S(1)} %copy-done.1), channel_id=1, replica_groups=mesh['dp'=8,'expert'=64] {'expert'}, dimensions={0} | all-to-all | bytes 2097152 | tf_op jit(solution)/shard_map/all_to_all | solution.py:133
  109.7 0.4 fusion.21
  110.2 0.7 slice.47
  110.9 0.0 copy-done
  110.9 0.2 fusion.13
  111.1 0.8 fusion.12
  111.9 0.0 reduce-scatter.2.cloned.1.call-done
  111.9 1.9 %slice_bitcast_fusion = (bf16[1,256,512]{2,1,0:T(8,128)(2,1)}, bf16[1,256,512]{2,1,0:T(8,128)(2,1)}) fusion(bf16[256,2,512]{2,0,1:T(8,128)(2,1)} %reduce-scatter.2.cloned.1.call-done), kind=kLoop, calls=%fused_computation.28 | loop fusion | bytes 1048576 | tf_op jit(solution)/shard_map/broadcast_in_dim;squeeze | solution.py:137
  (5 shorter events, 0.0 us)
Async XLA Ops:
  7.2 8.7 %copy-start.2 = (bf16[128,512]{1,0:T(8,128)(2,1)S(1)}, bf16[128,512]{1,0:T(8,128)(2,1)}, u32[]{:S(2)}) copy-start(bf16[128,512]{1,0:T(8,128)(2,1)} %param.15) | copy-start | bytes 393220
  7.2 55.4 %all-gather.2.cloned.1.call-start = ((), (), s32[]{:S(2)}) async-start(), calls=%async_computation.3 | async-start | bytes 4718592 | tf_op jit(solution)/shard_map/all_gather | solution.py:98
  9.2 102.7 %reduce-scatter.2.cloned.1.call-start = ((), (), s32[]{:S(2)}) async-start(), calls=%async_computation.4 | async-start | bytes 4718592 | tf_op jit(solution)/shard_map/reduce_scatter | solution.py:135
  73.6 1.2 %copy-start.1 = (bf16[64,16,512]{2,1,0:T(8,128)(2,1)S(1)}, bf16[64,16,512]{2,1,0:T(8,128)(2,1)}, u32[]{:S(2)}) copy-start(bf16[64,16,512]{2,1,0:T(8,128)(2,1)} %get-tuple-element.6) | copy-start | bytes 3145732
  73.6 37.3 %copy-start = (bf16[128,512]{1,0:T(8,128)(2,1)S(1)}, bf16[128,512]{1,0:T(8,128)(2,1)}, u32[]{:S(2)}) copy-start(bf16[128,512]{1,0:T(8,128)(2,1)} %param.8) | copy-start | bytes 393220
Sparse Core Ops, SparseCore 0:
  10.1 40.1 all-gather.1
  73.8 34.7 reduce-scatter.1

commit v8 on v7

v8 whole, which is shorter than its diff:
```python
import math

import jax
import jax.numpy as jnp
from jax import lax
from jax.experimental import pallas as pl
from jax.experimental.pallas import tpu as pltpu
from jax.sharding import PartitionSpec as P

root_half = 0.7071067811865476
density = 0.3989422804014327


def gelu_value(values):
    return values * 0.5 * (1.0 + lax.erf(values * root_half))


def gelu_slope(values):
    return (
        0.5 * (1.0 + lax.erf(values * root_half))
        + values * jnp.exp(-0.5 * values * values) * density
    )


def row_product(left_side, right_side, right_axis):
    numbers = (((1,), (right_axis,)), ((), ()))
    return lax.dot_general(left_side, right_side, numbers, preferred_element_type=jnp.float32)


def row_contract(left_side, right_side):
    numbers = (((0,), (0,)), ((), ()))
    return lax.dot_general(left_side, right_side, numbers, preferred_element_type=jnp.float32)


def expert_body(arrived_ref, up_ref, down_ref, leaving_ref, grads_ref, out_acc, back_acc, *, scale):
    step = pl.program_id(0)
    @pl.when(step == 0)
    def _():
        out_acc[...] = jnp.zeros_like(out_acc)
        back_acc[...] = jnp.zeros_like(back_acc)
    sources, both, width = arrived_ref.shape
    capacity = both // 2
    x = arrived_ref[:, :capacity, :].reshape(sources * capacity, width)
    g = arrived_ref[:, capacity:, :].reshape(sources * capacity, width)
    up = up_ref[0]
    down = down_ref[0]
    pre_act = row_product(x, up, 1)
    half_cdf = 0.5 * (1.0 + lax.erf(pre_act * root_half))
    activated = (pre_act * half_cdf).astype(jnp.bfloat16)
    out_acc[...] += row_product(activated, down, 0)
    hidden_grad = row_product(g, down, 1)
    slope = half_cdf + pre_act * jnp.exp(-0.5 * pre_act * pre_act) * density
    pre_grad = (hidden_grad * slope).astype(jnp.bfloat16)
    back_acc[...] += row_product(pre_grad, up, 0)
    grads_ref[0] = (row_contract(pre_grad, x) * scale).astype(jnp.bfloat16)
    grads_ref[1] = (row_contract(activated, g) * scale).astype(jnp.bfloat16)
    @pl.when(step == pl.num_programs(0) - 1)
    def _():
        leaving_ref[:, :capacity, :] = out_acc[...].astype(jnp.bfloat16).reshape(sources, capacity, width)
        leaving_ref[:, capacity:, :] = back_acc[...].astype(jnp.bfloat16).reshape(sources, capacity, width)

def expert_block(arrived, whole, scale, tile=512):
    sources, both, width = arrived.shape
    capacity = both // 2
    rows = sources * capacity
    hidden = whole.shape[1]
    return pl.pallas_call(
        lambda *refs: expert_body(*refs, scale=scale),
        grid=(hidden // tile,),
        in_specs=[
            pl.BlockSpec((sources, both, width), lambda j: (0, 0, 0)),
            pl.BlockSpec((1, tile, width), lambda j: (0, j, 0)),
            pl.BlockSpec((1, tile, width), lambda j: (1, j, 0)),
        ],
        out_specs=[
            pl.BlockSpec((sources, both, width), lambda j: (0, 0, 0)),
            pl.BlockSpec((2, tile, width), lambda j: (0, j, 0)),
        ],
        out_shape=[
            jax.ShapeDtypeStruct((sources, both, width), jnp.bfloat16),
            jax.ShapeDtypeStruct((2, hidden, width), jnp.bfloat16),
        ],
        scratch_shapes=[pltpu.VMEM((rows, width), jnp.float32), pltpu.VMEM((rows, width), jnp.float32)],
        cost_estimate=pl.CostEstimate(flops=12 * rows * hidden * width, transcendentals=2 * rows * hidden,
                                      bytes_accessed=2 * (4 * rows * width + 4 * hidden * width)),
    )(arrived, whole, whole)


def prologue_body(tokens_ref, cot_ref, modality_ref, gains_ref, routes_ref, share_ref, send_ref, back_side_ref,
                  *, experts, capacity):
    tok_count, width = tokens_ref.shape
    slots = experts * capacity
    x = tokens_ref[...].astype(jnp.float32)
    inv_rms = lax.rsqrt(jnp.mean(x * x, axis=-1, keepdims=True) + 1e-06)
    gains = gains_ref[...]
    gain_rows = jnp.where(modality_ref[...] == 1, gains[1:2, :], gains[0:1, :])
    normed = (x * inv_rms * gain_rows).astype(jnp.bfloat16)
    routes = routes_ref[...]
    first = routes[0:1, :]
    second = routes[1:2, :]
    expert_ids = lax.broadcasted_iota(jnp.int32, (experts, tok_count), 0)
    hot_first = (first == expert_ids).astype(jnp.float32)
    hot_second = (second == expert_ids).astype(jnp.float32)
    rows = lax.broadcasted_iota(jnp.int32, (tok_count, tok_count), 0)
    cols = lax.broadcasted_iota(jnp.int32, (tok_count, tok_count), 1)
    after = (rows < cols).astype(jnp.bfloat16)
    earlier = jnp.dot((hot_first + hot_second).astype(jnp.bfloat16), after, preferred_element_type=jnp.float32)
    rank_first = jnp.sum(earlier * hot_first, axis=0, keepdims=True).astype(jnp.int32)
    rank_second = jnp.sum(earlier * hot_second, axis=0, keepdims=True).astype(jnp.int32)
    slot_ids = lax.broadcasted_iota(jnp.int32, (slots, tok_count), 0)
    hit_first = slot_ids == first * capacity + rank_first
    hit_second = slot_ids == second * capacity + rank_second
    gate_first = share_ref[...].astype(jnp.float32) / 16.0
    pick = (hit_first | hit_second).astype(jnp.bfloat16)
    weigh = jnp.where(hit_first, gate_first, jnp.where(hit_second, 1.0 - gate_first, 0.0)).astype(jnp.bfloat16)
    token_rows = jnp.dot(pick, normed, preferred_element_type=jnp.float32).astype(jnp.bfloat16)
    grad_rows = jnp.dot(weigh, cot_ref[...], preferred_element_type=jnp.float32).astype(jnp.bfloat16)
    send_ref[:, :capacity, :] = token_rows.reshape(experts, capacity, width)
    send_ref[:, capacity:, :] = grad_rows.reshape(experts, capacity, width)
    blank = jnp.zeros_like(pick)
    back_side_ref[:, :capacity, :] = jnp.concatenate([weigh, blank], axis=1).reshape(experts, capacity, 2 * tok_count)
    back_side_ref[:, capacity:, :] = jnp.concatenate([blank, pick], axis=1).reshape(experts, capacity, 2 * tok_count)


def prologue(tokens, cotangent, modality, modal_gains, routes, gate_share, experts, capacity):
    tok_count, width = tokens.shape
    whole = lambda shape: pl.BlockSpec(shape, lambda: (0,) * len(shape))
    return pl.pallas_call(
        lambda *refs: prologue_body(*refs, experts=experts, capacity=capacity),
        in_specs=[whole((tok_count, width)), whole((tok_count, width)), whole((tok_count, 1)), whole((2, width)),
                  whole((2, tok_count)), whole((1, tok_count))],
        out_specs=[whole((experts, 2 * capacity, width)), whole((experts, 2 * capacity, 2 * tok_count))],
        out_shape=[
            jax.ShapeDtypeStruct((experts, 2 * capacity, width), jnp.bfloat16),
            jax.ShapeDtypeStruct((experts, 2 * capacity, 2 * tok_count), jnp.bfloat16),
        ],
    )(tokens, cotangent, modality.reshape(tok_count, 1), modal_gains, routes.T, gate_share.reshape(1, tok_count))


def on_device(tokens, modality, modal_gains, routes, gate_share, up_weight, down_weight, cotangent):
    tok_count = tokens.shape[0]
    model_width = tokens.shape[1]
    expert_count = lax.axis_size("expert")
    replica_count = lax.axis_size("dp")
    capacity = 4 * tok_count // expert_count
    slot_count = expert_count * capacity
    route_count = 2 * tok_count
    grad_scale = 1.0 / math.sqrt(2 * tok_count * replica_count)
    whole = lax.all_gather(jnp.concatenate([up_weight, down_weight], axis=0), "dp", axis=1, tiled=True)
    sending, return_side = prologue(tokens, cotangent, modality, modal_gains, routes, gate_share, expert_count, capacity)
    arrived = lax.all_to_all(sending, "expert", split_axis=0, concat_axis=0, tiled=True)
    leaving, parts = expert_block(arrived, whole, grad_scale)
    back = lax.all_to_all(leaving, "expert", split_axis=0, concat_axis=0, tiled=True)
    parts = parts.transpose(1, 0, 2)
    grad_pair = lax.psum_scatter(parts, "dp", scatter_dimension=0, tiled=True)
    up_grad = grad_pair[:, 0][None]
    down_grad = grad_pair[:, 1][None]
    combined = row_contract(return_side.reshape(2 * slot_count, 2 * tok_count), back.reshape(2 * slot_count, model_width))
    x_float = tokens.astype(jnp.float32)
    inv_rms = lax.rsqrt(jnp.mean(x_float * x_float, axis=-1, keepdims=True) + 1e-06)
    gain_rows = jnp.where(modality[:, None] == 1, modal_gains[1][None, :], modal_gains[0][None, :])
    moe_output = combined[:tok_count].astype(jnp.bfloat16)
    normed_grad = combined[tok_count:]
    scaled = gain_rows * normed_grad
    token_grad = (
        inv_rms * scaled - x_float * inv_rms**3 * jnp.mean(x_float * scaled, axis=-1, keepdims=True)
    ).astype(jnp.bfloat16)
    return (moe_output, token_grad, up_grad, down_grad)


def solution(mesh):
    placed = (
        P(("dp", "expert"), None),
        P(("dp", "expert")),
        P(),
        P(("dp", "expert"), None),
        P(("dp", "expert")),
        P("expert", "dp", None),
        P("expert", "dp", None),
        P(("dp", "expert"), None),
    )
    return jax.shard_map(
        on_device,
        mesh=mesh,
        in_specs=placed,
        out_specs=(
            P(("dp", "expert"), None),
            P(("dp", "expert"), None),
            P("expert", "dp", None),
            P("expert", "dp", None),
        ),
        check_vma=False,
    )
```

time: 121 us -> 118 us (0.975)
  blocking collectives: 81.2 us -> 46.5 us
  waiting for transfers between devices: 0.04 us -> 28.7 us
  starting transfers between devices: 0.08 us -> 6.65 us
  other arithmetic: 7.37 us -> 2.89 us
  Pallas kernels: 11.1 us -> 13.7 us
  local copies, waits for them, and re-layouts: 5.62 us -> 3.94 us
    all_to_all x2 -> x1, blocking collectives: 81.2 us -> 46.5 us  [on_device(): lax.all_to_all(sending, 'expert', split_axis=0, concat_axis=0, tiled=True)]
    all_to_all x0 -> x1, waiting for transfers between devices: none -> 28.7 us  [on_device(): lax.all_to_all(leaving, 'expert', split_axis=0, concat_axis=0, tiled=True)]
    all_to_all x0 -> x1, starting transfers between devices: none -> 6.57 us  [on_device(): lax.all_to_all(leaving, 'expert', split_axis=0, concat_axis=0, tiled=True)]
    pallas_call x0 -> x1, Pallas kernels: none -> 2.58 us  [prologue(): pl.pallas_call(lambda *refs: prologue_body(*refs, experts=experts, capaci...]
    unnamed x7 -> x8, local copies, waits for them, and re-layouts: 1.99 us -> 0.01 us
    reshape x0 -> x1, local copies, waits for them, and re-layouts: none -> 1.39 us  [prologue(): modality.reshape(tok_count, 1)]
    convert_element_type x4 -> x0, other arithmetic: 1.28 us -> none  [the longest x1 1.01 us: on_device(): normed = (x_float * inv_rms * gain_rows).astype(jnp.bfloat16)]
  transfers between devices with their start and end apart: 2 -> 3, of which waited for: 0 -> 1; matrix products, arithmetic and copies ran while one was open for 8% -> 3% of each run, Pallas kernels for 0% -> 2%
where the time goes in v8:
time: 118 us; the launch traced here: 117 us
  blocking collectives  46.5 us (39%)
  waiting for transfers between devices  28.7 us (24%)
  between operations  14.1 us (12%)
  Pallas kernels  13.7 us (12%)
  starting transfers between devices  6.65 us (6%)
  local copies, waits for them, and re-layouts  3.94 us (3%)
  other arithmetic  2.89 us (2%)
    all_to_all x1, blocking collectives, on_device(): lax.all_to_all(sending, 'expert', split_axis=0, concat_axis=0, tiled=True)  46.5 us
    all_to_all x1, waiting for transfers between devices, on_device(): lax.all_to_all(leaving, 'expert', split_axis=0, concat_axis=0, tiled=True)  28.7 us
    pallas_call x1, Pallas kernels, expert_block(): pl.pallas_call(lambda *refs: expert_body(*refs, scale=scale), grid=(hidde...  11.1 us
    all_to_all x1, starting transfers between devices, on_device(): lax.all_to_all(leaving, 'expert', split_axis=0, concat_axis=0, tiled=True)  6.57 us
    pallas_call x1, Pallas kernels, prologue(): pl.pallas_call(lambda *refs: prologue_body(*refs, experts=experts, capaci...  2.58 us
  transfers between devices with their start and end apart: 3, of which 1 were waited for; matrix products, arithmetic and copies ran while one was open for 3% of the time, Pallas kernels for 2%

profile of v8, /device:TPU:6, one launch (start us, length us, event | category | flops | bytes accessed | tf_op | source)
XLA Modules:
  0.0 116.9 jit_solution(1688352307157976203)
XLA Ops:
  7.2 0.0 all-gather.2.cloned.1.call-start
  7.2 1.9 %pad_maximum_fusion = bf16[2,256,512]{2,1,0:T(8,128)(2,1)} fusion(bf16[1,256,512]{2,1,0:T(8,128)(2,1)} %param.14, bf16[1,256,512]{2,1,0:T(8,128)(2,1)} %param.13), kind=kLoop, calls=%fused_computation.1 | loop fusion | flops 262144 | bytes 1048576 | tf_op jit(solution)/shard_map/concatenate | solution.py:149
  9.1 0.0 all-gather.2.cloned.1.call-update
  9.1 0.0 reduce-scatter.2.cloned.1.call-start
  9.2 1.4 %copy.12.refs_2_ = s32[128,1]{1,0:T(8,128)} copy(s32[128,1]{0,1:T(1,128)} %bitcast.21) | data formatting | bytes 1024 | tf_op jit(solution)/shard_map/reshape | solution.py:137
  10.6 2.6 %shard_map.111 = (bf16[64,16,512]{2,1,0:T(8,128)(2,1)}, bf16[64,16,256]{2,1,0:T(8,128)(2,1)}) custom-call(bf16[128,512]{1,0:T(8,128)(2,1)} %refs_0_.1, bf16[128,512]{1,0:T(8,128)(2,1)} %refs_1_.1, s32[128,1]{1,0:T(8,128)} %copy.12.refs_2_, f32[2,512]{1,0:T(2,128)} %refs_3_.1, s32[2,128]{1,0:T(2,128)} %bitcast.19, s32[1,128]{1,0:T(1,128)} %bitcast.20), custom_call_target="tpu_custom_call" | custom-call | tf_op jit(solution)/shard_map/pallas_call | solution.py:128
  13.1 46.5 %all_to_all.10.refs_0_ = bf16[64,16,512]{2,1,0:T(8,128)(2,1)} all-to-all(bf16[64,16,512]{2,1,0:T(8,128)(2,1)} %get-tuple-element.9), channel_id=1, replica_groups=mesh['dp'=8,'expert'=64] {'expert'}, dimensions={0} | all-to-all | bytes 2097152 | tf_op jit(solution)/shard_map/all_to_all | solution.py:151
  59.6 0.0 all-gather.2.cloned.1.call-done.refs_1_.refs_2_
  59.6 11.1 %shard_map.112 = (bf16[64,16,512]{2,1,0:T(8,128)(2,1)}, bf16[2,2048,512]{2,1,0:T(8,128)(2,1)}) custom-call(bf16[64,16,512]{2,1,0:T(8,128)(2,1)} %all_to_all.10.refs_0_, bf16[2,2048,512]{2,1,0:T(8,128)(2,1)} %all-gather.2.cloned.1.call-done.refs_1_.refs_2_, bf16[2,2048,512]{2,1,0:T(8,128)(2,1)} %all-gather.2.cloned.1.call-done.refs_1_.refs_2_), custom_call_target="tpu_custom_call" | custom-call | flops 6442450944 | bytes 10485760 | tf_op jit(solution)/shard_map/pallas_call | solution.py:67
  70.7 0.0 copy-start.2
  70.8 0.0 copy-start.1
  70.8 0.0 copy-start.3
  70.8 0.0 reduce-scatter.2.cloned.1.call-update
  70.8 6.6 %all-to-all-start.1 = ((bf16[64,16,512]{2,1,0:T(8,128)(2,1)}), bf16[64,16,512]{2,1,0:T(8,128)(2,1)S(1)}, u32[]{:S(2)}, u32[]{:S(2)}) async-start(bf16[64,16,512]{2,1,0:T(8,128)(2,1)} %get-tuple-element.10), calls=%async_computation.1 | async-start | bytes 2097152 | tf_op jit(solution)/shard_map/all_to_all | solution.py:153
  77.4 0.0 copy-done.2
  77.4 0.0 copy-done.1
  77.4 28.7 %all-to-all-done.1 = bf16[64,16,512]{2,1,0:T(8,128)(2,1)S(1)} async-done(((bf16[64,16,512]{2,1,0:T(8,128)(2,1)}), bf16[64,16,512]{2,1,0:T(8,128)(2,1)S(1)}, u32[]{:S(2)}, u32[]{:S(2)}) %all-to-all-start.1) | async-done | bytes 1048608 | tf_op jit(solution)/shard_map/all_to_all | solution.py:153
  106.1 0.0 copy-done.3
  106.1 0.0 copy-start
  106.1 0.4 convolution_bitcast_fusion
  106.5 0.7 slice.37
  107.2 0.0 copy-done
  107.2 0.2 fusion
  107.4 0.8 fusion.3
  108.2 0.0 reduce-scatter.2.cloned.1.call-done
  108.2 1.9 %slice_bitcast_fusion = (bf16[1,256,512]{2,1,0:T(8,128)(2,1)}, bf16[1,256,512]{2,1,0:T(8,128)(2,1)}) fusion(bf16[256,2,512]{2,0,1:T(8,128)(2,1)} %reduce-scatter.2.cloned.1.call-done), kind=kLoop, calls=%fused_computation.10 | loop fusion | bytes 1048576 | tf_op jit(solution)/shard_map/broadcast_in_dim;squeeze | solution.py:157
  (4 shorter events, 0.0 us)
Async XLA Ops:
  7.2 52.5 %all-gather.2.cloned.1.call-start = ((), (), s32[]{:S(2)}) async-start(), calls=%async_computation.3 | async-start | bytes 4718592 | tf_op jit(solution)/shard_map/all_gather | solution.py:149
  9.1 99.1 %reduce-scatter.2.cloned.1.call-start = ((), (), s32[]{:S(2)}) async-start(), calls=%async_computation.4 | async-start | bytes 4718592 | tf_op jit(solution)/shard_map/reduce_scatter | solution.py:155
  70.7 6.6 %copy-start.2 = (s32[128]{0:T(128)S(1)}, s32[128]{0:T(128)}, u32[]{:S(2)}) copy-start(s32[128]{0:T(128)} %param.9) | copy-start | bytes 1540
  70.8 6.6 %copy-start.1 = (f32[2,512]{1,0:T(2,128)S(1)}, f32[2,512]{1,0:T(2,128)}, u32[]{:S(2)}) copy-start(f32[2,512]{1,0:T(2,128)} %refs_3_.1) | copy-start | bytes 12292
  70.8 35.3 %copy-start.3 = (bf16[64,16,256]{2,1,0:T(8,128)(2,1)S(1)}, bf16[64,16,256]{2,1,0:T(8,128)(2,1)}, u32[]{:S(2)}) copy-start(bf16[64,16,256]{2,1,0:T(8,128)(2,1)} %get-tuple-element.8) | copy-start | bytes 1572868
  70.8 35.3 %all-to-all-start.1 = ((bf16[64,16,512]{2,1,0:T(8,128)(2,1)}), bf16[64,16,512]{2,1,0:T(8,128)(2,1)S(1)}, u32[]{:S(2)}, u32[]{:S(2)}) async-start(bf16[64,16,512]{2,1,0:T(8,128)(2,1)} %get-tuple-element.10), calls=%async_computation.1 | async-start | bytes 2097152 | tf_op jit(solution)/shard_map/all_to_all | solution.py:153
  106.1 1.1 copy-start
Sparse Core Ops, SparseCore 0:
  10.1 40.1 all-gather.1
  70.9 34.6 reduce-scatter.1

commit v9 on v8

--- a/solution.py
+++ b/solution.py
@@ -86,8 +86,10 @@
     )(arrived, whole, whole)
 
 
-def prologue_body(tokens_ref, cot_ref, modality_ref, gains_ref, routes_ref, share_ref, send_ref, back_side_ref,
-                  *, experts, capacity):
+def prologue_body(tokens_ref, cot_ref, modality_ref, gains_ref, routes_ref, share_ref, up_ref, down_ref,
+                  send_ref, back_side_ref, shard_ref, *, experts, capacity):
+    shard_ref[0] = up_ref[0]
+    shard_ref[1] = down_ref[0]
     tok_count, width = tokens_ref.shape
     slots = experts * capacity
     x = tokens_ref[...].astype(jnp.float32)
@@ -122,19 +124,22 @@
     back_side_ref[:, capacity:, :] = jnp.concatenate([blank, pick], axis=1).reshape(experts, capacity, 2 * tok_count)
 
 
-def prologue(tokens, cotangent, modality, modal_gains, routes, gate_share, experts, capacity):
+def prologue(tokens, cotangent, modality, modal_gains, routes, gate_share, up_weight, down_weight, experts, capacity):
     tok_count, width = tokens.shape
     whole = lambda shape: pl.BlockSpec(shape, lambda: (0,) * len(shape))
     return pl.pallas_call(
         lambda *refs: prologue_body(*refs, experts=experts, capacity=capacity),
         in_specs=[whole((tok_count, width)), whole((tok_count, width)), whole((tok_count, 1)), whole((2, width)),
-                  whole((2, tok_count)), whole((1, tok_count))],
-        out_specs=[whole((experts, 2 * capacity, width)), whole((experts, 2 * capacity, 2 * tok_count))],
+                  whole((2, tok_count)), whole((1, tok_count)), whole(up_weight.shape), whole(down_weight.shape)],
+        out_specs=[whole((experts, 2 * capacity, width)), whole((experts, 2 * capacity, 2 * tok_count)),
+                   whole((2,) + up_weight.shape[1:])],
         out_shape=[
             jax.ShapeDtypeStruct((experts, 2 * capacity, width), jnp.bfloat16),
             jax.ShapeDtypeStruct((experts, 2 * capacity, 2 * tok_count), jnp.bfloat16),
+            jax.ShapeDtypeStruct((2,) + up_weight.shape[1:], up_weight.dtype),
         ],
-    )(tokens, cotangent, modality.reshape(tok_count, 1), modal_gains, routes.T, gate_share.reshape(1, tok_count))
+    )(tokens, cotangent, modality.reshape(tok_count, 1), modal_gains, routes.T, gate_share.reshape(1, tok_count),
+      up_weight, down_weight)
 
 
 def on_device(tokens, modality, modal_gains, routes, gate_share, up_weight, down_weight, cotangent):
@@ -144,10 +149,11 @@
     replica_count = lax.axis_size("dp")
     capacity = 4 * tok_count // expert_count
     slot_count = expert_count * capacity
-    route_count = 2 * tok_count
     grad_scale = 1.0 / math.sqrt(2 * tok_count * replica_count)
-    whole = lax.all_gather(jnp.concatenate([up_weight, down_weight], axis=0), "dp", axis=1, tiled=True)
-    sending, return_side = prologue(tokens, cotangent, modality, modal_gains, routes, gate_share, expert_count, capacity)
+    sending, return_side, shard = prologue(
+        tokens, cotangent, modality, modal_gains, routes, gate_share, up_weight, down_weight, expert_count, capacity
+    )
+    whole = lax.all_gather(shard, "dp", axis=1, tiled=True)
     arrived = lax.all_to_all(sending, "expert", split_axis=0, concat_axis=0, tiled=True)
     leaving, parts = expert_block(arrived, whole, grad_scale)
     back = lax.all_to_all(leaving, "expert", split_axis=0, concat_axis=0, tiled=True)

time: 118 us -> 119 us (level)
  other arithmetic: 2.89 us -> 1.01 us
  waiting for transfers between devices: 28.7 us -> 30 us
    concatenate x1 -> x0, other arithmetic: 1.88 us -> none  [on_device(): jnp.concatenate([up_weight, down_weight], axis=0)]
    all_to_all x1, waiting for transfers between devices: 28.7 us -> 30 us  [on_device(): lax.all_to_all(leaving, 'expert', split_axis=0, concat_axis=0, tiled=True)]
  transfers between devices with their start and end apart: 3 -> 3, of which waited for: 1 -> 1; matrix products, arithmetic and copies ran while one was open for 3% -> 2% of each run, Pallas kernels for 2% -> 0%
where the time goes in v9:
time: 119 us; the launch traced here: 117 us
  blocking collectives  46.5 us (39%)
  waiting for transfers between devices  30 us (25%)
  Pallas kernels  14.1 us (12%)
  between operations  14.1 us (12%)
  starting transfers between devices  7.29 us (6%)
  local copies, waits for them, and re-layouts  3.94 us (3%)
    all_to_all x1, blocking collectives, on_device(): lax.all_to_all(sending, 'expert', split_axis=0, concat_axis=0, tiled=True)  46.5 us
    all_to_all x1, waiting for transfers between devices, on_device(): lax.all_to_all(leaving, 'expert', split_axis=0, concat_axis=0, tiled=True)  30 us
    pallas_call x1, Pallas kernels, expert_block(): pl.pallas_call(lambda *refs: expert_body(*refs, scale=scale), grid=(hidde...  11.1 us
    all_to_all x1, starting transfers between devices, on_device(): lax.all_to_all(leaving, 'expert', split_axis=0, concat_axis=0, tiled=True)  7.21 us
    pallas_call x1, Pallas kernels, prologue(): pl.pallas_call(lambda *refs: prologue_body(*refs, experts=experts, capaci...  2.96 us
  transfers between devices with their start and end apart: 3, of which 1 were waited for; matrix products, arithmetic and copies ran while one was open for 2% of the time, Pallas kernels for 0%

profile of v9, /device:TPU:6, one launch (start us, length us, event | category | flops | bytes accessed | tf_op | source)
XLA Modules:
  0.0 117.4 jit_solution(1657657745527923659)
XLA Ops:
  7.2 0.0 all-gather.2.cloned.1.call-start
  7.2 1.4 %copy.12.refs_2_ = s32[128,1]{1,0:T(8,128)} copy(s32[128,1]{0,1:T(1,128)} %bitcast.21) | data formatting | bytes 1024 | tf_op jit(solution)/shard_map/reshape | solution.py:141
  8.6 3.0 %shard_map.111 = (bf16[64,16,512]{2,1,0:T(8,128)(2,1)}, bf16[64,16,256]{2,1,0:T(8,128)(2,1)}, bf16[2,256,512]{2,1,0:T(8,128)(2,1)}) custom-call(bf16[128,512]{1,0:T(8,128)(2,1)} %refs_0_.1, bf16[128,512]{1,0:T(8,128)(2,1)} %refs_1_.1, s32[128,1]{1,0:T(8,128)} %copy.12.refs_2_, f32[2,512]{1,0:T(2,128)} %refs_3_.1, s32[2,128]{1,0:T(2,128)} %bitcast.19, ...), custom_call_target="tpu_custom_call" | custom-call | tf_op jit(solution)/shard_map/pallas_call | solution.py:130
  11.6 0.0 all-gather.2.cloned.1.call-update
  11.6 0.0 reduce-scatter.2.cloned.1.call-start
  11.6 46.5 %all_to_all.10.refs_0_ = bf16[64,16,512]{2,1,0:T(8,128)(2,1)} all-to-all(bf16[64,16,512]{2,1,0:T(8,128)(2,1)} %get-tuple-element.10), channel_id=1, replica_groups=mesh['dp'=8,'expert'=64] {'expert'}, dimensions={0} | all-to-all | bytes 2097152 | tf_op jit(solution)/shard_map/all_to_all | solution.py:157
  58.1 0.0 all-gather.2.cloned.1.call-done.refs_1_.refs_2_
  58.1 11.1 %shard_map.112 = (bf16[64,16,512]{2,1,0:T(8,128)(2,1)}, bf16[2,2048,512]{2,1,0:T(8,128)(2,1)}) custom-call(bf16[64,16,512]{2,1,0:T(8,128)(2,1)} %all_to_all.10.refs_0_, bf16[2,2048,512]{2,1,0:T(8,128)(2,1)} %all-gather.2.cloned.1.call-done.refs_1_.refs_2_, bf16[2,2048,512]{2,1,0:T(8,128)(2,1)} %all-gather.2.cloned.1.call-done.refs_1_.refs_2_), custom_call_target="tpu_custom_call" | custom-call | flops 6442450944 | bytes 10485760 | tf_op jit(solution)/shard_map/pallas_call | solution.py:67
  69.3 0.0 copy-start.2
  69.3 0.0 copy-start.1
  69.3 0.0 copy-start.3
  69.3 0.0 reduce-scatter.2.cloned.1.call-update
  69.3 7.2 %all-to-all-start.1 = ((bf16[64,16,512]{2,1,0:T(8,128)(2,1)}), bf16[64,16,512]{2,1,0:T(8,128)(2,1)S(1)}, u32[]{:S(2)}, u32[]{:S(2)}) async-start(bf16[64,16,512]{2,1,0:T(8,128)(2,1)} %get-tuple-element.12), calls=%async_computation.1 | async-start | bytes 2097152 | tf_op jit(solution)/shard_map/all_to_all | solution.py:159
  76.5 0.0 copy-done.2
  76.5 0.0 copy-done.1
  76.6 30.0 %all-to-all-done.1 = bf16[64,16,512]{2,1,0:T(8,128)(2,1)S(1)} async-done(((bf16[64,16,512]{2,1,0:T(8,128)(2,1)}), bf16[64,16,512]{2,1,0:T(8,128)(2,1)S(1)}, u32[]{:S(2)}, u32[]{:S(2)}) %all-to-all-start.1) | async-done | bytes 1048608 | tf_op jit(solution)/shard_map/all_to_all | solution.py:159
  106.5 0.0 copy-done.3
  106.5 0.0 copy-start
  106.6 0.4 convolution_bitcast_fusion
  107.0 0.7 slice.37
  107.7 0.0 copy-done
  107.7 0.2 fusion
  107.9 0.8 fusion.3
  108.7 0.0 reduce-scatter.2.cloned.1.call-done
  108.7 1.9 %slice_bitcast_fusion = (bf16[1,256,512]{2,1,0:T(8,128)(2,1)}, bf16[1,256,512]{2,1,0:T(8,128)(2,1)}) fusion(bf16[256,2,512]{2,0,1:T(8,128)(2,1)} %reduce-scatter.2.cloned.1.call-done), kind=kLoop, calls=%fused_computation.9 | loop fusion | bytes 1048576 | tf_op jit(solution)/shard_map/broadcast_in_dim;squeeze | solution.py:163
  (4 shorter events, 0.0 us)
Async XLA Ops:
  7.2 51.0 %all-gather.2.cloned.1.call-start = ((), (), s32[]{:S(2)}) async-start(), calls=%async_computation.3 | async-start | bytes 4718592 | tf_op jit(solution)/shard_map/all_gather | solution.py:156
  11.6 97.1 %reduce-scatter.2.cloned.1.call-start = ((), (), s32[]{:S(2)}) async-start(), calls=%async_computation.4 | async-start | bytes 4718592 | tf_op jit(solution)/shard_map/reduce_scatter | solution.py:161
  69.3 7.3 %copy-start.2 = (s32[128]{0:T(128)S(1)}, s32[128]{0:T(128)}, u32[]{:S(2)}) copy-start(s32[128]{0:T(128)} %param.9) | copy-start | bytes 1540
  69.3 7.3 %copy-start.1 = (f32[2,512]{1,0:T(2,128)S(1)}, f32[2,512]{1,0:T(2,128)}, u32[]{:S(2)}) copy-start(f32[2,512]{1,0:T(2,128)} %refs_3_.1) | copy-start | bytes 12292
  69.3 37.3 %copy-start.3 = (bf16[64,16,256]{2,1,0:T(8,128)(2,1)S(1)}, bf16[64,16,256]{2,1,0:T(8,128)(2,1)}, u32[]{:S(2)}) copy-start(bf16[64,16,256]{2,1,0:T(8,128)(2,1)} %get-tuple-element.9) | copy-start | bytes 1572868
  69.3 37.2 %all-to-all-start.1 = ((bf16[64,16,512]{2,1,0:T(8,128)(2,1)}), bf16[64,16,512]{2,1,0:T(8,128)(2,1)S(1)}, u32[]{:S(2)}, u32[]{:S(2)}) async-start(bf16[64,16,512]{2,1,0:T(8,128)(2,1)} %get-tuple-element.12), calls=%async_computation.1 | async-start | bytes 2097152 | tf_op jit(solution)/shard_map/all_to_all | solution.py:159
  106.5 1.1 copy-start
Sparse Core Ops, SparseCore 0:
  11.7 40.1 all-gather.1
  69.4 35.8 reduce-scatter.1

commit v10 on v8

--- a/solution.py
+++ b/solution.py
@@ -137,6 +137,45 @@
     )(tokens, cotangent, modality.reshape(tok_count, 1), modal_gains, routes.T, gate_share.reshape(1, tok_count))
 
 
+def epilogue_body(back_ref, side_ref, tokens_ref, modality_ref, gains_ref, grads_ref, moe_ref, token_grad_ref,
+                  up_ref, down_ref):
+    up_ref[0] = grads_ref[0]
+    down_ref[0] = grads_ref[1]
+    tok_count, width = tokens_ref.shape
+    sources, both, _ = back_ref.shape
+    back = back_ref[...].reshape(sources * both, width)
+    side = side_ref[...].reshape(sources * both, 2 * tok_count)
+    combined = row_contract(side, back)
+    moe_ref[...] = combined[:tok_count].astype(jnp.bfloat16)
+    normed_grad = combined[tok_count:]
+    x = tokens_ref[...].astype(jnp.float32)
+    inv_rms = lax.rsqrt(jnp.mean(x * x, axis=-1, keepdims=True) + 1e-06)
+    gains = gains_ref[...]
+    gain_rows = jnp.where(modality_ref[...] == 1, gains[1:2, :], gains[0:1, :])
+    scaled = gain_rows * normed_grad
+    token_grad_ref[...] = (
+        inv_rms * scaled - x * inv_rms**3 * jnp.mean(x * scaled, axis=-1, keepdims=True)
+    ).astype(jnp.bfloat16)
+
+
+def epilogue(back, side, tokens, modality, modal_gains, grads):
+    tok_count, width = tokens.shape
+    whole = lambda shape: pl.BlockSpec(shape, lambda: (0,) * len(shape))
+    one = (1,) + grads.shape[1:]
+    return pl.pallas_call(
+        epilogue_body,
+        in_specs=[whole(back.shape), whole(side.shape), whole(tokens.shape), whole((tok_count, 1)),
+                  whole(modal_gains.shape), whole(grads.shape)],
+        out_specs=[whole(tokens.shape), whole(tokens.shape), whole(one), whole(one)],
+        out_shape=[
+            jax.ShapeDtypeStruct(tokens.shape, jnp.bfloat16),
+            jax.ShapeDtypeStruct(tokens.shape, jnp.bfloat16),
+            jax.ShapeDtypeStruct(one, grads.dtype),
+            jax.ShapeDtypeStruct(one, grads.dtype),
+        ],
+    )(back, side, tokens, modality.reshape(tok_count, 1), modal_gains, grads)
+
+
 def on_device(tokens, modality, modal_gains, routes, gate_share, up_weight, down_weight, cotangent):
     tok_count = tokens.shape[0]
     model_width = tokens.shape[1]
@@ -151,20 +190,8 @@
     arrived = lax.all_to_all(sending, "expert", split_axis=0, concat_axis=0, tiled=True)
     leaving, parts = expert_block(arrived, whole, grad_scale)
     back = lax.all_to_all(leaving, "expert", split_axis=0, concat_axis=0, tiled=True)
-    parts = parts.transpose(1, 0, 2)
-    grad_pair = lax.psum_scatter(parts, "dp", scatter_dimension=0, tiled=True)
-    up_grad = grad_pair[:, 0][None]
-    down_grad = grad_pair[:, 1][None]
-    combined = row_contract(return_side.reshape(2 * slot_count, 2 * tok_count), back.reshape(2 * slot_count, model_width))
-    x_float = tokens.astype(jnp.float32)
-    inv_rms = lax.rsqrt(jnp.mean(x_float * x_float, axis=-1, keepdims=True) + 1e-06)
-    gain_rows = jnp.where(modality[:, None] == 1, modal_gains[1][None, :], modal_gains[0][None, :])
-    moe_output = combined[:tok_count].astype(jnp.bfloat16)
-    normed_grad = combined[tok_count:]
-    scaled = gain_rows * normed_grad
-    token_grad = (
-        inv_rms * scaled - x_float * inv_rms**3 * jnp.mean(x_float * scaled, axis=-1, keepdims=True)
-    ).astype(jnp.bfloat16)
+    grad_pair = lax.psum_scatter(parts, "dp", scatter_dimension=1, tiled=True)
+    moe_output, token_grad, up_grad, down_grad = epilogue(back, return_side, tokens, modality, modal_gains, grad_pair)
     return (moe_output, token_grad, up_grad, down_grad)
 
 

time: 118 us -> 119 us (level)
  the two profiles are of different devices: /device:TPU:6 before, /device:TPU:8 now
where the time goes in v10:
time: 119 us
  blocking collectives  81.9 us (69%)
  Pallas kernels  16.7 us (14%)
  between operations  14 us (12%)
  local copies, waits for them, and re-layouts  2.59 us (2%)
  waiting for transfers between devices  1.92 us (2%)
  other arithmetic  1.87 us (2%)
    all_to_all x1, blocking collectives, on_device(): lax.all_to_all(sending, 'expert', split_axis=0, concat_axis=0, tiled=True)  45.9 us
    all_to_all x1, blocking collectives, on_device(): lax.all_to_all(leaving, 'expert', split_axis=0, concat_axis=0, tiled=True)  36 us
    pallas_call x1, Pallas kernels, expert_block(): pl.pallas_call(lambda *refs: expert_body(*refs, scale=scale), grid=(hidde...  11.2 us
    pallas_call x1, Pallas kernels, epilogue(): pl.pallas_call(epilogue_body, in_specs=[whole(back.shape), whole(side.sha...  2.93 us
    pallas_call x1, Pallas kernels, prologue(): pl.pallas_call(lambda *refs: prologue_body(*refs, experts=experts, capaci...  2.59 us
  transfers between devices with their start and end apart: 2, of which 1 were waited for; matrix products, arithmetic and copies ran while one was open for 1% of the time, Pallas kernels for 2%

profile of v10, /device:TPU:8, one launch (start us, length us, event | category | flops | bytes accessed | tf_op | source)
XLA Modules:
  0.0 119.1 jit_solution(7336809516759063783)
XLA Ops:
  7.2 0.0 all-gather.2.cloned.1.call-start
  7.2 1.9 %pad_maximum_fusion = bf16[2,256,512]{2,1,0:T(8,128)(2,1)} fusion(bf16[1,256,512]{2,1,0:T(8,128)(2,1)} %param.14, bf16[1,256,512]{2,1,0:T(8,128)(2,1)} %param.13), kind=kLoop, calls=%fused_computation | loop fusion | flops 262144 | bytes 1048576 | tf_op jit(solution)/shard_map/concatenate | solution.py:188
  9.1 0.0 all-gather.2.cloned.1.call-update
  9.1 0.0 reduce-scatter.2.cloned.1.call-start
  9.2 1.4 %copy.12.refs_2_.modality_ref = s32[128,1]{1,0:T(8,128)} copy(s32[128,1]{0,1:T(1,128)} %bitcast.4) | data formatting | bytes 1024 | tf_op jit(solution)/shard_map/reshape | solution.py:137
  10.6 2.6 %shard_map.111 = (bf16[64,16,512]{2,1,0:T(8,128)(2,1)}, bf16[64,16,256]{2,1,0:T(8,128)(2,1)}) custom-call(bf16[128,512]{1,0:T(8,128)(2,1)} %tokens_ref.1, bf16[128,512]{1,0:T(8,128)(2,1)} %refs_1_.1, s32[128,1]{1,0:T(8,128)} %copy.12.refs_2_.modality_ref, f32[2,512]{1,0:T(2,128)} %gains_ref.1, s32[2,128]{1,0:T(2,128)} %bitcast.3, s32[1,128]{1,0:T(1,128)} %bitcast.5), custom_call_target="tpu_custom_call" | custom-call | tf_op jit(solution)/shard_map/pallas_call | solution.py:128
  13.1 45.9 %all_to_all.10.refs_0_ = bf16[64,16,512]{2,1,0:T(8,128)(2,1)} all-to-all(bf16[64,16,512]{2,1,0:T(8,128)(2,1)} %get-tuple-element.8), channel_id=1, replica_groups=mesh['dp'=8,'expert'=64] {'expert'}, dimensions={0} | all-to-all | bytes 2097152 | tf_op jit(solution)/shard_map/all_to_all | solution.py:190
  59.1 0.0 all-gather.2.cloned.1.call-done.refs_1_.refs_2_
  59.1 11.2 %shard_map.112 = (bf16[64,16,512]{2,1,0:T(8,128)(2,1)}, bf16[2,2048,512]{2,1,0:T(8,128)(2,1)}) custom-call(bf16[64,16,512]{2,1,0:T(8,128)(2,1)} %all_to_all.10.refs_0_, bf16[2,2048,512]{2,1,0:T(8,128)(2,1)} %all-gather.2.cloned.1.call-done.refs_1_.refs_2_, bf16[2,2048,512]{2,1,0:T(8,128)(2,1)} %all-gather.2.cloned.1.call-done.refs_1_.refs_2_), custom_call_target="tpu_custom_call" | custom-call | flops 6442450944 | bytes 10485760 | tf_op jit(solution)/shard_map/pallas_call | solution.py:67
  70.2 0.0 copy-start
  70.2 0.0 reduce-scatter.2.cloned.1.call-update
  70.3 1.2 %copy-done = bf16[64,16,512]{2,1,0:T(8,128)(2,1)S(1)} copy-done((bf16[64,16,512]{2,1,0:T(8,128)(2,1)S(1)}, bf16[64,16,512]{2,1,0:T(8,128)(2,1)}, u32[]{:S(2)}) %copy-start) | copy-done | bytes 1048600
  71.5 36.0 %all_to_all.11.back_ref = bf16[64,16,512]{2,1,0:T(8,128)(2,1)} all-to-all(bf16[64,16,512]{2,1,0:T(8,128)(2,1)S(1)} %copy-done), channel_id=1, replica_groups=mesh['dp'=8,'expert'=64] {'expert'}, dimensions={0} | all-to-all | bytes 2097152 | tf_op jit(solution)/shard_map/all_to_all | solution.py:192
  107.5 1.9 %reduce-scatter.2.cloned.1.call-done.grads_ref = bf16[2,256,512]{2,1,0:T(8,128)(2,1)} async-done(((bf16[2,2048,512]{2,1,0:T(8,128)(2,1)}), bf16[2,256,512]{2,1,0:T(8,128)(2,1)}) %reduce-scatter.2.cloned.1.call-update) | async-done | bytes 524304 | tf_op jit(solution)/shard_map/reduce_scatter | solution.py:193
  109.4 2.9 %shard_map.113 = (bf16[128,512]{1,0:T(8,128)(2,1)}, bf16[128,512]{1,0:T(8,128)(2,1)}, bf16[1,256,512]{2,1,0:T(8,128)(2,1)}, bf16[1,256,512]{2,1,0:T(8,128)(2,1)}) custom-call(bf16[64,16,512]{2,1,0:T(8,128)(2,1)} %all_to_all.11.back_ref, bf16[64,16,256]{2,1,0:T(8,128)(2,1)} %get-tuple-element.10.side_ref, bf16[128,512]{1,0:T(8,128)(2,1)} %tokens_ref.1, ...), custom_call_target="tpu_custom_call" | custom-call | tf_op jit(solution)/shard_map/pallas_call | solution.py:165
Async XLA Ops:
  7.2 51.9 %all-gather.2.cloned.1.call-start = ((), (), s32[]{:S(2)}) async-start(), calls=%async_computation.3 | async-start | bytes 4718592 | tf_op jit(solution)/shard_map/all_gather | solution.py:188
  9.1 100.3 %reduce-scatter.2.cloned.1.call-start = ((), (), s32[]{:S(2)}) async-start(), calls=%async_computation.4 | async-start | bytes 4718592 | tf_op jit(solution)/shard_map/reduce_scatter | solution.py:193
  70.2 1.2 %copy-start = (bf16[64,16,512]{2,1,0:T(8,128)(2,1)S(1)}, bf16[64,16,512]{2,1,0:T(8,128)(2,1)}, u32[]{:S(2)}) copy-start(bf16[64,16,512]{2,1,0:T(8,128)(2,1)} %get-tuple-element.9) | copy-start | bytes 3145732
Sparse Core Ops, SparseCore 0:
  10.1 41.9 all-gather.1
  70.4 38.9 reduce-scatter.1

commit v11 on v8

--- a/solution.py
+++ b/solution.py
@@ -140,7 +140,8 @@
 def on_device(tokens, modality, modal_gains, routes, gate_share, up_weight, down_weight, cotangent):
     tok_count = tokens.shape[0]
     model_width = tokens.shape[1]
-    expert_count = lax.axis_size("expert")
+    expert_count = lax.axis_size("z") * lax.axis_size("y")
+    rings = lax.axis_size("z")
     replica_count = lax.axis_size("dp")
     capacity = 4 * tok_count // expert_count
     slot_count = expert_count * capacity
@@ -148,9 +149,14 @@
     grad_scale = 1.0 / math.sqrt(2 * tok_count * replica_count)
     whole = lax.all_gather(jnp.concatenate([up_weight, down_weight], axis=0), "dp", axis=1, tiled=True)
     sending, return_side = prologue(tokens, cotangent, modality, modal_gains, routes, gate_share, expert_count, capacity)
-    arrived = lax.all_to_all(sending, "expert", split_axis=0, concat_axis=0, tiled=True)
+    staged = sending.reshape(rings, expert_count // rings, 2 * capacity, model_width)
+    staged = lax.all_to_all(staged, "z", split_axis=0, concat_axis=0, tiled=True)
+    staged = lax.all_to_all(staged, "y", split_axis=1, concat_axis=1, tiled=True)
+    arrived = staged.reshape(expert_count, 2 * capacity, model_width)
     leaving, parts = expert_block(arrived, whole, grad_scale)
-    back = lax.all_to_all(leaving, "expert", split_axis=0, concat_axis=0, tiled=True)
+    staged = leaving.reshape(rings, expert_count // rings, 2 * capacity, model_width)
+    staged = lax.all_to_all(staged, "y", split_axis=1, concat_axis=1, tiled=True)
+    back = lax.all_to_all(staged, "z", split_axis=0, concat_axis=0, tiled=True)
     parts = parts.transpose(1, 0, 2)
     grad_pair = lax.psum_scatter(parts, "dp", scatter_dimension=0, tiled=True)
     up_grad = grad_pair[:, 0][None]
@@ -169,25 +175,28 @@
 
 
 def solution(mesh):
+    dp_size, expert_size = mesh.devices.shape
+    rings = math.isqrt(expert_size)
+    mesh = jax.sharding.Mesh(mesh.devices.reshape(dp_size, rings, expert_size // rings), ("dp", "z", "y"))
     placed = (
-        P(("dp", "expert"), None),
-        P(("dp", "expert")),
+        P(("dp", "z", "y"), None),
+        P(("dp", "z", "y")),
         P(),
-        P(("dp", "expert"), None),
-        P(("dp", "expert")),
-        P("expert", "dp", None),
-        P("expert", "dp", None),
-        P(("dp", "expert"), None),
+        P(("dp", "z", "y"), None),
+        P(("dp", "z", "y")),
+        P(("z", "y"), "dp", None),
+        P(("z", "y"), "dp", None),
+        P(("dp", "z", "y"), None),
     )
     return jax.shard_map(
         on_device,
         mesh=mesh,
         in_specs=placed,
         out_specs=(
-            P(("dp", "expert"), None),
-            P(("dp", "expert"), None),
-            P("expert", "dp", None),
-            P("expert", "dp", None),
+            P(("dp", "z", "y"), None),
+            P(("dp", "z", "y"), None),
+            P(("z", "y"), "dp", None),
+            P(("z", "y"), "dp", None),
         ),
         check_vma=False,
     )

time: 118 us -> 170 us (1.44)
  blocking collectives: 46.5 us -> 102 us
  local copies, waits for them, and re-layouts: 3.94 us -> 7.54 us
  waiting for transfers between devices: 28.7 us -> 25.4 us
  starting transfers between devices: 6.65 us -> 4.27 us
    all_to_all x1 -> x3, blocking collectives: 46.5 us -> 102 us  [the longest x2 62.5 us: on_device(): lax.all_to_all(staged, 'y', split_axis=1, concat_axis=1, tiled=True)]
    all_to_all x1, waiting for transfers between devices: 28.7 us -> 25.4 us  [on_device(): back = lax.all_to_all(staged, 'z', split_axis=0, concat_axis=0, tiled=True)]
    all_to_all x1, starting transfers between devices: 6.57 us -> 4.19 us  [on_device(): back = lax.all_to_all(staged, 'z', split_axis=0, concat_axis=0, tiled=True)]
    all_to_all x0 -> x3, local copies, waits for them, and re-layouts: none -> 2.31 us  [the longest x2 2.23 us: on_device(): lax.all_to_all(staged, 'y', split_axis=1, concat_axis=1, tiled=True)]
where the time goes in v11:
time: 170 us
  blocking collectives  102 us (60%)
  waiting for transfers between devices  25.4 us (15%)
  between operations  14.1 us (8%)
  Pallas kernels  13.7 us (8%)
  local copies, waits for them, and re-layouts  7.54 us (4%)
  starting transfers between devices  4.27 us (3%)
  other arithmetic  2.9 us (2%)
    all_to_all x2, blocking collectives, on_device(): lax.all_to_all(staged, 'y', split_axis=1, concat_axis=1, tiled=True)  62.5 us
    all_to_all x1, blocking collectives, on_device(): lax.all_to_all(staged, 'z', split_axis=0, concat_axis=0, tiled=True)  39 us
    all_to_all x1, waiting for transfers between devices, on_device(): back = lax.all_to_all(staged, 'z', split_axis=0, concat_axis=0, tiled=True)  25.4 us
    pallas_call x1, Pallas kernels, expert_block(): pl.pallas_call(lambda *refs: expert_body(*refs, scale=scale), grid=(hidde...  11.1 us
    all_to_all x1, starting transfers between devices, on_device(): back = lax.all_to_all(staged, 'z', split_axis=0, concat_axis=0, tiled=True)  4.19 us
  transfers between devices with their start and end apart: 3, of which 1 were waited for; matrix products, arithmetic and copies ran while one was open for 3% of the time, Pallas kernels for 2%

profile of v11, /device:TPU:6, one launch (start us, length us, event | category | flops | bytes accessed | tf_op | source)
XLA Modules:
  0.0 169.9 jit_solution(8927641541547539346)
XLA Ops:
  7.2 0.0 all-gather.2.cloned.1.call-start
  7.2 1.9 %pad_maximum_fusion = bf16[2,256,512]{2,1,0:T(8,128)(2,1)} fusion(bf16[1,256,512]{2,1,0:T(8,128)(2,1)} %param.14, bf16[1,256,512]{2,1,0:T(8,128)(2,1)} %param.13), kind=kLoop, calls=%fused_computation | loop fusion | flops 262144 | bytes 1048576 | tf_op jit(solution)/shard_map/concatenate | solution.py:150
  9.1 0.0 all-gather.2.cloned.1.call-update
  9.1 0.0 reduce-scatter.2.cloned.1.call-start
  9.2 1.4 copy.22.refs_2_
  10.6 2.6 %shard_map.111 = (bf16[64,16,512]{2,1,0:T(8,128)(2,1)}, bf16[64,16,256]{2,1,0:T(8,128)(2,1)}) custom-call(bf16[128,512]{1,0:T(8,128)(2,1)} %refs_0_.1, bf16[128,512]{1,0:T(8,128)(2,1)} %refs_1_.1, s32[128,1]{1,0:T(8,128)} %copy.22.refs_2_, f32[2,512]{1,0:T(2,128)} %refs_3_.1, s32[2,128]{1,0:T(2,128)} %bitcast.27, s32[1,128]{1,0:T(1,128)} %bitcast.28), custom_call_target="tpu_custom_call" | custom-call | tf_op jit(solution)/shard_map/pallas_call | solution.py:128
  13.1 39.0 %all_to_all.20 = bf16[8,8,16,512]{3,2,1,0:T(8,128)(2,1)S(1)} all-to-all(bf16[8,8,16,512]{3,2,1,0:T(8,128)(2,1)} %bitcast.21), channel_id=1, replica_groups=mesh['dp'=8,'z'=8,'y'=8] {'z'}, dimensions={0} | all-to-all | bytes 2097152 | tf_op jit(solution)/shard_map/all_to_all | solution.py:153
  52.2 0.1 copy.23
  52.3 33.9 %all_to_all.21 = bf16[8,8,16,512]{3,2,0,1:T(8,128)(2,1)S(1)} all-to-all(bf16[8,8,16,512]{3,2,0,1:T(8,128)(2,1)S(1)} %copy.23), channel_id=1, replica_groups=mesh['dp'=8,'z'=8,'y'=8] {'y'}, dimensions={1} | all-to-all | bytes 2097152 | tf_op jit(solution)/shard_map/all_to_all | solution.py:154
  86.1 1.2 copy.24
  87.3 0.0 all-gather.2.cloned.1.call-done.refs_1_.refs_2_
  87.3 11.1 %shard_map.112 = (bf16[64,16,512]{2,1,0:T(8,128)(2,1)}, bf16[2,2048,512]{2,1,0:T(8,128)(2,1)}) custom-call(bf16[64,16,512]{2,1,0:T(8,128)(2,1)} %bitcast.20, bf16[2,2048,512]{2,1,0:T(8,128)(2,1)} %all-gather.2.cloned.1.call-done.refs_1_.refs_2_, bf16[2,2048,512]{2,1,0:T(8,128)(2,1)} %all-gather.2.cloned.1.call-done.refs_1_.refs_2_), custom_call_target="tpu_custom_call" | custom-call | flops 6442450944 | bytes 10485760 | tf_op jit(solution)/shard_map/pallas_call | solution.py:67
  98.4 0.0 copy-start.1
  98.4 0.0 reduce-scatter.2.cloned.1.call-update
  98.4 1.2 copy-done.1
  99.6 0.0 copy-start.4
  99.6 0.0 copy-start.3
  99.6 0.0 copy-start.2
  99.6 0.1 copy.25
  99.7 0.0 copy-start
  99.7 28.6 %all_to_all.22 = bf16[8,8,16,512]{3,2,0,1:T(8,128)(2,1)S(1)} all-to-all(bf16[8,8,16,512]{3,2,0,1:T(8,128)(2,1)S(1)} %copy.25), channel_id=1, replica_groups=mesh['dp'=8,'z'=8,'y'=8] {'y'}, dimensions={1} | all-to-all | bytes 2097152 | tf_op jit(solution)/shard_map/all_to_all | solution.py:158
  128.4 1.1 copy.26
  129.4 4.2 %all-to-all-start.3 = ((bf16[8,8,16,512]{3,2,1,0:T(8,128)(2,1)}), bf16[8,8,16,512]{3,2,1,0:T(8,128)(2,1)S(1)}, u32[]{:S(2)}, u32[]{:S(2)}) async-start(bf16[8,8,16,512]{3,2,1,0:T(8,128)(2,1)} %copy.26), calls=%async_computation.3 | async-start | bytes 2097152 | tf_op jit(solution)/shard_map/all_to_all | solution.py:159
  133.6 0.0 copy-done.4
  133.6 0.0 copy-done.3
  133.7 25.4 %all-to-all-done.3 = bf16[8,8,16,512]{3,2,1,0:T(8,128)(2,1)S(1)} async-done(((bf16[8,8,16,512]{3,2,1,0:T(8,128)(2,1)}), bf16[8,8,16,512]{3,2,1,0:T(8,128)(2,1)S(1)}, u32[]{:S(2)}, u32[]{:S(2)}) %all-to-all-start.3) | async-done | bytes 1048608 | tf_op jit(solution)/shard_map/all_to_all | solution.py:159
  159.1 0.0 copy-done.2
  159.1 0.4 fusion.6
  159.5 0.7 slice.37
  160.2 0.0 copy-done
  160.2 0.2 fusion
  160.4 0.8 fusion.3
  161.2 0.0 reduce-scatter.2.cloned.1.call-done
  161.2 1.9 %slice_bitcast_fusion = (bf16[1,256,512]{2,1,0:T(8,128)(2,1)}, bf16[1,256,512]{2,1,0:T(8,128)(2,1)}) fusion(bf16[256,2,512]{2,0,1:T(8,128)(2,1)} %reduce-scatter.2.cloned.1.call-done), kind=kLoop, calls=%fused_computation.9 | loop fusion | bytes 1048576 | tf_op jit(solution)/shard_map/broadcast_in_dim;squeeze | solution.py:163
  (4 shorter events, 0.0 us)
Async XLA Ops:
  7.2 80.1 %all-gather.2.cloned.1.call-start = ((), (), s32[]{:S(2)}) async-start(), calls=%async_computation.5 | async-start | bytes 4718592 | tf_op jit(solution)/shard_map/all_gather | solution.py:150
  9.1 152.1 %reduce-scatter.2.cloned.1.call-start = ((), (), s32[]{:S(2)}) async-start(), calls=%async_computation.6 | async-start | bytes 4718592 | tf_op jit(solution)/shard_map/reduce_scatter | solution.py:161
  98.4 1.2 copy-start.1
  99.6 34.0 %copy-start.4 = (s32[128]{0:T(128)S(1)}, s32[128]{0:T(128)}, u32[]{:S(2)}) copy-start(s32[128]{0:T(128)} %param.9) | copy-start | bytes 1540
  99.6 34.0 %copy-start.3 = (f32[2,512]{1,0:T(2,128)S(1)}, f32[2,512]{1,0:T(2,128)}, u32[]{:S(2)}) copy-start(f32[2,512]{1,0:T(2,128)} %refs_3_.1) | copy-start | bytes 12292
  99.6 59.4 %copy-start.2 = (bf16[64,16,256]{2,1,0:T(8,128)(2,1)S(1)}, bf16[64,16,256]{2,1,0:T(8,128)(2,1)}, u32[]{:S(2)}) copy-start(bf16[64,16,256]{2,1,0:T(8,128)(2,1)} %get-tuple-element.8) | copy-start | bytes 1572868
  99.7 60.5 %copy-start = (bf16[128,512]{1,0:T(8,128)(2,1)S(1)}, bf16[128,512]{1,0:T(8,128)(2,1)}, u32[]{:S(2)}) copy-start(bf16[128,512]{1,0:T(8,128)(2,1)} %refs_0_.1) | copy-start | bytes 393220
  129.4 29.6 %all-to-all-start.3 = ((bf16[8,8,16,512]{3,2,1,0:T(8,128)(2,1)}), bf16[8,8,16,512]{3,2,1,0:T(8,128)(2,1)S(1)}, u32[]{:S(2)}, u32[]{:S(2)}) async-start(bf16[8,8,16,512]{3,2,1,0:T(8,128)(2,1)} %copy.26), calls=%async_computation.3 | async-start | bytes 2097152 | tf_op jit(solution)/shard_map/all_to_all | solution.py:159
Sparse Core Ops, SparseCore 0:
  10.1 40.1 all-gather.1
  98.6 32.0 reduce-scatter.1

commit v12 on v8

--- a/solution.py
+++ b/solution.py
@@ -42,8 +42,8 @@
     capacity = both // 2
     x = arrived_ref[:, :capacity, :].reshape(sources * capacity, width)
     g = arrived_ref[:, capacity:, :].reshape(sources * capacity, width)
-    up = up_ref[0]
-    down = down_ref[0]
+    up = up_ref[...]
+    down = down_ref[...]
     pre_act = row_product(x, up, 1)
     half_cdf = 0.5 * (1.0 + lax.erf(pre_act * root_half))
     activated = (pre_act * half_cdf).astype(jnp.bfloat16)
@@ -52,8 +52,8 @@
     slope = half_cdf + pre_act * jnp.exp(-0.5 * pre_act * pre_act) * density
     pre_grad = (hidden_grad * slope).astype(jnp.bfloat16)
     back_acc[...] += row_product(pre_grad, up, 0)
-    grads_ref[0] = (row_contract(pre_grad, x) * scale).astype(jnp.bfloat16)
-    grads_ref[1] = (row_contract(activated, g) * scale).astype(jnp.bfloat16)
+    grads_ref[:, :width] = (row_contract(pre_grad, x) * scale).astype(jnp.bfloat16)
+    grads_ref[:, width:] = (row_contract(activated, g) * scale).astype(jnp.bfloat16)
     @pl.when(step == pl.num_programs(0) - 1)
     def _():
         leaving_ref[:, :capacity, :] = out_acc[...].astype(jnp.bfloat16).reshape(sources, capacity, width)
@@ -63,22 +63,22 @@
     sources, both, width = arrived.shape
     capacity = both // 2
     rows = sources * capacity
-    hidden = whole.shape[1]
+    hidden = whole.shape[0]
     return pl.pallas_call(
         lambda *refs: expert_body(*refs, scale=scale),
         grid=(hidden // tile,),
         in_specs=[
             pl.BlockSpec((sources, both, width), lambda j: (0, 0, 0)),
-            pl.BlockSpec((1, tile, width), lambda j: (0, j, 0)),
-            pl.BlockSpec((1, tile, width), lambda j: (1, j, 0)),
+            pl.BlockSpec((tile, width), lambda j: (j, 0)),
+            pl.BlockSpec((tile, width), lambda j: (j, 1)),
         ],
         out_specs=[
             pl.BlockSpec((sources, both, width), lambda j: (0, 0, 0)),
-            pl.BlockSpec((2, tile, width), lambda j: (0, j, 0)),
+            pl.BlockSpec((tile, 2 * width), lambda j: (j, 0)),
         ],
         out_shape=[
             jax.ShapeDtypeStruct((sources, both, width), jnp.bfloat16),
-            jax.ShapeDtypeStruct((2, hidden, width), jnp.bfloat16),
+            jax.ShapeDtypeStruct((hidden, 2 * width), jnp.bfloat16),
         ],
         scratch_shapes=[pltpu.VMEM((rows, width), jnp.float32), pltpu.VMEM((rows, width), jnp.float32)],
         cost_estimate=pl.CostEstimate(flops=12 * rows * hidden * width, transcendentals=2 * rows * hidden,
@@ -146,15 +146,14 @@
     slot_count = expert_count * capacity
     route_count = 2 * tok_count
     grad_scale = 1.0 / math.sqrt(2 * tok_count * replica_count)
-    whole = lax.all_gather(jnp.concatenate([up_weight, down_weight], axis=0), "dp", axis=1, tiled=True)
+    whole = lax.all_gather(jnp.concatenate([up_weight[0], down_weight[0]], axis=1), "dp", axis=0, tiled=True)
     sending, return_side = prologue(tokens, cotangent, modality, modal_gains, routes, gate_share, expert_count, capacity)
     arrived = lax.all_to_all(sending, "expert", split_axis=0, concat_axis=0, tiled=True)
     leaving, parts = expert_block(arrived, whole, grad_scale)
     back = lax.all_to_all(leaving, "expert", split_axis=0, concat_axis=0, tiled=True)
-    parts = parts.transpose(1, 0, 2)
     grad_pair = lax.psum_scatter(parts, "dp", scatter_dimension=0, tiled=True)
-    up_grad = grad_pair[:, 0][None]
-    down_grad = grad_pair[:, 1][None]
+    up_grad = grad_pair[:, :model_width][None]
+    down_grad = grad_pair[:, model_width:][None]
     combined = row_contract(return_side.reshape(2 * slot_count, 2 * tok_count), back.reshape(2 * slot_count, model_width))
     x_float = tokens.astype(jnp.float32)
     inv_rms = lax.rsqrt(jnp.mean(x_float * x_float, axis=-1, keepdims=True) + 1e-06)

time: 118 us -> 118 us (level)
    broadcast_in_dim x0 -> x1, local copies, waits for them, and re-layouts: none -> 1.85 us  [on_device(): down_grad = grad_pair[:, model_width:][None]]
    another operation x1 -> x0, local copies, waits for them, and re-layouts: 1.85 us -> none  [on_device(): down_grad = grad_pair[:, 1][None]]
where the time goes in v12:
time: 118 us; the launch traced here: 117 us
  blocking collectives  46.5 us (39%)
  waiting for transfers between devices  28.8 us (24%)
  between operations  14.1 us (12%)
  Pallas kernels  13.8 us (12%)
  starting transfers between devices  6.63 us (6%)
  local copies, waits for them, and re-layouts  3.94 us (3%)
  other arithmetic  2.89 us (2%)
    all_to_all x1, blocking collectives, on_device(): lax.all_to_all(sending, 'expert', split_axis=0, concat_axis=0, tiled=True)  46.5 us
    all_to_all x1, waiting for transfers between devices, on_device(): lax.all_to_all(leaving, 'expert', split_axis=0, concat_axis=0, tiled=True)  28.7 us
    pallas_call x1, Pallas kernels, expert_block(): pl.pallas_call(lambda *refs: expert_body(*refs, scale=scale), grid=(hidde...  11.3 us
    all_to_all x1, starting transfers between devices, on_device(): lax.all_to_all(leaving, 'expert', split_axis=0, concat_axis=0, tiled=True)  6.55 us
    pallas_call x1, Pallas kernels, prologue(): pl.pallas_call(lambda *refs: prologue_body(*refs, experts=experts, capaci...  2.58 us
  transfers between devices with their start and end apart: 3, of which 1 were waited for; matrix products, arithmetic and copies ran while one was open for 3% of the time, Pallas kernels for 2%

profile of v12, /device:TPU:6, one launch (start us, length us, event | category | flops | bytes accessed | tf_op | source)
XLA Modules:
  0.0 117.1 jit_solution(13535272075440331825)
XLA Ops:
  7.2 0.0 all-gather.2.cloned.1.call-start
  7.2 1.9 %pad_maximum_fusion = bf16[256,1024]{1,0:T(8,128)(2,1)} fusion(bf16[256,512]{1,0:T(8,128)(2,1)} %bitcast.15, bf16[256,512]{1,0:T(8,128)(2,1)} %bitcast.16), kind=kLoop, calls=%fused_computation.1 | loop fusion | flops 1048576 | bytes 1048576 | tf_op jit(solution)/shard_map/concatenate | solution.py:149
  9.1 0.0 all-gather.2.cloned.1.call-update
  9.1 0.0 reduce-scatter.2.cloned.1.call-start
  9.2 1.4 %copy.12.refs_2_ = s32[128,1]{1,0:T(8,128)} copy(s32[128,1]{0,1:T(1,128)} %bitcast.23) | data formatting | bytes 1024 | tf_op jit(solution)/shard_map/reshape | solution.py:137
  10.6 2.6 %shard_map.111 = (bf16[64,16,512]{2,1,0:T(8,128)(2,1)}, bf16[64,16,256]{2,1,0:T(8,128)(2,1)}) custom-call(bf16[128,512]{1,0:T(8,128)(2,1)} %refs_0_.1, bf16[128,512]{1,0:T(8,128)(2,1)} %refs_1_.1, s32[128,1]{1,0:T(8,128)} %copy.12.refs_2_, f32[2,512]{1,0:T(2,128)} %refs_3_.1, s32[2,128]{1,0:T(2,128)} %bitcast.21, s32[1,128]{1,0:T(1,128)} %bitcast.22), custom_call_target="tpu_custom_call" | custom-call | tf_op jit(solution)/shard_map/pallas_call | solution.py:128
  13.1 46.5 %all_to_all.10.refs_0_ = bf16[64,16,512]{2,1,0:T(8,128)(2,1)} all-to-all(bf16[64,16,512]{2,1,0:T(8,128)(2,1)} %get-tuple-element.9), channel_id=1, replica_groups=mesh['dp'=8,'expert'=64] {'expert'}, dimensions={0} | all-to-all | bytes 2097152 | tf_op jit(solution)/shard_map/all_to_all | solution.py:151
  59.6 0.0 all-gather.2.cloned.1.call-done.refs_1_.refs_2_
  59.6 11.3 %shard_map.112 = (bf16[64,16,512]{2,1,0:T(8,128)(2,1)}, bf16[2048,1024]{1,0:T(8,128)(2,1)}) custom-call(bf16[64,16,512]{2,1,0:T(8,128)(2,1)} %all_to_all.10.refs_0_, bf16[2048,1024]{1,0:T(8,128)(2,1)} %all-gather.2.cloned.1.call-done.refs_1_.refs_2_, bf16[2048,1024]{1,0:T(8,128)(2,1)} %all-gather.2.cloned.1.call-done.refs_1_.refs_2_), custom_call_target="tpu_custom_call" | custom-call | flops 6442450944 | bytes 10485760 | tf_op jit(solution)/shard_map/pallas_call | solution.py:67
  70.9 0.0 copy-start.2
  70.9 0.0 copy-start.1
  70.9 0.0 copy-start.3
  70.9 0.0 reduce-scatter.2.cloned.1.call-update
  70.9 6.6 %all-to-all-start.1 = ((bf16[64,16,512]{2,1,0:T(8,128)(2,1)}), bf16[64,16,512]{2,1,0:T(8,128)(2,1)S(1)}, u32[]{:S(2)}, u32[]{:S(2)}) async-start(bf16[64,16,512]{2,1,0:T(8,128)(2,1)} %get-tuple-element.10), calls=%async_computation.1 | async-start | bytes 2097152 | tf_op jit(solution)/shard_map/all_to_all | solution.py:153
  77.5 0.0 copy-done.2
  77.5 0.0 copy-done.1
  77.5 28.7 %all-to-all-done.1 = bf16[64,16,512]{2,1,0:T(8,128)(2,1)S(1)} async-done(((bf16[64,16,512]{2,1,0:T(8,128)(2,1)}), bf16[64,16,512]{2,1,0:T(8,128)(2,1)S(1)}, u32[]{:S(2)}, u32[]{:S(2)}) %all-to-all-start.1) | async-done | bytes 1048608 | tf_op jit(solution)/shard_map/all_to_all | solution.py:153
  106.2 0.0 copy-done.3
  106.2 0.0 copy-start
  106.2 0.4 convolution_bitcast_fusion
  106.7 0.7 slice.37
  107.4 0.0 copy-done
  107.4 0.2 fusion
  107.6 0.8 fusion.3
  108.4 0.0 reduce-scatter.2.cloned.1.call-done
  108.4 1.9 %slice_bitcast_fusion = (bf16[1,256,512]{2,1,0:T(8,128)(2,1)}, bf16[1,256,512]{2,1,0:T(8,128)(2,1)}) fusion(bf16[256,1024]{1,0:T(8,128)(2,1)} %reduce-scatter.2.cloned.1.call-done), kind=kLoop, calls=%fused_computation.10 | loop fusion | bytes 1048576 | tf_op jit(solution)/shard_map/broadcast_in_dim | solution.py:156
  (4 shorter events, 0.0 us)
Async XLA Ops:
  7.2 52.5 %all-gather.2.cloned.1.call-start = ((), (), s32[]{:S(2)}) async-start(), calls=%async_computation.3 | async-start | bytes 4718592 | tf_op jit(solution)/shard_map/all_gather | solution.py:149
  9.1 99.3 %reduce-scatter.2.cloned.1.call-start = ((), (), s32[]{:S(2)}) async-start(), calls=%async_computation.4 | async-start | bytes 4718592 | tf_op jit(solution)/shard_map/reduce_scatter | solution.py:154
  70.9 6.6 %copy-start.2 = (s32[128]{0:T(128)S(1)}, s32[128]{0:T(128)}, u32[]{:S(2)}) copy-start(s32[128]{0:T(128)} %param.9) | copy-start | bytes 1540
  70.9 6.6 %copy-start.1 = (f32[2,512]{1,0:T(2,128)S(1)}, f32[2,512]{1,0:T(2,128)}, u32[]{:S(2)}) copy-start(f32[2,512]{1,0:T(2,128)} %refs_3_.1) | copy-start | bytes 12292
  70.9 35.4 %copy-start.3 = (bf16[64,16,256]{2,1,0:T(8,128)(2,1)S(1)}, bf16[64,16,256]{2,1,0:T(8,128)(2,1)}, u32[]{:S(2)}) copy-start(bf16[64,16,256]{2,1,0:T(8,128)(2,1)} %get-tuple-element.8) | copy-start | bytes 1572868
  70.9 35.3 %all-to-all-start.1 = ((bf16[64,16,512]{2,1,0:T(8,128)(2,1)}), bf16[64,16,512]{2,1,0:T(8,128)(2,1)S(1)}, u32[]{:S(2)}, u32[]{:S(2)}) async-start(bf16[64,16,512]{2,1,0:T(8,128)(2,1)} %get-tuple-element.10), calls=%async_computation.1 | async-start | bytes 2097152 | tf_op jit(solution)/shard_map/all_to_all | solution.py:153
  106.2 1.1 copy-start
Sparse Core Ops, SparseCore 0:
  10.2 40.1 all-gather.1
  71.0 34.6 reduce-scatter.1

commit v13 on v8

--- a/solution.py
+++ b/solution.py
@@ -155,12 +155,13 @@
     grad_pair = lax.psum_scatter(parts, "dp", scatter_dimension=0, tiled=True)
     up_grad = grad_pair[:, 0][None]
     down_grad = grad_pair[:, 1][None]
-    combined = row_contract(return_side.reshape(2 * slot_count, 2 * tok_count), back.reshape(2 * slot_count, model_width))
+    side = return_side.reshape(2 * slot_count, 2 * tok_count)
+    returned = back.reshape(2 * slot_count, model_width)
     x_float = tokens.astype(jnp.float32)
     inv_rms = lax.rsqrt(jnp.mean(x_float * x_float, axis=-1, keepdims=True) + 1e-06)
     gain_rows = jnp.where(modality[:, None] == 1, modal_gains[1][None, :], modal_gains[0][None, :])
-    moe_output = combined[:tok_count].astype(jnp.bfloat16)
-    normed_grad = combined[tok_count:]
+    moe_output = row_contract(side[:, :tok_count], returned).astype(jnp.bfloat16)
+    normed_grad = row_contract(side[:, tok_count:], returned)
     scaled = gain_rows * normed_grad
     token_grad = (
         inv_rms * scaled - x_float * inv_rms**3 * jnp.mean(x_float * scaled, axis=-1, keepdims=True)

time: 118 us -> 118 us (level)
  no operation moved by 1% of the time
where the time goes in v13:
time: 118 us; the launch traced here: 117 us
  blocking collectives  46.5 us (39%)
  waiting for transfers between devices  28.7 us (24%)
  between operations  14.1 us (12%)
  Pallas kernels  13.7 us (12%)
  starting transfers between devices  6.62 us (6%)
  local copies, waits for them, and re-layouts  3.26 us (3%)
  other arithmetic  2.68 us (2%)
  matrix products  1.41 us (1%)
    all_to_all x1, blocking collectives, on_device(): lax.all_to_all(sending, 'expert', split_axis=0, concat_axis=0, tiled=True)  46.5 us
    all_to_all x1, waiting for transfers between devices, on_device(): lax.all_to_all(leaving, 'expert', split_axis=0, concat_axis=0, tiled=True)  28.7 us
    pallas_call x1, Pallas kernels, expert_block(): pl.pallas_call(lambda *refs: expert_body(*refs, scale=scale), grid=(hidde...  11.1 us
    all_to_all x1, starting transfers between devices, on_device(): lax.all_to_all(leaving, 'expert', split_axis=0, concat_axis=0, tiled=True)  6.54 us
    pallas_call x1, Pallas kernels, prologue(): pl.pallas_call(lambda *refs: prologue_body(*refs, experts=experts, capaci...  2.58 us
  transfers between devices with their start and end apart: 3, of which 1 were waited for; matrix products, arithmetic and copies ran while one was open for 3% of the time, Pallas kernels for 2%

profile of v13, /device:TPU:6, one launch (start us, length us, event | category | flops | bytes accessed | tf_op | source)
XLA Modules:
  0.0 117.0 jit_solution(15295985645965529038)
XLA Ops:
  7.2 0.0 all-gather.2.cloned.1.call-start
  7.2 1.9 %pad_maximum_fusion = bf16[2,256,512]{2,1,0:T(8,128)(2,1)} fusion(bf16[1,256,512]{2,1,0:T(8,128)(2,1)} %param.14, bf16[1,256,512]{2,1,0:T(8,128)(2,1)} %param.13), kind=kLoop, calls=%fused_computation.2 | loop fusion | flops 262144 | bytes 1048576 | tf_op jit(solution)/shard_map/concatenate | solution.py:149
  9.1 0.0 all-gather.2.cloned.1.call-update
  9.1 0.0 reduce-scatter.2.cloned.1.call-start
  9.2 1.4 %copy.12.refs_2_ = s32[128,1]{1,0:T(8,128)} copy(s32[128,1]{0,1:T(1,128)} %bitcast.23) | data formatting | bytes 1024 | tf_op jit(solution)/shard_map/reshape | solution.py:137
  10.6 2.6 %shard_map.111 = (bf16[64,16,512]{2,1,0:T(8,128)(2,1)}, bf16[64,16,256]{2,1,0:T(8,128)(2,1)}) custom-call(bf16[128,512]{1,0:T(8,128)(2,1)} %refs_0_.1, bf16[128,512]{1,0:T(8,128)(2,1)} %refs_1_.1, s32[128,1]{1,0:T(8,128)} %copy.12.refs_2_, f32[2,512]{1,0:T(2,128)} %refs_3_.1, s32[2,128]{1,0:T(2,128)} %bitcast.21, s32[1,128]{1,0:T(1,128)} %bitcast.22), custom_call_target="tpu_custom_call" | custom-call | tf_op jit(solution)/shard_map/pallas_call | solution.py:128
  13.1 46.5 %all_to_all.10.refs_0_ = bf16[64,16,512]{2,1,0:T(8,128)(2,1)} all-to-all(bf16[64,16,512]{2,1,0:T(8,128)(2,1)} %get-tuple-element.9), channel_id=1, replica_groups=mesh['dp'=8,'expert'=64] {'expert'}, dimensions={0} | all-to-all | bytes 2097152 | tf_op jit(solution)/shard_map/all_to_all | solution.py:151
  59.6 0.0 all-gather.2.cloned.1.call-done.refs_1_.refs_2_
  59.6 11.1 %shard_map.112 = (bf16[64,16,512]{2,1,0:T(8,128)(2,1)}, bf16[2,2048,512]{2,1,0:T(8,128)(2,1)}) custom-call(bf16[64,16,512]{2,1,0:T(8,128)(2,1)} %all_to_all.10.refs_0_, bf16[2,2048,512]{2,1,0:T(8,128)(2,1)} %all-gather.2.cloned.1.call-done.refs_1_.refs_2_, bf16[2,2048,512]{2,1,0:T(8,128)(2,1)} %all-gather.2.cloned.1.call-done.refs_1_.refs_2_), custom_call_target="tpu_custom_call" | custom-call | flops 6442450944 | bytes 10485760 | tf_op jit(solution)/shard_map/pallas_call | solution.py:67
  70.7 0.0 copy-start.3
  70.8 0.0 copy-start.2
  70.8 0.0 copy-start
  70.8 0.0 copy-start.1
  70.8 0.0 reduce-scatter.2.cloned.1.call-update
  70.8 6.5 %all-to-all-start.1 = ((bf16[64,16,512]{2,1,0:T(8,128)(2,1)}), bf16[64,16,512]{2,1,0:T(8,128)(2,1)S(1)}, u32[]{:S(2)}, u32[]{:S(2)}) async-start(bf16[64,16,512]{2,1,0:T(8,128)(2,1)} %get-tuple-element.10), calls=%async_computation.1 | async-start | bytes 2097152 | tf_op jit(solution)/shard_map/all_to_all | solution.py:153
  77.3 0.0 copy-done.3
  77.4 0.0 copy-done.2
  77.4 28.7 %all-to-all-done.1 = bf16[64,16,512]{2,1,0:T(8,128)(2,1)S(1)} async-done(((bf16[64,16,512]{2,1,0:T(8,128)(2,1)}), bf16[64,16,512]{2,1,0:T(8,128)(2,1)S(1)}, u32[]{:S(2)}, u32[]{:S(2)}) %all-to-all-start.1) | async-done | bytes 1048608 | tf_op jit(solution)/shard_map/all_to_all | solution.py:153
  106.1 0.0 copy-done
  106.1 0.0 copy-done.1
  106.1 0.4 fusion
  106.5 0.8 fusion.3
  107.3 1.0 convolution_convert_fusion
  108.3 0.0 reduce-scatter.2.cloned.1.call-done
  108.3 1.9 %slice_bitcast_fusion = (bf16[1,256,512]{2,1,0:T(8,128)(2,1)}, bf16[1,256,512]{2,1,0:T(8,128)(2,1)}) fusion(bf16[256,2,512]{2,0,1:T(8,128)(2,1)} %reduce-scatter.2.cloned.1.call-done), kind=kLoop, calls=%fused_computation.11 | loop fusion | bytes 1048576 | tf_op jit(solution)/shard_map/broadcast_in_dim;squeeze | solution.py:157
  (4 shorter events, 0.0 us)
Async XLA Ops:
  7.2 52.5 %all-gather.2.cloned.1.call-start = ((), (), s32[]{:S(2)}) async-start(), calls=%async_computation.3 | async-start | bytes 4718592 | tf_op jit(solution)/shard_map/all_gather | solution.py:149
  9.1 99.2 %reduce-scatter.2.cloned.1.call-start = ((), (), s32[]{:S(2)}) async-start(), calls=%async_computation.4 | async-start | bytes 4718592 | tf_op jit(solution)/shard_map/reduce_scatter | solution.py:155
  70.7 6.6 %copy-start.3 = (s32[128]{0:T(128)S(1)}, s32[128]{0:T(128)}, u32[]{:S(2)}) copy-start(s32[128]{0:T(128)} %param.9) | copy-start | bytes 1540
  70.8 6.6 %copy-start.2 = (f32[2,512]{1,0:T(2,128)S(1)}, f32[2,512]{1,0:T(2,128)}, u32[]{:S(2)}) copy-start(f32[2,512]{1,0:T(2,128)} %refs_3_.1) | copy-start | bytes 12292
  70.8 35.3 %copy-start = (bf16[128,512]{1,0:T(8,128)(2,1)S(1)}, bf16[128,512]{1,0:T(8,128)(2,1)}, u32[]{:S(2)}) copy-start(bf16[128,512]{1,0:T(8,128)(2,1)} %refs_0_.1) | copy-start | bytes 393220
  70.8 35.3 %copy-start.1 = (bf16[64,16,256]{2,1,0:T(8,128)(2,1)S(1)}, bf16[64,16,256]{2,1,0:T(8,128)(2,1)}, u32[]{:S(2)}) copy-start(bf16[64,16,256]{2,1,0:T(8,128)(2,1)} %get-tuple-element.8) | copy-start | bytes 1572868
  70.8 35.3 %all-to-all-start.1 = ((bf16[64,16,512]{2,1,0:T(8,128)(2,1)}), bf16[64,16,512]{2,1,0:T(8,128)(2,1)S(1)}, u32[]{:S(2)}, u32[]{:S(2)}) async-start(bf16[64,16,512]{2,1,0:T(8,128)(2,1)} %get-tuple-element.10), calls=%async_computation.1 | async-start | bytes 2097152 | tf_op jit(solution)/shard_map/all_to_all | solution.py:153
Sparse Core Ops, SparseCore 0:
  10.1 40.1 all-gather.1
  70.9 34.6 reduce-scatter.1

commit v14 on v13

--- a/solution.py
+++ b/solution.py
@@ -59,7 +59,7 @@
         leaving_ref[:, :capacity, :] = out_acc[...].astype(jnp.bfloat16).reshape(sources, capacity, width)
         leaving_ref[:, capacity:, :] = back_acc[...].astype(jnp.bfloat16).reshape(sources, capacity, width)
 
-def expert_block(arrived, whole, scale, tile=512):
+def expert_block(arrived, whole, scale, tile=1024):
     sources, both, width = arrived.shape
     capacity = both // 2
     rows = sources * capacity

time: 118 us -> 118 us (level)
  no operation moved by 1% of the time
where the time goes in v14:
time: 118 us; the launch traced here: 117 us
  blocking collectives  46.5 us (39%)
  waiting for transfers between devices  28.7 us (24%)
  between operations  14.1 us (12%)
  Pallas kernels  13.8 us (12%)
  starting transfers between devices  6.61 us (6%)
  local copies, waits for them, and re-layouts  3.26 us (3%)
  other arithmetic  2.68 us (2%)
  matrix products  1.41 us (1%)
    all_to_all x1, blocking collectives, on_device(): lax.all_to_all(sending, 'expert', split_axis=0, concat_axis=0, tiled=True)  46.5 us
    all_to_all x1, waiting for transfers between devices, on_device(): lax.all_to_all(leaving, 'expert', split_axis=0, concat_axis=0, tiled=True)  28.7 us
    pallas_call x1, Pallas kernels, expert_block(): pl.pallas_call(lambda *refs: expert_body(*refs, scale=scale), grid=(hidde...  11.2 us
    all_to_all x1, starting transfers between devices, on_device(): lax.all_to_all(leaving, 'expert', split_axis=0, concat_axis=0, tiled=True)  6.53 us
    pallas_call x1, Pallas kernels, prologue(): pl.pallas_call(lambda *refs: prologue_body(*refs, experts=experts, capaci...  2.58 us
  transfers between devices with their start and end apart: 3, of which 1 were waited for; matrix products, arithmetic and copies ran while one was open for 3% of the time, Pallas kernels for 2%

profile of v14, /device:TPU:6, one launch (start us, length us, event | category | flops | bytes accessed | tf_op | source)
XLA Modules:
  0.0 117.0 jit_solution(17526496717414852752)
XLA Ops:
  7.2 0.0 all-gather.2.cloned.1.call-start
  7.2 1.9 %pad_maximum_fusion = bf16[2,256,512]{2,1,0:T(8,128)(2,1)} fusion(bf16[1,256,512]{2,1,0:T(8,128)(2,1)} %param.14, bf16[1,256,512]{2,1,0:T(8,128)(2,1)} %param.13), kind=kLoop, calls=%fused_computation.2 | loop fusion | flops 262144 | bytes 1048576 | tf_op jit(solution)/shard_map/concatenate | solution.py:149
  9.1 0.0 all-gather.2.cloned.1.call-update
  9.1 0.0 reduce-scatter.2.cloned.1.call-start
  9.2 1.4 %copy.12.refs_2_ = s32[128,1]{1,0:T(8,128)} copy(s32[128,1]{0,1:T(1,128)} %bitcast.23) | data formatting | bytes 1024 | tf_op jit(solution)/shard_map/reshape | solution.py:137
  10.6 2.6 %shard_map.111 = (bf16[64,16,512]{2,1,0:T(8,128)(2,1)}, bf16[64,16,256]{2,1,0:T(8,128)(2,1)}) custom-call(bf16[128,512]{1,0:T(8,128)(2,1)} %refs_0_.1, bf16[128,512]{1,0:T(8,128)(2,1)} %refs_1_.1, s32[128,1]{1,0:T(8,128)} %copy.12.refs_2_, f32[2,512]{1,0:T(2,128)} %refs_3_.1, s32[2,128]{1,0:T(2,128)} %bitcast.21, s32[1,128]{1,0:T(1,128)} %bitcast.22), custom_call_target="tpu_custom_call" | custom-call | tf_op jit(solution)/shard_map/pallas_call | solution.py:128
  13.1 46.5 %all_to_all.10.refs_0_ = bf16[64,16,512]{2,1,0:T(8,128)(2,1)} all-to-all(bf16[64,16,512]{2,1,0:T(8,128)(2,1)} %get-tuple-element.9), channel_id=1, replica_groups=mesh['dp'=8,'expert'=64] {'expert'}, dimensions={0} | all-to-all | bytes 2097152 | tf_op jit(solution)/shard_map/all_to_all | solution.py:151
  59.6 0.0 all-gather.2.cloned.1.call-done.refs_1_.refs_2_
  59.6 11.2 %shard_map.112 = (bf16[64,16,512]{2,1,0:T(8,128)(2,1)}, bf16[2,2048,512]{2,1,0:T(8,128)(2,1)}) custom-call(bf16[64,16,512]{2,1,0:T(8,128)(2,1)} %all_to_all.10.refs_0_, bf16[2,2048,512]{2,1,0:T(8,128)(2,1)} %all-gather.2.cloned.1.call-done.refs_1_.refs_2_, bf16[2,2048,512]{2,1,0:T(8,128)(2,1)} %all-gather.2.cloned.1.call-done.refs_1_.refs_2_), custom_call_target="tpu_custom_call" | custom-call | flops 6442450944 | bytes 10485760 | tf_op jit(solution)/shard_map/pallas_call | solution.py:67
  70.8 0.0 copy-start.3
  70.8 0.0 copy-start.2
  70.8 0.0 copy-start
  70.8 0.0 copy-start.1
  70.8 0.0 reduce-scatter.2.cloned.1.call-update
  70.9 6.5 %all-to-all-start.1 = ((bf16[64,16,512]{2,1,0:T(8,128)(2,1)}), bf16[64,16,512]{2,1,0:T(8,128)(2,1)S(1)}, u32[]{:S(2)}, u32[]{:S(2)}) async-start(bf16[64,16,512]{2,1,0:T(8,128)(2,1)} %get-tuple-element.10), calls=%async_computation.1 | async-start | bytes 2097152 | tf_op jit(solution)/shard_map/all_to_all | solution.py:153
  77.4 0.0 copy-done.3
  77.4 0.0 copy-done.2
  77.4 28.7 %all-to-all-done.1 = bf16[64,16,512]{2,1,0:T(8,128)(2,1)S(1)} async-done(((bf16[64,16,512]{2,1,0:T(8,128)(2,1)}), bf16[64,16,512]{2,1,0:T(8,128)(2,1)S(1)}, u32[]{:S(2)}, u32[]{:S(2)}) %all-to-all-start.1) | async-done | bytes 1048608 | tf_op jit(solution)/shard_map/all_to_all | solution.py:153
  106.1 0.0 copy-done
  106.1 0.0 copy-done.1
  106.1 0.4 fusion
  106.5 0.8 fusion.3
  107.3 1.0 convolution_convert_fusion
  108.3 0.0 reduce-scatter.2.cloned.1.call-done
  108.3 1.9 %slice_bitcast_fusion = (bf16[1,256,512]{2,1,0:T(8,128)(2,1)}, bf16[1,256,512]{2,1,0:T(8,128)(2,1)}) fusion(bf16[256,2,512]{2,0,1:T(8,128)(2,1)} %reduce-scatter.2.cloned.1.call-done), kind=kLoop, calls=%fused_computation.11 | loop fusion | bytes 1048576 | tf_op jit(solution)/shard_map/broadcast_in_dim;squeeze | solution.py:157
  (4 shorter events, 0.0 us)
Async XLA Ops:
  7.2 52.5 %all-gather.2.cloned.1.call-start = ((), (), s32[]{:S(2)}) async-start(), calls=%async_computation.3 | async-start | bytes 4718592 | tf_op jit(solution)/shard_map/all_gather | solution.py:149
  9.1 99.2 %reduce-scatter.2.cloned.1.call-start = ((), (), s32[]{:S(2)}) async-start(), calls=%async_computation.4 | async-start | bytes 4718592 | tf_op jit(solution)/shard_map/reduce_scatter | solution.py:155
  70.8 6.6 %copy-start.3 = (s32[128]{0:T(128)S(1)}, s32[128]{0:T(128)}, u32[]{:S(2)}) copy-start(s32[128]{0:T(128)} %param.9) | copy-start | bytes 1540
  70.8 6.6 %copy-start.2 = (f32[2,512]{1,0:T(2,128)S(1)}, f32[2,512]{1,0:T(2,128)}, u32[]{:S(2)}) copy-start(f32[2,512]{1,0:T(2,128)} %refs_3_.1) | copy-start | bytes 12292
  70.8 35.3 %copy-start = (bf16[128,512]{1,0:T(8,128)(2,1)S(1)}, bf16[128,512]{1,0:T(8,128)(2,1)}, u32[]{:S(2)}) copy-start(bf16[128,512]{1,0:T(8,128)(2,1)} %refs_0_.1) | copy-start | bytes 393220
  70.8 35.3 %copy-start.1 = (bf16[64,16,256]{2,1,0:T(8,128)(2,1)S(1)}, bf16[64,16,256]{2,1,0:T(8,128)(2,1)}, u32[]{:S(2)}) copy-start(bf16[64,16,256]{2,1,0:T(8,128)(2,1)} %get-tuple-element.8) | copy-start | bytes 1572868
  70.9 35.2 %all-to-all-start.1 = ((bf16[64,16,512]{2,1,0:T(8,128)(2,1)}), bf16[64,16,512]{2,1,0:T(8,128)(2,1)S(1)}, u32[]{:S(2)}, u32[]{:S(2)}) async-start(bf16[64,16,512]{2,1,0:T(8,128)(2,1)} %get-tuple-element.10), calls=%async_computation.1 | async-start | bytes 2097152 | tf_op jit(solution)/shard_map/all_to_all | solution.py:153
Sparse Core Ops, SparseCore 0:
  10.1 40.1 all-gather.1
  71.0 34.7 reduce-scatter.1

commit v15 on v13

--- a/solution.py
+++ b/solution.py
@@ -93,7 +93,8 @@
     x = tokens_ref[...].astype(jnp.float32)
     inv_rms = lax.rsqrt(jnp.mean(x * x, axis=-1, keepdims=True) + 1e-06)
     gains = gains_ref[...]
-    gain_rows = jnp.where(modality_ref[...] == 1, gains[1:2, :], gains[0:1, :])
+    modality = jnp.transpose(jnp.broadcast_to(modality_ref[...].astype(jnp.float32), (tok_count, tok_count)))[:, 0:1]
+    gain_rows = jnp.where(modality > 0.5, gains[1:2, :], gains[0:1, :])
     normed = (x * inv_rms * gain_rows).astype(jnp.bfloat16)
     routes = routes_ref[...]
     first = routes[0:1, :]
@@ -127,14 +128,14 @@
     whole = lambda shape: pl.BlockSpec(shape, lambda: (0,) * len(shape))
     return pl.pallas_call(
         lambda *refs: prologue_body(*refs, experts=experts, capacity=capacity),
-        in_specs=[whole((tok_count, width)), whole((tok_count, width)), whole((tok_count, 1)), whole((2, width)),
+        in_specs=[whole((tok_count, width)), whole((tok_count, width)), whole((1, tok_count)), whole((2, width)),
                   whole((2, tok_count)), whole((1, tok_count))],
         out_specs=[whole((experts, 2 * capacity, width)), whole((experts, 2 * capacity, 2 * tok_count))],
         out_shape=[
             jax.ShapeDtypeStruct((experts, 2 * capacity, width), jnp.bfloat16),
             jax.ShapeDtypeStruct((experts, 2 * capacity, 2 * tok_count), jnp.bfloat16),
         ],
-    )(tokens, cotangent, modality.reshape(tok_count, 1), modal_gains, routes.T, gate_share.reshape(1, tok_count))
+    )(tokens, cotangent, modality.reshape(1, tok_count), modal_gains, routes.T, gate_share.reshape(1, tok_count))
 
 
 def on_device(tokens, modality, modal_gains, routes, gate_share, up_weight, down_weight, cotangent):

time: 118 us -> 118 us (level)
  local copies, waits for them, and re-layouts: 3.26 us -> 1.87 us
    reshape x1 -> x0, local copies, waits for them, and re-layouts: 1.39 us -> none  [prologue(): modality.reshape(tok_count, 1)]
  transfers between devices with their start and end apart: 3 -> 3, of which waited for: 1 -> 1; matrix products, arithmetic and copies ran while one was open for 3% -> 2% of each run, Pallas kernels for 2% -> 2%
where the time goes in v15:
time: 118 us; the launch traced here: 116 us
  blocking collectives  46.5 us (39%)
  waiting for transfers between devices  29.2 us (25%)
  between operations  14.1 us (12%)
  Pallas kernels  13.8 us (12%)
  starting transfers between devices  6.63 us (6%)
  other arithmetic  2.68 us (2%)
  local copies, waits for them, and re-layouts  1.87 us (2%)
  matrix products  1.41 us (1%)
    all_to_all x1, blocking collectives, on_device(): lax.all_to_all(sending, 'expert', split_axis=0, concat_axis=0, tiled=True)  46.5 us
    all_to_all x1, waiting for transfers between devices, on_device(): lax.all_to_all(leaving, 'expert', split_axis=0, concat_axis=0, tiled=True)  29.2 us
    pallas_call x1, Pallas kernels, expert_block(): pl.pallas_call(lambda *refs: expert_body(*refs, scale=scale), grid=(hidde...  11.1 us
    all_to_all x1, starting transfers between devices, on_device(): lax.all_to_all(leaving, 'expert', split_axis=0, concat_axis=0, tiled=True)  6.55 us
    pallas_call x1, Pallas kernels, prologue(): pl.pallas_call(lambda *refs: prologue_body(*refs, experts=experts, capaci...  2.63 us
  transfers between devices with their start and end apart: 3, of which 1 were waited for; matrix products, arithmetic and copies ran while one was open for 2% of the time, Pallas kernels for 2%

profile of v15, /device:TPU:6, one launch (start us, length us, event | category | flops | bytes accessed | tf_op | source)
XLA Modules:
  0.0 116.1 jit_solution(4725995900065568380)
XLA Ops:
  7.2 0.0 all-gather.2.cloned.1.call-start
  7.2 1.9 %pad_maximum_fusion = bf16[2,256,512]{2,1,0:T(8,128)(2,1)} fusion(bf16[1,256,512]{2,1,0:T(8,128)(2,1)} %param.14, bf16[1,256,512]{2,1,0:T(8,128)(2,1)} %param.13), kind=kLoop, calls=%fused_computation.2 | loop fusion | flops 262144 | bytes 1048576 | tf_op jit(solution)/shard_map/concatenate | solution.py:150
  9.1 0.0 all-gather.2.cloned.1.call-update
  9.1 0.0 reduce-scatter.2.cloned.1.call-start
  9.2 2.6 %shard_map.111 = (bf16[64,16,512]{2,1,0:T(8,128)(2,1)}, bf16[64,16,256]{2,1,0:T(8,128)(2,1)}) custom-call(bf16[128,512]{1,0:T(8,128)(2,1)} %refs_0_.1, bf16[128,512]{1,0:T(8,128)(2,1)} %refs_1_.1, s32[1,128]{1,0:T(1,128)} %bitcast.23, f32[2,512]{1,0:T(2,128)} %refs_3_.1, s32[2,128]{1,0:T(2,128)} %bitcast.21, s32[1,128]{1,0:T(1,128)} %bitcast.22), custom_call_target="tpu_custom_call" | custom-call | tf_op jit(solution)/shard_map/pallas_call | solution.py:129
  11.8 46.5 %all_to_all.10.refs_0_ = bf16[64,16,512]{2,1,0:T(8,128)(2,1)} all-to-all(bf16[64,16,512]{2,1,0:T(8,128)(2,1)} %get-tuple-element.9), channel_id=1, replica_groups=mesh['dp'=8,'expert'=64] {'expert'}, dimensions={0} | all-to-all | bytes 2097152 | tf_op jit(solution)/shard_map/all_to_all | solution.py:152
  58.3 0.0 all-gather.2.cloned.1.call-done.refs_1_.refs_2_
  58.3 11.1 %shard_map.112 = (bf16[64,16,512]{2,1,0:T(8,128)(2,1)}, bf16[2,2048,512]{2,1,0:T(8,128)(2,1)}) custom-call(bf16[64,16,512]{2,1,0:T(8,128)(2,1)} %all_to_all.10.refs_0_, bf16[2,2048,512]{2,1,0:T(8,128)(2,1)} %all-gather.2.cloned.1.call-done.refs_1_.refs_2_, bf16[2,2048,512]{2,1,0:T(8,128)(2,1)} %all-gather.2.cloned.1.call-done.refs_1_.refs_2_), custom_call_target="tpu_custom_call" | custom-call | flops 6442450944 | bytes 10485760 | tf_op jit(solution)/shard_map/pallas_call | solution.py:67
  69.4 0.0 copy-start.3
  69.4 0.0 copy-start.2
  69.4 0.0 copy-start
  69.4 0.0 copy-start.1
  69.4 0.0 reduce-scatter.2.cloned.1.call-update
  69.5 6.5 %all-to-all-start.1 = ((bf16[64,16,512]{2,1,0:T(8,128)(2,1)}), bf16[64,16,512]{2,1,0:T(8,128)(2,1)S(1)}, u32[]{:S(2)}, u32[]{:S(2)}) async-start(bf16[64,16,512]{2,1,0:T(8,128)(2,1)} %get-tuple-element.10), calls=%async_computation.1 | async-start | bytes 2097152 | tf_op jit(solution)/shard_map/all_to_all | solution.py:154
  76.0 0.0 copy-done.3
  76.0 0.0 copy-done.2
  76.1 29.2 %all-to-all-done.1 = bf16[64,16,512]{2,1,0:T(8,128)(2,1)S(1)} async-done(((bf16[64,16,512]{2,1,0:T(8,128)(2,1)}), bf16[64,16,512]{2,1,0:T(8,128)(2,1)S(1)}, u32[]{:S(2)}, u32[]{:S(2)}) %all-to-all-start.1) | async-done | bytes 1048608 | tf_op jit(solution)/shard_map/all_to_all | solution.py:154
  105.2 0.0 copy-done
  105.2 0.0 copy-done.1
  105.2 0.4 fusion
  105.7 0.8 fusion.3
  106.5 1.0 convolution_convert_fusion
  107.5 0.0 reduce-scatter.2.cloned.1.call-done
  107.5 1.9 %slice_bitcast_fusion = (bf16[1,256,512]{2,1,0:T(8,128)(2,1)}, bf16[1,256,512]{2,1,0:T(8,128)(2,1)}) fusion(bf16[256,2,512]{2,0,1:T(8,128)(2,1)} %reduce-scatter.2.cloned.1.call-done), kind=kLoop, calls=%fused_computation.11 | loop fusion | bytes 1048576 | tf_op jit(solution)/shard_map/broadcast_in_dim;squeeze | solution.py:158
  (4 shorter events, 0.0 us)
Async XLA Ops:
  7.2 51.1 %all-gather.2.cloned.1.call-start = ((), (), s32[]{:S(2)}) async-start(), calls=%async_computation.3 | async-start | bytes 4718592 | tf_op jit(solution)/shard_map/all_gather | solution.py:150
  9.1 98.3 %reduce-scatter.2.cloned.1.call-start = ((), (), s32[]{:S(2)}) async-start(), calls=%async_computation.4 | async-start | bytes 4718592 | tf_op jit(solution)/shard_map/reduce_scatter | solution.py:156
  69.4 6.6 %copy-start.3 = (s32[128]{0:T(128)S(1)}, s32[128]{0:T(128)}, u32[]{:S(2)}) copy-start(s32[128]{0:T(128)} %param.9) | copy-start | bytes 1540
  69.4 6.6 %copy-start.2 = (f32[2,512]{1,0:T(2,128)S(1)}, f32[2,512]{1,0:T(2,128)}, u32[]{:S(2)}) copy-start(f32[2,512]{1,0:T(2,128)} %refs_3_.1) | copy-start | bytes 12292
  69.4 35.8 %copy-start = (bf16[128,512]{1,0:T(8,128)(2,1)S(1)}, bf16[128,512]{1,0:T(8,128)(2,1)}, u32[]{:S(2)}) copy-start(bf16[128,512]{1,0:T(8,128)(2,1)} %refs_0_.1) | copy-start | bytes 393220
  69.4 35.8 %copy-start.1 = (bf16[64,16,256]{2,1,0:T(8,128)(2,1)S(1)}, bf16[64,16,256]{2,1,0:T(8,128)(2,1)}, u32[]{:S(2)}) copy-start(bf16[64,16,256]{2,1,0:T(8,128)(2,1)} %get-tuple-element.8) | copy-start | bytes 1572868
  69.5 35.8 %all-to-all-start.1 = ((bf16[64,16,512]{2,1,0:T(8,128)(2,1)}), bf16[64,16,512]{2,1,0:T(8,128)(2,1)S(1)}, u32[]{:S(2)}, u32[]{:S(2)}) async-start(bf16[64,16,512]{2,1,0:T(8,128)(2,1)} %get-tuple-element.10), calls=%async_computation.1 | async-start | bytes 2097152 | tf_op jit(solution)/shard_map/all_to_all | solution.py:154
Sparse Core Ops, SparseCore 0:
  10.1 40.1 all-gather.1
  69.6 34.6 reduce-scatter.1
